TPU v7x, 1024 devices: a whole 8x8x8 slice. The times are simulated.
1024 devices in a mesh: ctx: 64 (over x_hi, y, core), chan: 16 (over x_lo, z).
Axes of the slice: x: 8 (x_hi: 4, x_lo: 2; x = x_hi * 2 + x_lo), y: 8, z: 8, core: 2. Of those that a mesh axis runs over, the one named last changes fastest.
Arguments:
- query_gate: bfloat16 [8192, 8192], P('ctx', 'chan'), may hold values from -6 to 6
- key_gate: bfloat16 [8192, 8192], P('ctx', 'chan'), may hold values from -6 to 6
- value_input: bfloat16 [8192, 8192], P('ctx', 'chan'), may hold values from -6 to 6
- cotangent: bfloat16 [8192, 8192], P('ctx', 'chan'), may hold values from -16 to 16
- residues: float32 [16, 8192], P(None, 'chan'), may hold values from -1.5 to 1.5
- decay_rate: float32 [16, 8192], P(None, 'chan'), may hold values from 2.3841858e-06 to 0.0333333333, as said below
Outputs:
- output: bfloat16 [8192, 8192], P('ctx', 'chan')
- grad_query: bfloat16 [8192, 8192], P('ctx', 'chan')
- grad_key: bfloat16 [8192, 8192], P('ctx', 'chan')
- grad_value: bfloat16 [8192, 8192], P('ctx', 'chan')
- grad_residue: float32 [16, 8192], P(None, ('chan', 'ctx'))
- grad_lograte: float32 [16, 8192], P(None, ('chan', 'ctx'))
Inputs may be any that keep to these rules, and one draw needn't show every extreme that they name: `decay_rate`: decay rates of the filters' poles.
All inputs are finite; a program needn't handle non-finite values.
Results may differ from a plain program's by a relative error of at most 0.001.
Values sent between devices are 32-bit elements; how exact they have to be, the bound alone decides.
No kernel may reach another device: no remote copies, remote signals or barrier semaphores. Data moves between devices by JAX's collectives and lax.ppermute only.
A program may use at most 32 MiB of HBM per device.

v0:
```python
import math

import jax
import jax.numpy as jnp
from jax import lax
from jax.sharding import PartitionSpec as P

WIDTH = 8192
MODES = 16


def carried_in(shard, axis, combine, identity, reverse):
    peers, index = (lax.axis_size(axis), lax.axis_index(axis))
    everything = jax.tree.map(lambda part: lax.all_gather(part, axis), shard)
    start = jax.tree.map(
        lambda part, zero: jnp.broadcast_to(jnp.asarray(zero, part.dtype), part.shape),
        shard,
        identity,
    )

    def hop(k, before):
        at = peers - 1 - k if reverse else k
        reached = at > index if reverse else at < index
        new = combine(before, jax.tree.map(lambda part: part[at], everything))
        return jax.tree.map(lambda a, b: jnp.where(reached, a, b), new, before)

    return lax.fori_loop(0, peers, hop, start)


def link_blocks(earlier, later):
    return (earlier[0] * later[0], later[0] * earlier[1] + later[1])


def local_pieces(source, drive, rates, mixing, steps):
    where = jnp.arange(steps, dtype=jnp.float32)[None, :, None]
    rising = jnp.exp(rates[:, None, :] * where)
    falling = jnp.exp(-rates[:, None, :] * where)
    states = falling * jnp.cumsum(rising * source[None], axis=1)
    adjoint = rising * lax.cumsum(
        falling * (mixing[:, None, :] * drive[None]), axis=1, reverse=True
    )
    return (states, adjoint, where)


def local(query_gate, key_gate, value_input, cotangent, residues, decay_rate):
    steps = query_gate.shape[0]
    modes, columns = residues.shape
    group = 4
    count = modes // group
    query = query_gate.astype(jnp.float32)
    keyed = key_gate.astype(jnp.float32)
    values = value_input.astype(jnp.float32)
    upstream = cotangent.astype(jnp.float32)
    source = keyed * values
    drive = upstream * query
    decay = jnp.exp(-decay_rate)
    norm_factor = jnp.sqrt(-jnp.expm1(-2.0 * decay_rate))
    mixing = residues * norm_factor
    rate_groups = decay_rate.reshape(count, group, columns)
    mix_groups = mixing.reshape(count, group, columns)
    offsets = jnp.arange(steps, dtype=jnp.float32)[None, :, None]
    fading = jnp.exp(-decay_rate[:, None, :] * offsets)
    ends = jnp.sum(fading * source[::-1][None], axis=1)
    heads = mixing * jnp.sum(fading * drive[None], axis=1)
    block_decay = jnp.exp(-decay_rate * steps)
    neutral = (jnp.ones_like(decay_rate), jnp.zeros_like(decay_rate))
    _, incoming = carried_in((block_decay, ends), "ctx", link_blocks, neutral, False)
    _, upper = carried_in((block_decay, heads), "ctx", link_blocks, neutral, True)

    def second_pass(carry, item):
        mixed, grad_source = carry
        rates, mix, start, after = item
        states, adjoint, where = local_pieces(source, drive, rates, mix, steps)
        states = states + jnp.exp(-rates[:, None, :] * (where + 1.0)) * start[:, None, :]
        adjoint = adjoint + jnp.exp(-rates[:, None, :] * (steps - where)) * after[:, None, :]
        previous = jnp.concatenate([start[:, None, :], states[:, :-1, :]], axis=1)
        mixed = mixed + jnp.sum(mix[:, None, :] * states, axis=0)
        grad_source = grad_source + jnp.sum(adjoint, axis=0)
        grad_w = jnp.sum(drive[None] * states, axis=1)
        grad_a = jnp.sum(adjoint * previous, axis=1)
        return ((mixed, grad_source), (grad_w, grad_a))

    blank = jnp.zeros((steps, columns), jnp.float32)
    items = (
        rate_groups,
        mix_groups,
        incoming.reshape(count, group, columns),
        upper.reshape(count, group, columns),
    )
    (mixed, grad_source), (grad_ws, grad_as) = lax.scan(second_pass, (blank, blank), items)
    grad_mixing = grad_ws.reshape(modes, columns)
    grad_decay = grad_as.reshape(modes, columns)
    raw_residue = grad_mixing * norm_factor
    raw_lograte = decay_rate * (
        grad_mixing * residues * decay * decay / norm_factor - decay * grad_decay
    )
    own_residue, own_lograte = (
        lax.psum_scatter(raw_residue, "ctx", scatter_dimension=1, tiled=True),
        lax.psum_scatter(raw_lograte, "ctx", scatter_dimension=1, tiled=True),
    )
    total = lax.psum(
        jnp.sum(own_residue * own_residue) + jnp.sum(own_lograte * own_lograte), ("ctx", "chan")
    )
    limit = math.sqrt(2.0 * MODES * WIDTH)
    scale = jnp.minimum(1.0, limit / jnp.sqrt(total + 1e-06))
    output = (query * mixed).astype(jnp.bfloat16)
    grad_query = (upstream * mixed).astype(jnp.bfloat16)
    grad_key = (grad_source * values).astype(jnp.bfloat16)
    grad_value = (grad_source * keyed).astype(jnp.bfloat16)
    return (output, grad_query, grad_key, grad_value, own_residue * scale, own_lograte * scale)


def solution(mesh):
    placed = (
        P("ctx", "chan"),
        P("ctx", "chan"),
        P("ctx", "chan"),
        P("ctx", "chan"),
        P(None, "chan"),
        P(None, "chan"),
    )
    return jax.shard_map(
        local,
        mesh=mesh,
        in_specs=placed,
        out_specs=(
            P("ctx", "chan"),
            P("ctx", "chan"),
            P("ctx", "chan"),
            P("ctx", "chan"),
            P(None, ("chan", "ctx")),
            P(None, ("chan", "ctx")),
        ),
        check_vma=False,
    )
```

profile of v0, /device:TPU:1, one launch (start us, length us, event | category | flops | bytes accessed | tf_op | source)
XLA Modules:
  0.0 1116.8 jit_solution(17943990118295323352)
XLA Ops:
  7.2 2.0 convert_multiply_fusion.1
  11.7 2.6 multiply_reduce_fusion.2
  19.2 97.6 %all-gather.7.cloned.1.call-done = f32[1024,512]{1,0:T(8,128)} async-done(((f32[16,512]{1,0:T(8,128)}), f32[1024,512]{1,0:T(8,128)}) %all-gather.7.cloned.1.call-update) | async-done | bytes 2097168 | tf_op jit(solution)/shard_map/all_gather | solution.py:14
  116.8 91.7 %all-gather.11.cloned.1.call-done = f32[1024,512]{1,0:T(8,128)} async-done(((f32[16,512]{1,0:T(8,128)}), f32[1024,512]{1,0:T(8,128)}) %all-gather.11.cloned.1.call-update) | async-done | bytes 2097168 | tf_op jit(solution)/shard_map/all_gather | solution.py:14
  208.5 52.4 %while.48 = (s32[]{:T(128)}, f32[16,512]{1,0:T(8,128)S(1)}, s32[]{:T(128)}, f32[64,16,512]{2,1,0:T(8,128)}, f32[64,16,512]{2,1,0:T(8,128)}, /*index=5*/s32[]{:T(128)}, s32[]{:T(128)}, s32[]{:T(128)}, s32[]{:T(128)}) while((s32[]{:T(128)}, f32[16,512]{1,0:T(8,128)S(1)}, s32[]{:T(128)}, f32[64,16,512]{2,1,0:T(8,128)}, ...), condition=%wide.region_5.6_spmd.clone, body=%wide.region_4.5_spmd.clone.sunk | while | flops 32776 | bytes 131235 | solution.py:27
  261.6 38.7 %all-gather.9.cloned.1.call-done = f32[1024,512]{1,0:T(8,128)} async-done(((f32[16,512]{1,0:T(8,128)}), f32[1024,512]{1,0:T(8,128)}) %all-gather.9.cloned.1.call-update) | async-done | bytes 2097168 | tf_op jit(solution)/shard_map/all_gather | solution.py:14
  300.2 52.0 %while.47 = (s32[]{:T(128)}, f32[16,512]{1,0:T(8,128)S(1)}, s32[]{:T(128)}, f32[64,16,512]{2,1,0:T(8,128)}, f32[64,16,512]{2,1,0:T(8,128)}, /*index=5*/s32[]{:T(128)}, s32[]{:T(128)}) while((s32[]{:T(128)}, f32[16,512]{1,0:T(8,128)S(1)}, s32[]{:T(128)}, f32[64,16,512]{2,1,0:T(8,128)}, f32[64,16,512]{2,1,0:T(8,128)}, ...), condition=%wide.region_2.3_spmd.clone, body=%wide.region_1.0_spmd.clone.sunk | while | flops 32772 | bytes 131173 | solution.py:27
  352.3 147.5 %while.49 = (s32[]{:T(128)}, f32[128,512]{1,0:T(8,128)}, f32[128,512]{1,0:T(8,128)}, f32[4,4,512]{2,1,0:T(4,128)}, f32[4,4,512]{2,1,0:T(4,128)}, /*index=5*/f32[...) while((s32[]{:T(128)}, f32[128,512]{1,0:T(8,128)}, ...), condition=%wide.region_13.14_spmd.clone, body=%wide.region_6.13_spmd.clone.sunk | while | flops 72481024 | bytes 17517256 | solution.py:90
  353.4 1.9 reduce_window_sum.25
  356.1 2.5 multiply_reduce_fusion.7
  358.6 27.0 %reduce_window_sum.26 = f32[4,128,512]{2,1,0:T(8,128)S(1)} reduce-window(f32[4,128,512]{2,1,0:T(8,128)S(1)} %get-tuple-element.655, f32[]{:T(128)} %constant.98.clone.8..sunk), window={size=1x128x1 pad=0_0x0_127x0_0}, to_apply=%region_9.9 | reduce-window | flops 33292288 | bytes 2097156 | tf_op jit(solution)/shard_map/while/body/eval_jaxpr/reduce_window_sum | solution.py:39
  389.5 1.9 reduce_window_sum.25
  392.2 2.5 multiply_reduce_fusion.7
  394.7 27.0 %reduce_window_sum.26 = f32[4,128,512]{2,1,0:T(8,128)S(1)} reduce-window(f32[4,128,512]{2,1,0:T(8,128)S(1)} %get-tuple-element.655, f32[]{:T(128)} %constant.98.clone.8..sunk), window={size=1x128x1 pad=0_0x0_127x0_0}, to_apply=%region_9.9 | reduce-window | flops 33292288 | bytes 2097156 | tf_op jit(solution)/shard_map/while/body/eval_jaxpr/reduce_window_sum | solution.py:39
  423.6 1.9 select_add_fusion.3
  426.6 1.9 reduce_window_sum.25
  429.3 2.5 multiply_reduce_fusion.7
  431.8 27.0 %reduce_window_sum.26 = f32[4,128,512]{2,1,0:T(8,128)S(1)} reduce-window(f32[4,128,512]{2,1,0:T(8,128)S(1)} %get-tuple-element.655, f32[]{:T(128)} %constant.98.clone.8..sunk), window={size=1x128x1 pad=0_0x0_127x0_0}, to_apply=%region_9.9 | reduce-window | flops 33292288 | bytes 2097156 | tf_op jit(solution)/shard_map/while/body/eval_jaxpr/reduce_window_sum | solution.py:39
  460.7 1.9 select_add_fusion.3
  463.7 1.9 reduce_window_sum.25
  466.4 2.5 multiply_reduce_fusion.7
  468.9 27.0 %reduce_window_sum.26 = f32[4,128,512]{2,1,0:T(8,128)S(1)} reduce-window(f32[4,128,512]{2,1,0:T(8,128)S(1)} %get-tuple-element.655, f32[]{:T(128)} %constant.98.clone.8..sunk), window={size=1x128x1 pad=0_0x0_127x0_0}, to_apply=%region_9.9 | reduce-window | flops 33292288 | bytes 2097156 | tf_op jit(solution)/shard_map/while/body/eval_jaxpr/reduce_window_sum | solution.py:39
  504.5 480.9 %all-reduce.5.cloned.1.call-done = (f32[16,512]{1,0:T(8,128)}, f32[16,512]{1,0:T(8,128)}) async-done(((f32[16,512]{1,0:T(8,128)}, f32[16,512]{1,0:T(8,128)}), (f32[16,512]{1,0:T(8,128)}, f32[16,512]{1,0:T(8,128)})) %all-reduce.5.cloned.1.call-update) | async-done | bytes 65552
  991.3 115.4 %psum.7 = f32[]{:T(128)} all-reduce(f32[]{:T(128)S(6)} %add.105), channel_id=1, replica_groups=mesh['ctx'=64,'chan'=16] {'ctx','chan'}, use_global_device_ids=true, to_apply=%region_18.19 | all-reduce | flops 1 | bytes 8 | tf_op jit(solution)/shard_map/psum | solution.py:101
  (219 shorter events, 138.2 us)
Async XLA Ops:
  7.2 7.2 copy-start.1
  7.2 7.2 copy-start.2
  7.2 109.6 %all-gather.7.cloned.1.call-start = ((), (), s32[]{:S(2)}) async-start(), calls=%async_computation | async-start | bytes 2129920 | tf_op jit(solution)/shard_map/all_gather | solution.py:14
  15.0 193.4 %all-gather.11.cloned.1.call-start = ((), (), s32[]{:S(2)}) async-start(), calls=%async_computation.2 | async-start | bytes 2129920 | tf_op jit(solution)/shard_map/all_gather | solution.py:14
  15.8 284.4 %all-gather.9.cloned.1.call-start = ((), (), s32[]{:S(2)}) async-start(), calls=%async_computation.1 | async-start | bytes 2129920 | tf_op jit(solution)/shard_map/all_gather | solution.py:14
  16.5 968.9 %all-reduce.5.cloned.1.call-start = ((), (), s32[]{:S(2)}) async-start(), calls=%async_computation.3 | async-start | bytes 131072
  358.6 27.7 %copy-start = (f32[4,128,512]{2,1,0:T(8,128)S(1)}, f32[4,128,512]{2,1,0:T(8,128)}, u32[]{:S(2)}) copy-start(f32[4,128,512]{2,1,0:T(8,128)} %get-tuple-element.654) | copy-start | bytes 3145732 | tf_op jit(solution)/shard_map/while
  394.7 27.7 %copy-start = (f32[4,128,512]{2,1,0:T(8,128)S(1)}, f32[4,128,512]{2,1,0:T(8,128)}, u32[]{:S(2)}) copy-start(f32[4,128,512]{2,1,0:T(8,128)} %get-tuple-element.654) | copy-start | bytes 3145732 | tf_op jit(solution)/shard_map/while
  431.8 27.7 %copy-start = (f32[4,128,512]{2,1,0:T(8,128)S(1)}, f32[4,128,512]{2,1,0:T(8,128)}, u32[]{:S(2)}) copy-start(f32[4,128,512]{2,1,0:T(8,128)} %get-tuple-element.654) | copy-start | bytes 3145732 | tf_op jit(solution)/shard_map/while
  468.9 27.7 %copy-start = (f32[4,128,512]{2,1,0:T(8,128)S(1)}, f32[4,128,512]{2,1,0:T(8,128)}, u32[]{:S(2)}) copy-start(f32[4,128,512]{2,1,0:T(8,128)} %get-tuple-element.654) | copy-start | bytes 3145732 | tf_op jit(solution)/shard_map/while
Sparse Core Ops, SparseCore 0:
  15.2 101.5 all-gather.6
  121.9 86.5 all-gather.10
  213.6 86.6 all-gather.8
  502.8 482.5 all-reduce.4
where the time goes:
time: 1130 us; the launch traced here: 1120 us
  waiting for transfers between devices  710 us (63%)
  other arithmetic  255 us (23%)
  blocking collectives  115 us (10%)
  between operations  16.5 us (1%)
  local copies, waits for them, and re-layouts  15.4 us (1%)
    unnamed x5, waiting for transfers between devices  482 us
    all_gather x3, waiting for transfers between devices, carried_in(): everything = jax.tree.map(lambda part: lax.all_gather(part, axis), shard)  228 us
    psum x1, blocking collectives, local(): lax.psum(jnp.sum(own_residue * own_residue) + jnp.sum(own_lograte * own_l...  115 us
    another operation x4, other arithmetic, local_pieces(): lax.cumsum(falling * (mixing[:, None, :] * drive[None]), axis=1, reverse=...  108 us
    select_n x128, other arithmetic, hop(): return jax.tree.map(lambda a, b: jnp.where(reached, a, b), new, before)  101 us
  transfers between devices with their start and end apart: 4, of which 4 were waited for; matrix products, arithmetic and copies ran while one was open for 5% of the time, Pallas kernels for 0%

commit v1 on v0

v1 whole, which is shorter than its diff:
```python
import math

import jax
import jax.numpy as jnp
from jax import lax
from jax.sharding import PartitionSpec as P

WIDTH = 8192
MODES = 16

HIGHEST = lax.Precision.HIGHEST


def from_lower(x, axis, d, n):
    return lax.ppermute(x, axis, [(j, j + d) for j in range(n - d)])


def from_upper(x, axis, d, n):
    return lax.ppermute(x, axis, [(j + d, j) for j in range(n - d)])


def exclusive_scan(values, rates, steps, axis, n, shift):
    if n == 1:
        return jnp.zeros_like(values)
    window = 1
    result = shift(values, axis, 1, n)
    if n > 2:
        result = result + jnp.exp(-rates * steps) * shift(values, axis, 2, n)
        window = 2
    while window < n:
        result = result + jnp.exp(-rates * (steps * window)) * shift(result, axis, window, n)
        window *= 2
    return result


def butterfly_sum(x, axis, n):
    d = 1
    while d < n:
        x = x + lax.ppermute(x, axis, [(j, j ^ d) for j in range(n)])
        d *= 2
    return x


def local(query_gate, key_gate, value_input, cotangent, residues, decay_rate):
    steps = query_gate.shape[0]
    modes, columns = residues.shape
    peers = lax.axis_size("ctx")
    lanes = lax.axis_size("chan")
    assert peers & (peers - 1) == 0 and lanes & (lanes - 1) == 0
    query = query_gate.astype(jnp.float32)
    keyed = key_gate.astype(jnp.float32)
    values = value_input.astype(jnp.float32)
    upstream = cotangent.astype(jnp.float32)
    source = keyed * values
    drive = upstream * query
    decay = jnp.exp(-decay_rate)
    norm_factor = jnp.sqrt(-jnp.expm1(-2.0 * decay_rate))
    mixing = residues * norm_factor

    rate = decay_rate[None]
    where = jnp.arange(steps, dtype=jnp.float32)[:, None, None]
    rising = jnp.exp(rate * where)
    falling = jnp.exp(-rate * where)

    ends = jnp.sum(jnp.exp(-rate * (steps - 1.0 - where)) * source[:, None, :], axis=0)
    heads = mixing * jnp.sum(falling * drive[:, None, :], axis=0)
    incoming = exclusive_scan(ends, decay_rate, steps, "ctx", peers, from_lower)
    upper = exclusive_scan(heads, decay_rate, steps, "ctx", peers, from_upper)

    row = jnp.arange(steps)[:, None]
    col = jnp.arange(steps)[None, :]
    lower_tri = (col <= row).astype(jnp.float32)
    upper_tri = (col >= row).astype(jnp.float32)
    flat = (steps, modes * columns)
    climbed = (rising * source[:, None, :]).reshape(flat)
    fallen = (falling * (mixing[None] * drive[:, None, :])).reshape(flat)
    states0 = falling * jnp.dot(lower_tri, climbed, precision=HIGHEST).reshape(rising.shape)
    adjoint0 = rising * jnp.dot(upper_tri, fallen, precision=HIGHEST).reshape(rising.shape)

    states = states0 + jnp.exp(-rate * (where + 1.0)) * incoming[None]
    adjoint = adjoint0 + jnp.exp(-rate * (steps - where)) * upper[None]
    previous = jnp.concatenate([incoming[None], states[:-1]], axis=0)
    mixed = jnp.sum(mixing[None] * states, axis=1)
    grad_source = jnp.sum(adjoint, axis=1)
    grad_w = jnp.sum(drive[:, None, :] * states, axis=0)
    grad_a = jnp.sum(adjoint * previous, axis=0)

    sums = butterfly_sum(jnp.stack([grad_w, grad_a]), "ctx", peers)
    grad_mixing, grad_decay = sums[0], sums[1]
    raw_residue = grad_mixing * norm_factor
    raw_lograte = decay_rate * (
        grad_mixing * residues * decay * decay / norm_factor - decay * grad_decay
    )
    part = jnp.sum(raw_residue * raw_residue) + jnp.sum(raw_lograte * raw_lograte)
    total = butterfly_sum(part.reshape(1), "chan", lanes)[0]
    limit = math.sqrt(2.0 * MODES * WIDTH)
    scale = jnp.minimum(1.0, limit / jnp.sqrt(total + 1e-06))
    width = columns // peers
    at = lax.axis_index("ctx") * width
    own_residue = lax.dynamic_slice_in_dim(raw_residue, at, width, axis=1)
    own_lograte = lax.dynamic_slice_in_dim(raw_lograte, at, width, axis=1)
    output = (query * mixed).astype(jnp.bfloat16)
    grad_query = (upstream * mixed).astype(jnp.bfloat16)
    grad_key = (grad_source * values).astype(jnp.bfloat16)
    grad_value = (grad_source * keyed).astype(jnp.bfloat16)
    return (output, grad_query, grad_key, grad_value, own_residue * scale, own_lograte * scale)


def solution(mesh):
    placed = (
        P("ctx", "chan"),
        P("ctx", "chan"),
        P("ctx", "chan"),
        P("ctx", "chan"),
        P(None, "chan"),
        P(None, "chan"),
    )
    return jax.shard_map(
        local,
        mesh=mesh,
        in_specs=placed,
        out_specs=(
            P("ctx", "chan"),
            P("ctx", "chan"),
            P("ctx", "chan"),
            P("ctx", "chan"),
            P(None, ("chan", "ctx")),
            P(None, ("chan", "ctx")),
        ),
        check_vma=False,
    )
```

time: 1130 us -> 231 us (0.20)
  the two profiles are of different devices: /device:TPU:1 before, /device:TPU:116 now
where the time goes in v1:
time: 231 us; the launch traced here: 230 us
  waiting for transfers between devices  111 us (48%)
  starting transfers between devices  87.7 us (38%)
  other arithmetic  13.4 us (6%)
  matrix products  10.6 us (5%)
  between operations  4.95 us (2%)
    ppermute x7, waiting for transfers between devices, from_upper(): return lax.ppermute(x, axis, [(j + d, j) for j in range(n - d)])  62.2 us
    ppermute x10, starting transfers between devices, butterfly_sum(): x = x + lax.ppermute(x, axis, [(j, j ^ d) for j in range(n)])  43.5 us
    ppermute x10, waiting for transfers between devices, butterfly_sum(): x = x + lax.ppermute(x, axis, [(j, j ^ d) for j in range(n)])  34.2 us
    ppermute x7, starting transfers between devices, from_lower(): return lax.ppermute(x, axis, [(j, j + d) for j in range(n - d)])  26.9 us
    ppermute x7, starting transfers between devices, from_upper(): return lax.ppermute(x, axis, [(j + d, j) for j in range(n - d)])  17.2 us
    ppermute x7, waiting for transfers between devices, from_lower(): return lax.ppermute(x, axis, [(j, j + d) for j in range(n - d)])  14.8 us
    dot_general x1, matrix products, local(): jnp.dot(lower_tri, climbed, precision=HIGHEST).reshape(rising.shape)  6.07 us
  transfers between devices with their start and end apart: 24, of which 22 were waited for; matrix products, arithmetic and copies ran while one was open for 2% of the time, Pallas kernels for 0%

profile of v1, /device:TPU:116, one launch (start us, length us, event | category | flops | bytes accessed | tf_op | source)
XLA Modules:
  0.0 229.5 jit_solution(685975652308061788)
XLA Ops:
  5.2 3.9 %collective-permute-start.1 = (f32[16,512]{1,0:T(8,128)S(1)}, f32[16,512]{1,0:T(8,128)S(1)}, u32[]{:S(2)}, u32[]{:S(2)}) collective-permute-start(f32[16,512]{1,0:T(8,128)S(1)} %multiply_reduce_fusion.3), channel_id=1, source_target_pairs={{0,32},{16,48},{32,64},{48,80},{64,96},{80,112},{96,128},{112,144}... | collective-permute-start | bytes 98312 | tf_op jit(solution)/shard_map/ppermute | solution.py:15
  11.8 8.5 %collective-permute-start.2 = (f32[16,512]{1,0:T(8,128)S(1)}, f32[16,512]{1,0:T(8,128)S(1)}, u32[]{:S(2)}, u32[]{:S(2)}) collective-permute-start(f32[16,512]{1,0:T(8,128)S(1)} %multiply_add_fusion.13), channel_id=1, source_target_pairs={{0,32},{16,48},{32,64},{48,80},{64,96},{80,112},{96,128},{112,144}... | collective-permute-start | bytes 98312 | tf_op jit(solution)/shard_map/ppermute | solution.py:15
  22.6 3.7 %collective-permute-start.3 = (f32[16,512]{1,0:T(8,128)S(1)}, f32[16,512]{1,0:T(8,128)S(1)}, u32[]{:S(2)}, u32[]{:S(2)}) collective-permute-start(f32[16,512]{1,0:T(8,128)S(1)} %get-tuple-element.36), channel_id=1, source_target_pairs={{0,64},{16,80},{32,96},{48,112},{64,128},{80,144},{96,160},{112,17... | collective-permute-start | bytes 98312 | tf_op jit(solution)/shard_map/ppermute | solution.py:15
  30.1 5.2 %collective-permute-start.4 = (f32[16,512]{1,0:T(8,128)S(1)}, f32[16,512]{1,0:T(8,128)S(1)}, u32[]{:S(2)}, u32[]{:S(2)}) collective-permute-start(f32[16,512]{1,0:T(8,128)S(1)} %multiply_add_fusion.11), channel_id=1, source_target_pairs={{0,128},{16,144},{32,160},{48,176},{64,192},{80,208},{96,224},{112... | collective-permute-start | bytes 98312 | tf_op jit(solution)/shard_map/ppermute | solution.py:15
  35.4 4.6 %collective-permute-done.4 = f32[16,512]{1,0:T(8,128)S(1)} collective-permute-done((f32[16,512]{1,0:T(8,128)S(1)}, f32[16,512]{1,0:T(8,128)S(1)}, u32[]{:S(2)}, u32[]{:S(2)}) %collective-permute-start.4) | collective-permute-done | bytes 32800 | tf_op jit(solution)/shard_map/ppermute | solution.py:15
  43.8 3.6 %collective-permute-done.5 = f32[16,512]{1,0:T(8,128)S(1)} collective-permute-done((f32[16,512]{1,0:T(8,128)S(1)}, f32[16,512]{1,0:T(8,128)S(1)}, u32[]{:S(2)}, u32[]{:S(2)}) %collective-permute-start.5) | collective-permute-done | bytes 32800 | tf_op jit(solution)/shard_map/ppermute | solution.py:15
  51.4 6.1 %multiply_reduce_fusion = (f32[16,512]{1,0:T(8,128)S(1)}, f32[128,512]{1,0:T(8,128)S(1)}, f32[16,512]{1,0:T(8,128)S(1)}, f32[128,16,512]{2,0,1:T(8,128)}) fusion(f32[128,512]{1,0:T(8,128)S(1)} %convert_multiply_fusion, f32[16,512]{1,0:T(8,128)S(1)} %get-tuple-element.35, f32[16,512]{1,0:T(8,128)S(1)} %neg.6, f32[16,512]{1,0:T(8,128)S(1)} %multiply_add_fusion.8, ...), kind=kOutput, calls=%fused_computation.5 | convolution fusion | flops 1622081536 | bytes 9077248 | tf_op jit(solution)/shard_map/dot_general | solution.py:77
  59.5 6.2 %collective-permute-start.8 = (f32[16,512]{1,0:T(8,128)S(1)}, f32[16,512]{1,0:T(8,128)S(1)}, u32[]{:S(2)}, u32[]{:S(2)}) collective-permute-start(f32[16,512]{1,0:T(8,128)S(1)} %mul.344), channel_id=1, source_target_pairs={{32,0},{48,16},{64,32},{80,48},{96,64},{112,80},{128,96},{144,112}... | collective-permute-start | bytes 98312 | tf_op jit(solution)/shard_map/ppermute | solution.py:19
  65.7 19.6 %collective-permute-done.8 = f32[16,512]{1,0:T(8,128)S(1)} collective-permute-done((f32[16,512]{1,0:T(8,128)S(1)}, f32[16,512]{1,0:T(8,128)S(1)}, u32[]{:S(2)}, u32[]{:S(2)}) %collective-permute-start.8) | collective-permute-done | bytes 32800 | tf_op jit(solution)/shard_map/ppermute | solution.py:19
  87.3 8.2 %collective-permute-done.9 = f32[16,512]{1,0:T(8,128)S(1)} collective-permute-done((f32[16,512]{1,0:T(8,128)S(1)}, f32[16,512]{1,0:T(8,128)S(1)}, u32[]{:S(2)}, u32[]{:S(2)}) %collective-permute-start.9) | collective-permute-done | bytes 32800 | tf_op jit(solution)/shard_map/ppermute | solution.py:19
  97.4 9.0 %collective-permute-done.10 = f32[16,512]{1,0:T(8,128)S(1)} collective-permute-done((f32[16,512]{1,0:T(8,128)S(1)}, f32[16,512]{1,0:T(8,128)S(1)}, u32[]{:S(2)}, u32[]{:S(2)}) %collective-permute-start.10) | collective-permute-done | bytes 32800 | tf_op jit(solution)/shard_map/ppermute | solution.py:19
  108.4 10.8 %collective-permute-done.11 = f32[16,512]{1,0:T(8,128)S(1)} collective-permute-done((f32[16,512]{1,0:T(8,128)S(1)}, f32[16,512]{1,0:T(8,128)S(1)}, u32[]{:S(2)}, u32[]{:S(2)}) %collective-permute-start.11) | collective-permute-done | bytes 32800 | tf_op jit(solution)/shard_map/ppermute | solution.py:19
  121.1 6.3 %collective-permute-done.12 = f32[16,512]{1,0:T(8,128)S(1)} collective-permute-done((f32[16,512]{1,0:T(8,128)S(1)}, f32[16,512]{1,0:T(8,128)S(1)}, u32[]{:S(2)}, u32[]{:S(2)}) %collective-permute-start.12) | collective-permute-done | bytes 32800 | tf_op jit(solution)/shard_map/ppermute | solution.py:19
  128.9 8.2 %collective-permute-done.13 = f32[16,512]{1,0:T(8,128)S(1)} collective-permute-done((f32[16,512]{1,0:T(8,128)S(1)}, f32[16,512]{1,0:T(8,128)S(1)}, u32[]{:S(2)}, u32[]{:S(2)}) %collective-permute-start.13) | collective-permute-done | bytes 32800 | tf_op jit(solution)/shard_map/ppermute | solution.py:19
  139.6 4.5 %fusion = (f32[16,512]{1,0:T(8,128)S(1)}, f32[128,512]{1,0:T(8,128)S(1)}) fusion(f32[127,16,512]{2,0,1:T(8,128)S(1)} %bitcast.66, f32[1,16,512]{2,0,1:T(1,128)S(1)} %broadcast_in_dim.2, f32[16,512]{1,0:T(8,128)S(1)} %get-tuple-element.33, f32[128]{0:T(128)S(1)} %iota_subtract_fusion, f32[16,512]{1,0:T(8,128)S(1)} %copy-done, f32[16,512]{1,0:T(8,128)S(1)} %neg.6, ...), kind=kOutput, calls=%fused_computation.1 | convolution fusion | flops 1619992576 | bytes 8782336 | tf_op jit(solution)/shard_map/dot_general | solution.py:78
  149.3 4.2 %collective-permute-done.15 = f32[2,16,512]{2,1,0:T(8,128)S(1)} collective-permute-done((f32[2,16,512]{2,1,0:T(8,128)S(1)}, f32[2,16,512]{2,1,0:T(8,128)S(1)}, u32[]{:S(2)}, u32[]{:S(2)}) %collective-permute-start.15) | collective-permute-done | bytes 65568 | tf_op jit(solution)/shard_map/ppermute | solution.py:39
  155.4 5.5 %collective-permute-done.16 = f32[2,16,512]{2,1,0:T(8,128)S(1)} collective-permute-done((f32[2,16,512]{2,1,0:T(8,128)S(1)}, f32[2,16,512]{2,1,0:T(8,128)S(1)}, u32[]{:S(2)}, u32[]{:S(2)}) %collective-permute-start.16) | collective-permute-done | bytes 65568 | tf_op jit(solution)/shard_map/ppermute | solution.py:39
  162.8 8.1 %collective-permute-done.17 = f32[2,16,512]{2,1,0:T(8,128)S(1)} collective-permute-done((f32[2,16,512]{2,1,0:T(8,128)S(1)}, f32[2,16,512]{2,1,0:T(8,128)S(1)}, u32[]{:S(2)}, u32[]{:S(2)}) %collective-permute-start.17) | collective-permute-done | bytes 65568 | tf_op jit(solution)/shard_map/ppermute | solution.py:39
  173.7 4.9 %collective-permute-done.18 = f32[2,16,512]{2,1,0:T(8,128)S(1)} collective-permute-done((f32[2,16,512]{2,1,0:T(8,128)S(1)}, f32[2,16,512]{2,1,0:T(8,128)S(1)}, u32[]{:S(2)}, u32[]{:S(2)}) %collective-permute-start.18) | collective-permute-done | bytes 65568 | tf_op jit(solution)/shard_map/ppermute | solution.py:39
  181.3 7.5 %collective-permute-done.19 = f32[2,16,512]{2,1,0:T(8,128)S(1)} collective-permute-done((f32[2,16,512]{2,1,0:T(8,128)S(1)}, f32[2,16,512]{2,1,0:T(8,128)S(1)}, u32[]{:S(2)}, u32[]{:S(2)}) %collective-permute-start.19) | collective-permute-done | bytes 65568 | tf_op jit(solution)/shard_map/ppermute | solution.py:39
  190.8 6.5 %collective-permute-start.20 = (f32[1]{0:T(128)}, f32[1]{0:T(128)}, u32[]{:S(2)}, u32[]{:S(2)}) collective-permute-start(f32[1]{0:T(128)} %bitcast.12), channel_id=1, source_target_pairs={{0,1},{1,0},{2,3},{3,2},{4,5},{5,4},{6,7},{7,6},{8,9},{9,8},{10,11... | collective-permute-start | bytes 20 | tf_op jit(solution)/shard_map/ppermute | solution.py:39
  198.1 9.2 %collective-permute-start.21 = (f32[1]{0:T(128)}, f32[1]{0:T(128)}, u32[]{:S(2)}, u32[]{:S(2)}) collective-permute-start(f32[1]{0:T(128)} %add.118), channel_id=1, source_target_pairs={{0,2},{1,3},{2,0},{3,1},{4,6},{5,7},{6,4},{7,5},{8,10},{9,11},{10,... | collective-permute-start | bytes 20 | tf_op jit(solution)/shard_map/ppermute | solution.py:39
  208.1 13.1 %collective-permute-start.22 = (f32[1]{0:T(128)}, f32[1]{0:T(128)}, u32[]{:S(2)}, u32[]{:S(2)}) collective-permute-start(f32[1]{0:T(128)} %add.119), channel_id=1, source_target_pairs={{0,4},{1,5},{2,6},{3,7},{4,0},{5,1},{6,2},{7,3},{8,12},{9,13},{10,... | collective-permute-start | bytes 20 | tf_op jit(solution)/shard_map/ppermute | solution.py:39
  222.1 3.2 %collective-permute-start.23 = (f32[1]{0:T(128)}, f32[1]{0:T(128)}, u32[]{:S(2)}, u32[]{:S(2)}) collective-permute-start(f32[1]{0:T(128)} %add.120), channel_id=1, source_target_pairs={{0,8},{1,9},{2,10},{3,11},{4,12},{5,13},{6,14},{7,15},{8,0},{9,1},... | collective-permute-start | bytes 20 | tf_op jit(solution)/shard_map/ppermute | solution.py:39
  (81 shorter events, 53.9 us)
Async XLA Ops:
  3.3 5.9 %collective-permute-start = (f32[16,512]{1,0:T(8,128)S(1)}, f32[16,512]{1,0:T(8,128)S(1)}, u32[]{:S(2)}, u32[]{:S(2)}) collective-permute-start(f32[16,512]{1,0:T(8,128)S(1)} %multiply_reduce_fusion.3), channel_id=1, source_target_pairs={{0,16},{16,32},{32,48},{48,64},{64,80},{80,96},{96,112},{112,128},... | collective-permute-start | bytes 98312 | tf_op jit(solution)/shard_map/ppermute | solution.py:15
  5.2 5.8 %collective-permute-start.1 = (f32[16,512]{1,0:T(8,128)S(1)}, f32[16,512]{1,0:T(8,128)S(1)}, u32[]{:S(2)}, u32[]{:S(2)}) collective-permute-start(f32[16,512]{1,0:T(8,128)S(1)} %multiply_reduce_fusion.3), channel_id=1, source_target_pairs={{0,32},{16,48},{32,64},{48,80},{64,96},{80,112},{96,128},{112,144}... | collective-permute-start | bytes 98312 | tf_op jit(solution)/shard_map/ppermute | solution.py:15
  11.8 10.1 %collective-permute-start.2 = (f32[16,512]{1,0:T(8,128)S(1)}, f32[16,512]{1,0:T(8,128)S(1)}, u32[]{:S(2)}, u32[]{:S(2)}) collective-permute-start(f32[16,512]{1,0:T(8,128)S(1)} %multiply_add_fusion.13), channel_id=1, source_target_pairs={{0,32},{16,48},{32,64},{48,80},{64,96},{80,112},{96,128},{112,144}... | collective-permute-start | bytes 98312 | tf_op jit(solution)/shard_map/ppermute | solution.py:15
  22.6 6.7 %collective-permute-start.3 = (f32[16,512]{1,0:T(8,128)S(1)}, f32[16,512]{1,0:T(8,128)S(1)}, u32[]{:S(2)}, u32[]{:S(2)}) collective-permute-start(f32[16,512]{1,0:T(8,128)S(1)} %get-tuple-element.36), channel_id=1, source_target_pairs={{0,64},{16,80},{32,96},{48,112},{64,128},{80,144},{96,160},{112,17... | collective-permute-start | bytes 98312 | tf_op jit(solution)/shard_map/ppermute | solution.py:15
  30.1 9.8 %collective-permute-start.4 = (f32[16,512]{1,0:T(8,128)S(1)}, f32[16,512]{1,0:T(8,128)S(1)}, u32[]{:S(2)}, u32[]{:S(2)}) collective-permute-start(f32[16,512]{1,0:T(8,128)S(1)} %multiply_add_fusion.11), channel_id=1, source_target_pairs={{0,128},{16,144},{32,160},{48,176},{64,192},{80,208},{96,224},{112... | collective-permute-start | bytes 98312 | tf_op jit(solution)/shard_map/ppermute | solution.py:15
  40.7 6.7 %collective-permute-start.5 = (f32[16,512]{1,0:T(8,128)S(1)}, f32[16,512]{1,0:T(8,128)S(1)}, u32[]{:S(2)}, u32[]{:S(2)}) collective-permute-start(f32[16,512]{1,0:T(8,128)S(1)} %multiply_add_fusion.10), channel_id=1, source_target_pairs={{0,256},{16,272},{32,288},{48,304},{64,320},{80,336},{96,352},{112... | collective-permute-start | bytes 98312 | tf_op jit(solution)/shard_map/ppermute | solution.py:15
  48.2 3.1 %collective-permute-start.6 = (f32[16,512]{1,0:T(8,128)S(1)}, f32[16,512]{1,0:T(8,128)S(1)}, u32[]{:S(2)}, u32[]{:S(2)}) collective-permute-start(f32[16,512]{1,0:T(8,128)S(1)} %multiply_add_fusion.9), channel_id=1, source_target_pairs={{0,512},{16,528},{32,544},{48,560},{64,576},{80,592},{96,608},{112... | collective-permute-start | bytes 98312 | tf_op jit(solution)/shard_map/ppermute | solution.py:15
  57.4 8.3 %collective-permute-start.7 = (f32[16,512]{1,0:T(8,128)S(1)}, f32[16,512]{1,0:T(8,128)S(1)}, u32[]{:S(2)}, u32[]{:S(2)}) collective-permute-start(f32[16,512]{1,0:T(8,128)S(1)} %mul.344), channel_id=1, source_target_pairs={{16,0},{32,16},{48,32},{64,48},{80,64},{96,80},{112,96},{128,112},... | collective-permute-start | bytes 98312 | tf_op jit(solution)/shard_map/ppermute | solution.py:19
  59.5 25.8 %collective-permute-start.8 = (f32[16,512]{1,0:T(8,128)S(1)}, f32[16,512]{1,0:T(8,128)S(1)}, u32[]{:S(2)}, u32[]{:S(2)}) collective-permute-start(f32[16,512]{1,0:T(8,128)S(1)} %mul.344), channel_id=1, source_target_pairs={{32,0},{48,16},{64,32},{80,48},{96,64},{112,80},{128,96},{144,112}... | collective-permute-start | bytes 98312 | tf_op jit(solution)/shard_map/ppermute | solution.py:19
  85.4 10.1 %collective-permute-start.9 = (f32[16,512]{1,0:T(8,128)S(1)}, f32[16,512]{1,0:T(8,128)S(1)}, u32[]{:S(2)}, u32[]{:S(2)}) collective-permute-start(f32[16,512]{1,0:T(8,128)S(1)} %multiply_add_fusion.7), channel_id=1, source_target_pairs={{32,0},{48,16},{64,32},{80,48},{96,64},{112,80},{128,96},{144,112}... | collective-permute-start | bytes 98312 | tf_op jit(solution)/shard_map/ppermute | solution.py:19
  95.5 10.9 %collective-permute-start.10 = (f32[16,512]{1,0:T(8,128)S(1)}, f32[16,512]{1,0:T(8,128)S(1)}, u32[]{:S(2)}, u32[]{:S(2)}) collective-permute-start(f32[16,512]{1,0:T(8,128)S(1)} %multiply_add_fusion.6), channel_id=1, source_target_pairs={{64,0},{80,16},{96,32},{112,48},{128,64},{144,80},{160,96},{176,11... | collective-permute-start | bytes 98312 | tf_op jit(solution)/shard_map/ppermute | solution.py:19
  106.5 12.7 %collective-permute-start.11 = (f32[16,512]{1,0:T(8,128)S(1)}, f32[16,512]{1,0:T(8,128)S(1)}, u32[]{:S(2)}, u32[]{:S(2)}) collective-permute-start(f32[16,512]{1,0:T(8,128)S(1)} %multiply_add_fusion.5), channel_id=1, source_target_pairs={{128,0},{144,16},{160,32},{176,48},{192,64},{208,80},{224,96},{240... | collective-permute-start | bytes 98312 | tf_op jit(solution)/shard_map/ppermute | solution.py:19
  119.2 8.2 %collective-permute-start.12 = (f32[16,512]{1,0:T(8,128)S(1)}, f32[16,512]{1,0:T(8,128)S(1)}, u32[]{:S(2)}, u32[]{:S(2)}) collective-permute-start(f32[16,512]{1,0:T(8,128)S(1)} %multiply_add_fusion.4), channel_id=1, source_target_pairs={{256,0},{272,16},{288,32},{304,48},{320,64},{336,80},{352,96},{368... | collective-permute-start | bytes 98312 | tf_op jit(solution)/shard_map/ppermute | solution.py:19
  127.4 9.7 %collective-permute-start.13 = (f32[16,512]{1,0:T(8,128)S(1)}, f32[16,512]{1,0:T(8,128)S(1)}, u32[]{:S(2)}, u32[]{:S(2)}) collective-permute-start(f32[16,512]{1,0:T(8,128)S(1)} %multiply_add_fusion.3), channel_id=1, source_target_pairs={{512,0},{528,16},{544,32},{560,48},{576,64},{592,80},{608,96},{624... | collective-permute-start | bytes 98312 | tf_op jit(solution)/shard_map/ppermute | solution.py:19
  144.2 3.1 %collective-permute-start.14 = (f32[2,16,512]{2,1,0:T(8,128)S(1)}, f32[2,16,512]{2,1,0:T(8,128)S(1)}, u32[]{:S(2)}, u32[]{:S(2)}) collective-permute-start(f32[2,16,512]{2,1,0:T(8,128)S(1)} %pad_maximum_fusion), channel_id=1, source_target_pairs={{0,16},{16,0},{32,48},{48,32},{64,80},{80,64},{96,112},{112,96},{1... | collective-permute-start | bytes 196616 | tf_op jit(solution)/shard_map/ppermute | solution.py:39
  147.3 6.2 %collective-permute-start.15 = (f32[2,16,512]{2,1,0:T(8,128)S(1)}, f32[2,16,512]{2,1,0:T(8,128)S(1)}, u32[]{:S(2)}, u32[]{:S(2)}) collective-permute-start(f32[2,16,512]{2,1,0:T(8,128)S(1)} %fusion.21), channel_id=1, source_target_pairs={{0,32},{16,48},{32,0},{48,16},{64,96},{80,112},{96,64},{112,80},{1... | collective-permute-start | bytes 196616 | tf_op jit(solution)/shard_map/ppermute | solution.py:39
  153.5 7.4 %collective-permute-start.16 = (f32[2,16,512]{2,1,0:T(8,128)S(1)}, f32[2,16,512]{2,1,0:T(8,128)S(1)}, u32[]{:S(2)}, u32[]{:S(2)}) collective-permute-start(f32[2,16,512]{2,1,0:T(8,128)S(1)} %fusion.26), channel_id=1, source_target_pairs={{0,64},{16,80},{32,96},{48,112},{64,0},{80,16},{96,32},{112,48},{1... | collective-permute-start | bytes 196616 | tf_op jit(solution)/shard_map/ppermute | solution.py:39
  160.9 10.1 %collective-permute-start.17 = (f32[2,16,512]{2,1,0:T(8,128)S(1)}, f32[2,16,512]{2,1,0:T(8,128)S(1)}, u32[]{:S(2)}, u32[]{:S(2)}) collective-permute-start(f32[2,16,512]{2,1,0:T(8,128)S(1)} %add.112), channel_id=1, source_target_pairs={{0,128},{16,144},{32,160},{48,176},{64,192},{80,208},{96,224},{112... | collective-permute-start | bytes 196616 | tf_op jit(solution)/shard_map/ppermute | solution.py:39
  171.0 7.6 %collective-permute-start.18 = (f32[2,16,512]{2,1,0:T(8,128)S(1)}, f32[2,16,512]{2,1,0:T(8,128)S(1)}, u32[]{:S(2)}, u32[]{:S(2)}) collective-permute-start(f32[2,16,512]{2,1,0:T(8,128)S(1)} %add.113), channel_id=1, source_target_pairs={{0,256},{16,272},{32,288},{48,304},{64,320},{80,336},{96,352},{112... | collective-permute-start | bytes 196616 | tf_op jit(solution)/shard_map/ppermute | solution.py:39
  178.6 10.2 %collective-permute-start.19 = (f32[2,16,512]{2,1,0:T(8,128)S(1)}, f32[2,16,512]{2,1,0:T(8,128)S(1)}, u32[]{:S(2)}, u32[]{:S(2)}) collective-permute-start(f32[2,16,512]{2,1,0:T(8,128)S(1)} %add.114), channel_id=1, source_target_pairs={{0,512},{16,528},{32,544},{48,560},{64,576},{80,592},{96,608},{112... | collective-permute-start | bytes 196616 | tf_op jit(solution)/shard_map/ppermute | solution.py:39
  190.8 6.7 %collective-permute-start.20 = (f32[1]{0:T(128)}, f32[1]{0:T(128)}, u32[]{:S(2)}, u32[]{:S(2)}) collective-permute-start(f32[1]{0:T(128)} %bitcast.12), channel_id=1, source_target_pairs={{0,1},{1,0},{2,3},{3,2},{4,5},{5,4},{6,7},{7,6},{8,9},{9,8},{10,11... | collective-permute-start | bytes 20 | tf_op jit(solution)/shard_map/ppermute | solution.py:39
  198.1 9.4 %collective-permute-start.21 = (f32[1]{0:T(128)}, f32[1]{0:T(128)}, u32[]{:S(2)}, u32[]{:S(2)}) collective-permute-start(f32[1]{0:T(128)} %add.118), channel_id=1, source_target_pairs={{0,2},{1,3},{2,0},{3,1},{4,6},{5,7},{6,4},{7,5},{8,10},{9,11},{10,... | collective-permute-start | bytes 20 | tf_op jit(solution)/shard_map/ppermute | solution.py:39
  208.1 13.3 %collective-permute-start.22 = (f32[1]{0:T(128)}, f32[1]{0:T(128)}, u32[]{:S(2)}, u32[]{:S(2)}) collective-permute-start(f32[1]{0:T(128)} %add.119), channel_id=1, source_target_pairs={{0,4},{1,5},{2,6},{3,7},{4,0},{5,1},{6,2},{7,3},{8,12},{9,13},{10,... | collective-permute-start | bytes 20 | tf_op jit(solution)/shard_map/ppermute | solution.py:39
  222.1 5.4 %collective-permute-start.23 = (f32[1]{0:T(128)}, f32[1]{0:T(128)}, u32[]{:S(2)}, u32[]{:S(2)}) collective-permute-start(f32[1]{0:T(128)} %add.120), channel_id=1, source_target_pairs={{0,8},{1,9},{2,10},{3,11},{4,12},{5,13},{6,14},{7,15},{8,0},{9,1},... | collective-permute-start | bytes 20 | tf_op jit(solution)/shard_map/ppermute | solution.py:39
  (7 other events, 257.9 us)

commit v2 on v1

--- a/solution.py
+++ b/solution.py
@@ -9,35 +9,56 @@
 MODES = 16
 
 HIGHEST = lax.Precision.HIGHEST
+CTX_GROUPS = (2, 8, 4)
+CHAN_GROUPS = (8, 2)
 
 
-def from_lower(x, axis, d, n):
-    return lax.ppermute(x, axis, [(j, j + d) for j in range(n - d)])
+def levels_of(n, groups):
+    out, stride = [], 1
+    for size in groups:
+        out.append((stride, size))
+        stride *= size
+    assert stride == n
+    return out
 
 
-def from_upper(x, axis, d, n):
-    return lax.ppermute(x, axis, [(j + d, j) for j in range(n - d)])
+def level_gather(x, axis, n, stride, size):
+    got = []
+    for q in range(1, size):
+        perm = []
+        for i in range(n):
+            r = (i // stride) % size
+            perm.append((i, i + ((r + q) % size - r) * stride))
+        got.append(lax.ppermute(x, axis, perm))
+    return got
 
 
-def exclusive_scan(values, rates, steps, axis, n, shift):
-    if n == 1:
-        return jnp.zeros_like(values)
-    window = 1
-    result = shift(values, axis, 1, n)
-    if n > 2:
-        result = result + jnp.exp(-rates * steps) * shift(values, axis, 2, n)
-        window = 2
-    while window < n:
-        result = result + jnp.exp(-rates * (steps * window)) * shift(result, axis, window, n)
-        window *= 2
-    return result
+def carried_scan(ends, heads, rates, steps, axis, n, groups):
+    index = lax.axis_index(axis)
+    power = lambda k: jnp.exp(-rates * (steps * k.astype(jnp.float32)))
+    incoming = jnp.zeros_like(ends)
+    upper = jnp.zeros_like(heads)
+    total, btotal = ends, heads
+    for stride, size in levels_of(n, groups):
+        r = (index // stride) % size
+        p = index % stride
+        got = level_gather(jnp.stack([total, btotal]), axis, n, stride, size)
+        new_total = power((size - 1 - r) * stride) * total
+        new_btotal = power(r * stride) * btotal
+        for q, pair in zip(range(1, size), got):
+            rq = (r - q) % size
+            lower = q <= r
+            incoming = incoming + jnp.where(lower, power((q - 1) * stride + p) * pair[0], 0.0)
+            upper = upper + jnp.where(lower, 0.0, power((size - q) * stride - p - 1) * pair[1])
+            new_total = new_total + power((size - 1 - rq) * stride) * pair[0]
+            new_btotal = new_btotal + power(rq * stride) * pair[1]
+        total, btotal = new_total, new_btotal
+    return incoming, upper
 
 
-def butterfly_sum(x, axis, n):
-    d = 1
-    while d < n:
-        x = x + lax.ppermute(x, axis, [(j, j ^ d) for j in range(n)])
-        d *= 2
+def group_sum(x, axis, n, groups):
+    for stride, size in levels_of(n, groups):
+        x = x + sum(level_gather(x, axis, n, stride, size))
     return x
 
 
@@ -46,7 +67,6 @@
     modes, columns = residues.shape
     peers = lax.axis_size("ctx")
     lanes = lax.axis_size("chan")
-    assert peers & (peers - 1) == 0 and lanes & (lanes - 1) == 0
     query = query_gate.astype(jnp.float32)
     keyed = key_gate.astype(jnp.float32)
     values = value_input.astype(jnp.float32)
@@ -64,8 +84,7 @@
 
     ends = jnp.sum(jnp.exp(-rate * (steps - 1.0 - where)) * source[:, None, :], axis=0)
     heads = mixing * jnp.sum(falling * drive[:, None, :], axis=0)
-    incoming = exclusive_scan(ends, decay_rate, steps, "ctx", peers, from_lower)
-    upper = exclusive_scan(heads, decay_rate, steps, "ctx", peers, from_upper)
+    incoming, upper = carried_scan(ends, heads, decay_rate, steps, "ctx", peers, CTX_GROUPS)
 
     row = jnp.arange(steps)[:, None]
     col = jnp.arange(steps)[None, :]
@@ -85,14 +104,14 @@
     grad_w = jnp.sum(drive[:, None, :] * states, axis=0)
     grad_a = jnp.sum(adjoint * previous, axis=0)
 
-    sums = butterfly_sum(jnp.stack([grad_w, grad_a]), "ctx", peers)
+    sums = group_sum(jnp.stack([grad_w, grad_a]), "ctx", peers, CTX_GROUPS)
     grad_mixing, grad_decay = sums[0], sums[1]
     raw_residue = grad_mixing * norm_factor
     raw_lograte = decay_rate * (
         grad_mixing * residues * decay * decay / norm_factor - decay * grad_decay
     )
     part = jnp.sum(raw_residue * raw_residue) + jnp.sum(raw_lograte * raw_lograte)
-    total = butterfly_sum(part.reshape(1), "chan", lanes)[0]
+    total = group_sum(part.reshape(1), "chan", lanes, CHAN_GROUPS)[0]
     limit = math.sqrt(2.0 * MODES * WIDTH)
     scale = jnp.minimum(1.0, limit / jnp.sqrt(total + 1e-06))
     width = columns // peers

time: 231 us -> 184 us (0.80)
  the two profiles are of different devices: /device:TPU:116 before, /device:TPU:48 now
where the time goes in v2:
time: 184 us; the launch traced here: 183 us
  starting transfers between devices  131 us (71%)
  waiting for transfers between devices  23.2 us (13%)
  other arithmetic  9.78 us (5%)
  matrix products  9.21 us (5%)
  between operations  7.96 us (4%)
    ppermute x30, starting transfers between devices, level_gather(): got.append(lax.ppermute(x, axis, perm))  131 us
    ppermute x30, waiting for transfers between devices, level_gather(): got.append(lax.ppermute(x, axis, perm))  23.2 us
    dot_general x1, matrix products, local(): jnp.dot(upper_tri, fallen, precision=HIGHEST).reshape(rising.shape)  4.61 us
    dot_general x1, matrix products, local(): jnp.dot(lower_tri, climbed, precision=HIGHEST).reshape(rising.shape)  4.59 us
  transfers between devices with their start and end apart: 30, of which 10 were waited for; matrix products, arithmetic and copies ran while one was open for 3% of the time, Pallas kernels for 0%

profile of v2, /device:TPU:48, one launch (start us, length us, event | category | flops | bytes accessed | tf_op | source)
XLA Modules:
  0.0 182.7 jit_solution(12297560771521896153)
XLA Ops:
  7.4 4.8 %collective-permute-start.1 = (f32[2,16,512]{2,1,0:T(8,128)S(1)}, f32[2,16,512]{2,1,0:T(8,128)S(1)}, u32[]{:S(2)}, u32[]{:S(2)}) collective-permute-start(f32[2,16,512]{2,1,0:T(8,128)S(1)} %pad_maximum_fusion.1), channel_id=1, source_target_pairs={{0,32},{16,48},{32,64},{48,80},{64,96},{80,112},{96,128},{112,144}... | collective-permute-start | bytes 196616 | tf_op jit(solution)/shard_map/ppermute | solution.py:32
  16.9 13.2 %collective-permute-start.3 = (f32[2,16,512]{2,1,0:T(8,128)S(1)}, f32[2,16,512]{2,1,0:T(8,128)S(1)}, u32[]{:S(2)}, u32[]{:S(2)}) collective-permute-start(f32[2,16,512]{2,1,0:T(8,128)S(1)} %pad_maximum_fusion.1), channel_id=1, source_target_pairs={{0,96},{16,112},{32,128},{48,144},{64,160},{80,176},{96,192},{112,... | collective-permute-start | bytes 196616 | tf_op jit(solution)/shard_map/ppermute | solution.py:32
  32.1 5.7 %collective-permute-start.5 = (f32[2,16,512]{2,1,0:T(8,128)S(1)}, f32[2,16,512]{2,1,0:T(8,128)S(1)}, u32[]{:S(2)}, u32[]{:S(2)}) collective-permute-start(f32[2,16,512]{2,1,0:T(8,128)S(1)} %pad_maximum_fusion.1), channel_id=1, source_target_pairs={{0,160},{16,176},{32,192},{48,208},{64,224},{80,240},{96,0},{112,1... | collective-permute-start | bytes 196616 | tf_op jit(solution)/shard_map/ppermute | solution.py:32
  37.8 6.0 %collective-permute-start.6 = (f32[2,16,512]{2,1,0:T(8,128)S(1)}, f32[2,16,512]{2,1,0:T(8,128)S(1)}, u32[]{:S(2)}, u32[]{:S(2)}) collective-permute-start(f32[2,16,512]{2,1,0:T(8,128)S(1)} %pad_maximum_fusion.1), channel_id=1, source_target_pairs={{0,192},{16,208},{32,224},{48,240},{64,0},{80,16},{96,32},{112,48}... | collective-permute-start | bytes 196616 | tf_op jit(solution)/shard_map/ppermute | solution.py:32
  47.5 3.8 %collective-permute-done.7 = f32[2,16,512]{2,1,0:T(8,128)S(1)} collective-permute-done((f32[2,16,512]{2,1,0:T(8,128)S(1)}, f32[2,16,512]{2,1,0:T(8,128)S(1)}, u32[]{:S(2)}, u32[]{:S(2)}) %collective-permute-start.7) | collective-permute-done | bytes 65568 | tf_op jit(solution)/shard_map/ppermute | solution.py:32
  53.3 4.8 %collective-permute-start.8 = (f32[2,16,512]{2,1,0:T(8,128)S(1)}, f32[2,16,512]{2,1,0:T(8,128)S(1)}, u32[]{:S(2)}, u32[]{:S(2)}) collective-permute-start(f32[2,16,512]{2,1,0:T(8,128)S(1)} %pad_maximum_fusion.2), channel_id=1, source_target_pairs={{0,256},{16,272},{32,288},{48,304},{64,320},{80,336},{96,352},{112... | collective-permute-start | bytes 196616 | tf_op jit(solution)/shard_map/ppermute | solution.py:32
  62.7 5.6 %collective-permute-done.9 = f32[2,16,512]{2,1,0:T(8,128)S(1)} collective-permute-done((f32[2,16,512]{2,1,0:T(8,128)S(1)}, f32[2,16,512]{2,1,0:T(8,128)S(1)}, u32[]{:S(2)}, u32[]{:S(2)}) %collective-permute-start.9) | collective-permute-done | bytes 65568 | tf_op jit(solution)/shard_map/ppermute | solution.py:32
  68.4 4.6 %multiply_reduce_fusion = (f32[16,512]{1,0:T(8,128)S(1)}, f32[128,512]{1,0:T(8,128)S(1)}, f32[128,16,512]{2,0,1:T(8,128)S(1)}) fusion(f32[128,512]{1,0:T(8,128)S(1)} %get-tuple-element.40, f32[16,512]{1,0:T(8,128)S(1)} %get-tuple-element.29, f32[16,512]{1,0:T(8,128)S(1)} %fusion.27, f32[128]{0:T(128)S(1)} %iota_add_fusion, ...), kind=kOutput, calls=%fused_computation.5 | convolution fusion | flops 1619992576 | bytes 9044480 | tf_op jit(solution)/shard_map/dot_general | solution.py:96
  73.1 4.6 %fusion = (f32[16,512]{1,0:T(8,128)S(1)}, f32[128,512]{1,0:T(8,128)S(1)}) fusion(f32[127,16,512]{2,0,1:T(8,128)S(1)} %bitcast.232, f32[1,16,512]{2,0,1:T(1,128)S(1)} %broadcast_in_dim.40, f32[16,512]{1,0:T(8,128)S(1)} %fusion.18, f32[128]{0:T(128)S(1)} %iota_subtract_fusion, f32[16,512]{1,0:T(8,128)S(1)} %copy-done, f32[16,512]{1,0:T(8,128)S(1)} %neg.6, ...), kind=kOutput, calls=%fused_computation.1 | convolution fusion | flops 1619992576 | bytes 8782336 | tf_op jit(solution)/shard_map/dot_general | solution.py:97
  85.7 4.7 %collective-permute-start.14 = (f32[2,16,512]{2,1,0:T(8,128)S(1)}, f32[2,16,512]{2,1,0:T(8,128)S(1)}, u32[]{:S(2)}, u32[]{:S(2)}) collective-permute-start(f32[2,16,512]{2,1,0:T(8,128)S(1)} %fusion.37), channel_id=1, source_target_pairs={{0,96},{16,112},{32,128},{48,144},{64,160},{80,176},{96,192},{112,... | collective-permute-start | bytes 196616 | tf_op jit(solution)/shard_map/ppermute | solution.py:32
  90.4 4.7 %collective-permute-start.15 = (f32[2,16,512]{2,1,0:T(8,128)S(1)}, f32[2,16,512]{2,1,0:T(8,128)S(1)}, u32[]{:S(2)}, u32[]{:S(2)}) collective-permute-start(f32[2,16,512]{2,1,0:T(8,128)S(1)} %fusion.37), channel_id=1, source_target_pairs={{0,128},{16,144},{32,160},{48,176},{64,192},{80,208},{96,224},{112... | collective-permute-start | bytes 196616 | tf_op jit(solution)/shard_map/ppermute | solution.py:32
  95.1 3.7 %collective-permute-start.16 = (f32[2,16,512]{2,1,0:T(8,128)S(1)}, f32[2,16,512]{2,1,0:T(8,128)S(1)}, u32[]{:S(2)}, u32[]{:S(2)}) collective-permute-start(f32[2,16,512]{2,1,0:T(8,128)S(1)} %fusion.37), channel_id=1, source_target_pairs={{0,160},{16,176},{32,192},{48,208},{64,224},{80,240},{96,0},{112,1... | collective-permute-start | bytes 196616 | tf_op jit(solution)/shard_map/ppermute | solution.py:32
  98.8 4.5 %collective-permute-start.17 = (f32[2,16,512]{2,1,0:T(8,128)S(1)}, f32[2,16,512]{2,1,0:T(8,128)S(1)}, u32[]{:S(2)}, u32[]{:S(2)}) collective-permute-start(f32[2,16,512]{2,1,0:T(8,128)S(1)} %fusion.37), channel_id=1, source_target_pairs={{0,192},{16,208},{32,224},{48,240},{64,0},{80,16},{96,32},{112,48}... | collective-permute-start | bytes 196616 | tf_op jit(solution)/shard_map/ppermute | solution.py:32
  103.3 2.9 %collective-permute-start.18 = (f32[2,16,512]{2,1,0:T(8,128)S(1)}, f32[2,16,512]{2,1,0:T(8,128)S(1)}, u32[]{:S(2)}, u32[]{:S(2)}) collective-permute-start(f32[2,16,512]{2,1,0:T(8,128)S(1)} %fusion.37), channel_id=1, source_target_pairs={{0,224},{16,240},{32,0},{48,16},{64,32},{80,48},{96,64},{112,80},{... | collective-permute-start | bytes 196616 | tf_op jit(solution)/shard_map/ppermute | solution.py:32
  107.1 3.6 %collective-permute-done.18 = f32[2,16,512]{2,1,0:T(8,128)S(1)} collective-permute-done((f32[2,16,512]{2,1,0:T(8,128)S(1)}, f32[2,16,512]{2,1,0:T(8,128)S(1)}, u32[]{:S(2)}, u32[]{:S(2)}) %collective-permute-start.18) | collective-permute-done | bytes 65568 | tf_op jit(solution)/shard_map/ppermute | solution.py:32
  112.7 5.2 %collective-permute-start.20 = (f32[2,16,512]{2,1,0:T(8,128)S(1)}, f32[2,16,512]{2,1,0:T(8,128)S(1)}, u32[]{:S(2)}, u32[]{:S(2)}) collective-permute-start(f32[2,16,512]{2,1,0:T(8,128)S(1)} %add_add_fusion.1), channel_id=1, source_target_pairs={{0,512},{16,528},{32,544},{48,560},{64,576},{80,592},{96,608},{112... | collective-permute-start | bytes 196616 | tf_op jit(solution)/shard_map/ppermute | solution.py:32
  127.2 3.2 %collective-permute-start.22 = (f32[1]{0:T(128)}, f32[1]{0:T(128)}, u32[]{:S(2)}, u32[]{:S(2)}) collective-permute-start(f32[1]{0:T(128)} %bitcast.40), channel_id=1, source_target_pairs={{0,1},{1,2},{2,3},{3,4},{4,5},{5,6},{6,7},{7,0},{8,9},{9,10},{10,1... | collective-permute-start | bytes 20 | tf_op jit(solution)/shard_map/ppermute | solution.py:32
  130.4 8.7 %collective-permute-start.23 = (f32[1]{0:T(128)}, f32[1]{0:T(128)}, u32[]{:S(2)}, u32[]{:S(2)}) collective-permute-start(f32[1]{0:T(128)} %bitcast.40), channel_id=1, source_target_pairs={{0,2},{1,3},{2,4},{3,5},{4,6},{5,7},{6,0},{7,1},{8,10},{9,11},{10,... | collective-permute-start | bytes 20 | tf_op jit(solution)/shard_map/ppermute | solution.py:32
  139.1 11.3 %collective-permute-start.24 = (f32[1]{0:T(128)}, f32[1]{0:T(128)}, u32[]{:S(2)}, u32[]{:S(2)}) collective-permute-start(f32[1]{0:T(128)} %bitcast.40), channel_id=1, source_target_pairs={{0,3},{1,4},{2,5},{3,6},{4,7},{5,0},{6,1},{7,2},{8,11},{9,12},{10,... | collective-permute-start | bytes 20 | tf_op jit(solution)/shard_map/ppermute | solution.py:32
  150.4 5.0 %collective-permute-start.25 = (f32[1]{0:T(128)}, f32[1]{0:T(128)}, u32[]{:S(2)}, u32[]{:S(2)}) collective-permute-start(f32[1]{0:T(128)} %bitcast.40), channel_id=1, source_target_pairs={{0,4},{1,5},{2,6},{3,7},{4,0},{5,1},{6,2},{7,3},{8,12},{9,13},{10,... | collective-permute-start | bytes 20 | tf_op jit(solution)/shard_map/ppermute | solution.py:32
  155.4 8.2 %collective-permute-start.26 = (f32[1]{0:T(128)}, f32[1]{0:T(128)}, u32[]{:S(2)}, u32[]{:S(2)}) collective-permute-start(f32[1]{0:T(128)} %bitcast.40), channel_id=1, source_target_pairs={{0,5},{1,6},{2,7},{3,0},{4,1},{5,2},{6,3},{7,4},{8,13},{9,14},{10,... | collective-permute-start | bytes 20 | tf_op jit(solution)/shard_map/ppermute | solution.py:32
  163.6 3.2 %collective-permute-start.27 = (f32[1]{0:T(128)}, f32[1]{0:T(128)}, u32[]{:S(2)}, u32[]{:S(2)}) collective-permute-start(f32[1]{0:T(128)} %bitcast.40), channel_id=1, source_target_pairs={{0,6},{1,7},{2,0},{3,1},{4,2},{5,3},{6,4},{7,5},{8,14},{9,15},{10,... | collective-permute-start | bytes 20 | tf_op jit(solution)/shard_map/ppermute | solution.py:32
  166.8 3.7 %collective-permute-start.28 = (f32[1]{0:T(128)}, f32[1]{0:T(128)}, u32[]{:S(2)}, u32[]{:S(2)}) collective-permute-start(f32[1]{0:T(128)} %bitcast.40), channel_id=1, source_target_pairs={{0,7},{1,0},{2,1},{3,2},{4,3},{5,4},{6,5},{7,6},{8,15},{9,8},{10,9... | collective-permute-start | bytes 20 | tf_op jit(solution)/shard_map/ppermute | solution.py:32
  175.0 3.2 %collective-permute-start.29 = (f32[1]{0:T(128)}, f32[1]{0:T(128)}, u32[]{:S(2)}, u32[]{:S(2)}) collective-permute-start(f32[1]{0:T(128)} %add.367), channel_id=1, source_target_pairs={{0,8},{1,9},{2,10},{3,11},{4,12},{5,13},{6,14},{7,15},{8,0},{9,1},... | collective-permute-start | bytes 20 | tf_op jit(solution)/shard_map/ppermute | solution.py:32
  (84 shorter events, 45.8 us)
Async XLA Ops:
  7.4 30.4 %collective-permute-start.1 = (f32[2,16,512]{2,1,0:T(8,128)S(1)}, f32[2,16,512]{2,1,0:T(8,128)S(1)}, u32[]{:S(2)}, u32[]{:S(2)}) collective-permute-start(f32[2,16,512]{2,1,0:T(8,128)S(1)} %pad_maximum_fusion.1), channel_id=1, source_target_pairs={{0,32},{16,48},{32,64},{48,80},{64,96},{80,112},{96,128},{112,144}... | collective-permute-start | bytes 196616 | tf_op jit(solution)/shard_map/ppermute | solution.py:32
  12.2 31.6 %collective-permute-start.2 = (f32[2,16,512]{2,1,0:T(8,128)S(1)}, f32[2,16,512]{2,1,0:T(8,128)S(1)}, u32[]{:S(2)}, u32[]{:S(2)}) collective-permute-start(f32[2,16,512]{2,1,0:T(8,128)S(1)} %pad_maximum_fusion.1), channel_id=1, source_target_pairs={{0,64},{16,80},{32,96},{48,112},{64,128},{80,144},{96,160},{112,17... | collective-permute-start | bytes 196616 | tf_op jit(solution)/shard_map/ppermute | solution.py:32
  16.9 28.9 %collective-permute-start.3 = (f32[2,16,512]{2,1,0:T(8,128)S(1)}, f32[2,16,512]{2,1,0:T(8,128)S(1)}, u32[]{:S(2)}, u32[]{:S(2)}) collective-permute-start(f32[2,16,512]{2,1,0:T(8,128)S(1)} %pad_maximum_fusion.1), channel_id=1, source_target_pairs={{0,96},{16,112},{32,128},{48,144},{64,160},{80,176},{96,192},{112,... | collective-permute-start | bytes 196616 | tf_op jit(solution)/shard_map/ppermute | solution.py:32
  30.2 15.7 %collective-permute-start.4 = (f32[2,16,512]{2,1,0:T(8,128)S(1)}, f32[2,16,512]{2,1,0:T(8,128)S(1)}, u32[]{:S(2)}, u32[]{:S(2)}) collective-permute-start(f32[2,16,512]{2,1,0:T(8,128)S(1)} %pad_maximum_fusion.1), channel_id=1, source_target_pairs={{0,128},{16,144},{32,160},{48,176},{64,192},{80,208},{96,224},{112... | collective-permute-start | bytes 196616 | tf_op jit(solution)/shard_map/ppermute | solution.py:32
  32.1 14.6 %collective-permute-start.5 = (f32[2,16,512]{2,1,0:T(8,128)S(1)}, f32[2,16,512]{2,1,0:T(8,128)S(1)}, u32[]{:S(2)}, u32[]{:S(2)}) collective-permute-start(f32[2,16,512]{2,1,0:T(8,128)S(1)} %pad_maximum_fusion.1), channel_id=1, source_target_pairs={{0,160},{16,176},{32,192},{48,208},{64,224},{80,240},{96,0},{112,1... | collective-permute-start | bytes 196616 | tf_op jit(solution)/shard_map/ppermute | solution.py:32
  37.8 9.7 %collective-permute-start.6 = (f32[2,16,512]{2,1,0:T(8,128)S(1)}, f32[2,16,512]{2,1,0:T(8,128)S(1)}, u32[]{:S(2)}, u32[]{:S(2)}) collective-permute-start(f32[2,16,512]{2,1,0:T(8,128)S(1)} %pad_maximum_fusion.1), channel_id=1, source_target_pairs={{0,192},{16,208},{32,224},{48,240},{64,0},{80,16},{96,32},{112,48}... | collective-permute-start | bytes 196616 | tf_op jit(solution)/shard_map/ppermute | solution.py:32
  51.4 11.2 %collective-permute-start.10 = (f32[2,16,512]{2,1,0:T(8,128)S(1)}, f32[2,16,512]{2,1,0:T(8,128)S(1)}, u32[]{:S(2)}, u32[]{:S(2)}) collective-permute-start(f32[2,16,512]{2,1,0:T(8,128)S(1)} %pad_maximum_fusion.2), channel_id=1, source_target_pairs={{0,768},{16,784},{32,800},{48,816},{64,832},{80,848},{96,864},{112... | collective-permute-start | bytes 196616 | tf_op jit(solution)/shard_map/ppermute | solution.py:32
  53.3 9.3 %collective-permute-start.8 = (f32[2,16,512]{2,1,0:T(8,128)S(1)}, f32[2,16,512]{2,1,0:T(8,128)S(1)}, u32[]{:S(2)}, u32[]{:S(2)}) collective-permute-start(f32[2,16,512]{2,1,0:T(8,128)S(1)} %pad_maximum_fusion.2), channel_id=1, source_target_pairs={{0,256},{16,272},{32,288},{48,304},{64,320},{80,336},{96,352},{112... | collective-permute-start | bytes 196616 | tf_op jit(solution)/shard_map/ppermute | solution.py:32
  58.2 10.1 %collective-permute-start.9 = (f32[2,16,512]{2,1,0:T(8,128)S(1)}, f32[2,16,512]{2,1,0:T(8,128)S(1)}, u32[]{:S(2)}, u32[]{:S(2)}) collective-permute-start(f32[2,16,512]{2,1,0:T(8,128)S(1)} %pad_maximum_fusion.2), channel_id=1, source_target_pairs={{0,512},{16,528},{32,544},{48,560},{64,576},{80,592},{96,608},{112... | collective-permute-start | bytes 196616 | tf_op jit(solution)/shard_map/ppermute | solution.py:32
  80.9 17.9 %collective-permute-start.12 = (f32[2,16,512]{2,1,0:T(8,128)S(1)}, f32[2,16,512]{2,1,0:T(8,128)S(1)}, u32[]{:S(2)}, u32[]{:S(2)}) collective-permute-start(f32[2,16,512]{2,1,0:T(8,128)S(1)} %fusion.37), channel_id=1, source_target_pairs={{0,32},{16,48},{32,64},{48,80},{64,96},{80,112},{96,128},{112,144}... | collective-permute-start | bytes 196616 | tf_op jit(solution)/shard_map/ppermute | solution.py:32
  82.9 20.4 %collective-permute-start.13 = (f32[2,16,512]{2,1,0:T(8,128)S(1)}, f32[2,16,512]{2,1,0:T(8,128)S(1)}, u32[]{:S(2)}, u32[]{:S(2)}) collective-permute-start(f32[2,16,512]{2,1,0:T(8,128)S(1)} %fusion.37), channel_id=1, source_target_pairs={{0,64},{16,80},{32,96},{48,112},{64,128},{80,144},{96,160},{112,17... | collective-permute-start | bytes 196616 | tf_op jit(solution)/shard_map/ppermute | solution.py:32
  85.7 21.4 %collective-permute-start.14 = (f32[2,16,512]{2,1,0:T(8,128)S(1)}, f32[2,16,512]{2,1,0:T(8,128)S(1)}, u32[]{:S(2)}, u32[]{:S(2)}) collective-permute-start(f32[2,16,512]{2,1,0:T(8,128)S(1)} %fusion.37), channel_id=1, source_target_pairs={{0,96},{16,112},{32,128},{48,144},{64,160},{80,176},{96,192},{112,... | collective-permute-start | bytes 196616 | tf_op jit(solution)/shard_map/ppermute | solution.py:32
  90.4 16.6 %collective-permute-start.15 = (f32[2,16,512]{2,1,0:T(8,128)S(1)}, f32[2,16,512]{2,1,0:T(8,128)S(1)}, u32[]{:S(2)}, u32[]{:S(2)}) collective-permute-start(f32[2,16,512]{2,1,0:T(8,128)S(1)} %fusion.37), channel_id=1, source_target_pairs={{0,128},{16,144},{32,160},{48,176},{64,192},{80,208},{96,224},{112... | collective-permute-start | bytes 196616 | tf_op jit(solution)/shard_map/ppermute | solution.py:32
  95.1 12.0 %collective-permute-start.16 = (f32[2,16,512]{2,1,0:T(8,128)S(1)}, f32[2,16,512]{2,1,0:T(8,128)S(1)}, u32[]{:S(2)}, u32[]{:S(2)}) collective-permute-start(f32[2,16,512]{2,1,0:T(8,128)S(1)} %fusion.37), channel_id=1, source_target_pairs={{0,160},{16,176},{32,192},{48,208},{64,224},{80,240},{96,0},{112,1... | collective-permute-start | bytes 196616 | tf_op jit(solution)/shard_map/ppermute | solution.py:32
  98.8 8.3 %collective-permute-start.17 = (f32[2,16,512]{2,1,0:T(8,128)S(1)}, f32[2,16,512]{2,1,0:T(8,128)S(1)}, u32[]{:S(2)}, u32[]{:S(2)}) collective-permute-start(f32[2,16,512]{2,1,0:T(8,128)S(1)} %fusion.37), channel_id=1, source_target_pairs={{0,192},{16,208},{32,224},{48,240},{64,0},{80,16},{96,32},{112,48}... | collective-permute-start | bytes 196616 | tf_op jit(solution)/shard_map/ppermute | solution.py:32
  110.7 10.7 %collective-permute-start.19 = (f32[2,16,512]{2,1,0:T(8,128)S(1)}, f32[2,16,512]{2,1,0:T(8,128)S(1)}, u32[]{:S(2)}, u32[]{:S(2)}) collective-permute-start(f32[2,16,512]{2,1,0:T(8,128)S(1)} %add_add_fusion.1), channel_id=1, source_target_pairs={{0,256},{16,272},{32,288},{48,304},{64,320},{80,336},{96,352},{112... | collective-permute-start | bytes 196616 | tf_op jit(solution)/shard_map/ppermute | solution.py:32
  112.7 10.1 %collective-permute-start.20 = (f32[2,16,512]{2,1,0:T(8,128)S(1)}, f32[2,16,512]{2,1,0:T(8,128)S(1)}, u32[]{:S(2)}, u32[]{:S(2)}) collective-permute-start(f32[2,16,512]{2,1,0:T(8,128)S(1)} %add_add_fusion.1), channel_id=1, source_target_pairs={{0,512},{16,528},{32,544},{48,560},{64,576},{80,592},{96,608},{112... | collective-permute-start | bytes 196616 | tf_op jit(solution)/shard_map/ppermute | solution.py:32
  127.2 36.4 %collective-permute-start.22 = (f32[1]{0:T(128)}, f32[1]{0:T(128)}, u32[]{:S(2)}, u32[]{:S(2)}) collective-permute-start(f32[1]{0:T(128)} %bitcast.40), channel_id=1, source_target_pairs={{0,1},{1,2},{2,3},{3,4},{4,5},{5,6},{6,7},{7,0},{8,9},{9,10},{10,1... | collective-permute-start | bytes 20 | tf_op jit(solution)/shard_map/ppermute | solution.py:32
  130.4 36.4 %collective-permute-start.23 = (f32[1]{0:T(128)}, f32[1]{0:T(128)}, u32[]{:S(2)}, u32[]{:S(2)}) collective-permute-start(f32[1]{0:T(128)} %bitcast.40), channel_id=1, source_target_pairs={{0,2},{1,3},{2,4},{3,5},{4,6},{5,7},{6,0},{7,1},{8,10},{9,11},{10,... | collective-permute-start | bytes 20 | tf_op jit(solution)/shard_map/ppermute | solution.py:32
  139.1 32.7 %collective-permute-start.24 = (f32[1]{0:T(128)}, f32[1]{0:T(128)}, u32[]{:S(2)}, u32[]{:S(2)}) collective-permute-start(f32[1]{0:T(128)} %bitcast.40), channel_id=1, source_target_pairs={{0,3},{1,4},{2,5},{3,6},{4,7},{5,0},{6,1},{7,2},{8,11},{9,12},{10,... | collective-permute-start | bytes 20 | tf_op jit(solution)/shard_map/ppermute | solution.py:32
  150.4 22.0 %collective-permute-start.25 = (f32[1]{0:T(128)}, f32[1]{0:T(128)}, u32[]{:S(2)}, u32[]{:S(2)}) collective-permute-start(f32[1]{0:T(128)} %bitcast.40), channel_id=1, source_target_pairs={{0,4},{1,5},{2,6},{3,7},{4,0},{5,1},{6,2},{7,3},{8,12},{9,13},{10,... | collective-permute-start | bytes 20 | tf_op jit(solution)/shard_map/ppermute | solution.py:32
  155.4 17.7 %collective-permute-start.26 = (f32[1]{0:T(128)}, f32[1]{0:T(128)}, u32[]{:S(2)}, u32[]{:S(2)}) collective-permute-start(f32[1]{0:T(128)} %bitcast.40), channel_id=1, source_target_pairs={{0,5},{1,6},{2,7},{3,0},{4,1},{5,2},{6,3},{7,4},{8,13},{9,14},{10,... | collective-permute-start | bytes 20 | tf_op jit(solution)/shard_map/ppermute | solution.py:32
  163.6 10.2 %collective-permute-start.27 = (f32[1]{0:T(128)}, f32[1]{0:T(128)}, u32[]{:S(2)}, u32[]{:S(2)}) collective-permute-start(f32[1]{0:T(128)} %bitcast.40), channel_id=1, source_target_pairs={{0,6},{1,7},{2,0},{3,1},{4,2},{5,3},{6,4},{7,5},{8,14},{9,15},{10,... | collective-permute-start | bytes 20 | tf_op jit(solution)/shard_map/ppermute | solution.py:32
  166.8 7.5 %collective-permute-start.28 = (f32[1]{0:T(128)}, f32[1]{0:T(128)}, u32[]{:S(2)}, u32[]{:S(2)}) collective-permute-start(f32[1]{0:T(128)} %bitcast.40), channel_id=1, source_target_pairs={{0,7},{1,0},{2,1},{3,2},{4,3},{5,4},{6,5},{7,6},{8,15},{9,8},{10,9... | collective-permute-start | bytes 20 | tf_op jit(solution)/shard_map/ppermute | solution.py:32
  (12 other events, 202.5 us)

commit v3 on v2

--- a/solution.py
+++ b/solution.py
@@ -10,7 +10,7 @@
 
 HIGHEST = lax.Precision.HIGHEST
 CTX_GROUPS = (2, 8, 4)
-CHAN_GROUPS = (8, 2)
+CHAN_GROUPS = (2, 2, 2, 2)
 
 
 def levels_of(n, groups):
@@ -96,13 +96,22 @@
     states0 = falling * jnp.dot(lower_tri, climbed, precision=HIGHEST).reshape(rising.shape)
     adjoint0 = rising * jnp.dot(upper_tri, fallen, precision=HIGHEST).reshape(rising.shape)
 
-    states = states0 + jnp.exp(-rate * (where + 1.0)) * incoming[None]
-    adjoint = adjoint0 + jnp.exp(-rate * (steps - where)) * upper[None]
-    previous = jnp.concatenate([incoming[None], states[:-1]], axis=0)
+    grown = jnp.exp(-rate * (where + 1.0))
+    shrunk = jnp.exp(-rate * (steps - where))
+    previous0 = jnp.concatenate([jnp.zeros_like(states0[:1]), states0[:-1]], axis=0)
+    w_free = jnp.sum(drive[:, None, :] * states0, axis=0)
+    w_in = jnp.sum(drive[:, None, :] * grown, axis=0)
+    a_free = jnp.sum(adjoint0 * previous0, axis=0)
+    a_in = jnp.sum(adjoint0 * falling, axis=0)
+    a_up = jnp.sum(shrunk * previous0, axis=0)
+    a_both = steps * jnp.exp(-decay_rate * steps)
+    grad_w = w_free + incoming * w_in
+    grad_a = a_free + incoming * a_in + upper * a_up + incoming * upper * a_both
+
+    states = states0 + grown * incoming[None]
+    adjoint = adjoint0 + shrunk * upper[None]
     mixed = jnp.sum(mixing[None] * states, axis=1)
     grad_source = jnp.sum(adjoint, axis=1)
-    grad_w = jnp.sum(drive[:, None, :] * states, axis=0)
-    grad_a = jnp.sum(adjoint * previous, axis=0)
 
     sums = group_sum(jnp.stack([grad_w, grad_a]), "ctx", peers, CTX_GROUPS)
     grad_mixing, grad_decay = sums[0], sums[1]

time: 184 us -> 166 us (0.902)
  the two profiles are of different devices: /device:TPU:48 before, /device:TPU:2 now
where the time goes in v3:
time: 166 us; the launch traced here: 165 us
  starting transfers between devices  112 us (67%)
  waiting for transfers between devices  23.5 us (14%)
  matrix products  12.6 us (8%)
  other arithmetic  9.81 us (6%)
  between operations  5.18 us (3%)
    ppermute x26, starting transfers between devices, level_gather(): got.append(lax.ppermute(x, axis, perm))  112 us
    ppermute x26, waiting for transfers between devices, level_gather(): got.append(lax.ppermute(x, axis, perm))  23.5 us
    dot_general x1, matrix products, local(): jnp.dot(upper_tri, fallen, precision=HIGHEST).reshape(rising.shape)  7.52 us
    dot_general x1, matrix products, local(): jnp.dot(lower_tri, climbed, precision=HIGHEST).reshape(rising.shape)  5.05 us
  transfers between devices with their start and end apart: 26, of which 12 were waited for; matrix products, arithmetic and copies ran while one was open for 6% of the time, Pallas kernels for 0%

profile of v3, /device:TPU:2, one launch (start us, length us, event | category | flops | bytes accessed | tf_op | source)
XLA Modules:
  0.0 165.0 jit_solution(8854430642413283485)
XLA Ops:
  7.4 6.2 %collective-permute-start.7 = (f32[2,16,512]{2,1,0:T(8,128)S(1)}, f32[2,16,512]{2,1,0:T(8,128)S(1)}, u32[]{:S(2)}, u32[]{:S(2)}) collective-permute-start(f32[2,16,512]{2,1,0:T(8,128)S(1)} %pad_maximum_fusion.1), channel_id=1, source_target_pairs={{0,224},{16,240},{32,0},{48,16},{64,32},{80,48},{96,64},{112,80},{... | collective-permute-start | bytes 196616 | tf_op jit(solution)/shard_map/ppermute | solution.py:32
  13.6 3.8 %collective-permute-start.6 = (f32[2,16,512]{2,1,0:T(8,128)S(1)}, f32[2,16,512]{2,1,0:T(8,128)S(1)}, u32[]{:S(2)}, u32[]{:S(2)}) collective-permute-start(f32[2,16,512]{2,1,0:T(8,128)S(1)} %pad_maximum_fusion.1), channel_id=1, source_target_pairs={{0,192},{16,208},{32,224},{48,240},{64,0},{80,16},{96,32},{112,48}... | collective-permute-start | bytes 196616 | tf_op jit(solution)/shard_map/ppermute | solution.py:32
  18.7 2.7 %collective-permute-start.5 = (f32[2,16,512]{2,1,0:T(8,128)S(1)}, f32[2,16,512]{2,1,0:T(8,128)S(1)}, u32[]{:S(2)}, u32[]{:S(2)}) collective-permute-start(f32[2,16,512]{2,1,0:T(8,128)S(1)} %pad_maximum_fusion.1), channel_id=1, source_target_pairs={{0,160},{16,176},{32,192},{48,208},{64,224},{80,240},{96,0},{112,1... | collective-permute-start | bytes 196616 | tf_op jit(solution)/shard_map/ppermute | solution.py:32
  21.4 6.4 %collective-permute-start.4 = (f32[2,16,512]{2,1,0:T(8,128)S(1)}, f32[2,16,512]{2,1,0:T(8,128)S(1)}, u32[]{:S(2)}, u32[]{:S(2)}) collective-permute-start(f32[2,16,512]{2,1,0:T(8,128)S(1)} %pad_maximum_fusion.1), channel_id=1, source_target_pairs={{0,128},{16,144},{32,160},{48,176},{64,192},{80,208},{96,224},{112... | collective-permute-start | bytes 196616 | tf_op jit(solution)/shard_map/ppermute | solution.py:32
  29.8 5.0 %collective-permute-start.2 = (f32[2,16,512]{2,1,0:T(8,128)S(1)}, f32[2,16,512]{2,1,0:T(8,128)S(1)}, u32[]{:S(2)}, u32[]{:S(2)}) collective-permute-start(f32[2,16,512]{2,1,0:T(8,128)S(1)} %pad_maximum_fusion.1), channel_id=1, source_target_pairs={{0,64},{16,80},{32,96},{48,112},{64,128},{80,144},{96,160},{112,17... | collective-permute-start | bytes 196616 | tf_op jit(solution)/shard_map/ppermute | solution.py:32
  34.8 3.6 %collective-permute-start.1 = (f32[2,16,512]{2,1,0:T(8,128)S(1)}, f32[2,16,512]{2,1,0:T(8,128)S(1)}, u32[]{:S(2)}, u32[]{:S(2)}) collective-permute-start(f32[2,16,512]{2,1,0:T(8,128)S(1)} %pad_maximum_fusion.1), channel_id=1, source_target_pairs={{0,32},{16,48},{32,64},{48,80},{64,96},{80,112},{96,128},{112,144}... | collective-permute-start | bytes 196616 | tf_op jit(solution)/shard_map/ppermute | solution.py:32
  38.4 5.0 %fusion.1 = f32[128,16,512]{2,0,1:T(8,128)} fusion(f32[16,512,128]{2,1,0:T(8,128)S(1)} %bitcast.217, f32[16,512]{1,0:T(8,128)S(1)} %neg.6), kind=kOutput, calls=%fused_computation.16 | convolution fusion | flops 1612726272 | bytes 8421376 | tf_op jit(solution)/shard_map/dot_general | solution.py:96
  44.0 5.0 %collective-permute-start.10 = (f32[2,16,512]{2,1,0:T(8,128)S(1)}, f32[2,16,512]{2,1,0:T(8,128)S(1)}, u32[]{:S(2)}, u32[]{:S(2)}) collective-permute-start(f32[2,16,512]{2,1,0:T(8,128)S(1)} %pad_maximum_fusion.2), channel_id=1, source_target_pairs={{0,768},{16,784},{32,800},{48,816},{64,832},{80,848},{96,864},{112... | collective-permute-start | bytes 196616 | tf_op jit(solution)/shard_map/ppermute | solution.py:32
  49.0 5.1 %collective-permute-start.9 = (f32[2,16,512]{2,1,0:T(8,128)S(1)}, f32[2,16,512]{2,1,0:T(8,128)S(1)}, u32[]{:S(2)}, u32[]{:S(2)}) collective-permute-start(f32[2,16,512]{2,1,0:T(8,128)S(1)} %pad_maximum_fusion.2), channel_id=1, source_target_pairs={{0,512},{16,528},{32,544},{48,560},{64,576},{80,592},{96,608},{112... | collective-permute-start | bytes 196616 | tf_op jit(solution)/shard_map/ppermute | solution.py:32
  54.0 3.6 %collective-permute-start.8 = (f32[2,16,512]{2,1,0:T(8,128)S(1)}, f32[2,16,512]{2,1,0:T(8,128)S(1)}, u32[]{:S(2)}, u32[]{:S(2)}) collective-permute-start(f32[2,16,512]{2,1,0:T(8,128)S(1)} %pad_maximum_fusion.2), channel_id=1, source_target_pairs={{0,256},{16,272},{32,288},{48,304},{64,320},{80,336},{96,352},{112... | collective-permute-start | bytes 196616 | tf_op jit(solution)/shard_map/ppermute | solution.py:32
  60.0 5.9 %collective-permute-done.8 = f32[2,16,512]{2,1,0:T(8,128)S(1)} collective-permute-done((f32[2,16,512]{2,1,0:T(8,128)S(1)}, f32[2,16,512]{2,1,0:T(8,128)S(1)}, u32[]{:S(2)}, u32[]{:S(2)}) %collective-permute-start.8) | collective-permute-done | bytes 65568 | tf_op jit(solution)/shard_map/ppermute | solution.py:32
  66.2 7.5 %multiply_reduce_fusion.4 = (f32[16,512]{1,0:T(8,128)S(1)}, f32[128,512]{1,0:T(8,128)S(1)}, f32[16,512]{1,0:T(8,128)S(1)}, f32[16,512]{1,0:T(8,128)S(1)}, f32[16...) fusion(f32[128,16,512]{2,0,1:T(8,128)S(1)} %copy-done, f32[128,512]{1,0:T(8,128)S(1)} %get-tuple-element.43, ...), kind=kOutput, calls=%fused_computation.7 | convolution fusion | flops 1633525760 | bytes 13665280 | tf_op jit(solution)/shard_map/dot_general | solution.py:97
  77.0 2.6 %collective-permute-start.18 = (f32[2,16,512]{2,1,0:T(8,128)S(1)}, f32[2,16,512]{2,1,0:T(8,128)S(1)}, u32[]{:S(2)}, u32[]{:S(2)}) collective-permute-start(f32[2,16,512]{2,1,0:T(8,128)S(1)} %fusion.36), channel_id=1, source_target_pairs={{0,224},{16,240},{32,0},{48,16},{64,32},{80,48},{96,64},{112,80},{... | collective-permute-start | bytes 196616 | tf_op jit(solution)/shard_map/ppermute | solution.py:32
  81.5 6.4 %collective-permute-start.16 = (f32[2,16,512]{2,1,0:T(8,128)S(1)}, f32[2,16,512]{2,1,0:T(8,128)S(1)}, u32[]{:S(2)}, u32[]{:S(2)}) collective-permute-start(f32[2,16,512]{2,1,0:T(8,128)S(1)} %fusion.36), channel_id=1, source_target_pairs={{0,160},{16,176},{32,192},{48,208},{64,224},{80,240},{96,0},{112,1... | collective-permute-start | bytes 196616 | tf_op jit(solution)/shard_map/ppermute | solution.py:32
  87.9 3.4 %collective-permute-start.15 = (f32[2,16,512]{2,1,0:T(8,128)S(1)}, f32[2,16,512]{2,1,0:T(8,128)S(1)}, u32[]{:S(2)}, u32[]{:S(2)}) collective-permute-start(f32[2,16,512]{2,1,0:T(8,128)S(1)} %fusion.36), channel_id=1, source_target_pairs={{0,128},{16,144},{32,160},{48,176},{64,192},{80,208},{96,224},{112... | collective-permute-start | bytes 196616 | tf_op jit(solution)/shard_map/ppermute | solution.py:32
  91.2 3.7 %collective-permute-start.14 = (f32[2,16,512]{2,1,0:T(8,128)S(1)}, f32[2,16,512]{2,1,0:T(8,128)S(1)}, u32[]{:S(2)}, u32[]{:S(2)}) collective-permute-start(f32[2,16,512]{2,1,0:T(8,128)S(1)} %fusion.36), channel_id=1, source_target_pairs={{0,96},{16,112},{32,128},{48,144},{64,160},{80,176},{96,192},{112,... | collective-permute-start | bytes 196616 | tf_op jit(solution)/shard_map/ppermute | solution.py:32
  95.0 5.1 %collective-permute-start.12 = (f32[2,16,512]{2,1,0:T(8,128)S(1)}, f32[2,16,512]{2,1,0:T(8,128)S(1)}, u32[]{:S(2)}, u32[]{:S(2)}) collective-permute-start(f32[2,16,512]{2,1,0:T(8,128)S(1)} %fusion.36), channel_id=1, source_target_pairs={{0,32},{16,48},{32,64},{48,80},{64,96},{80,112},{96,128},{112,144}... | collective-permute-start | bytes 196616 | tf_op jit(solution)/shard_map/ppermute | solution.py:32
  104.4 4.0 %collective-permute-done.13 = f32[2,16,512]{2,1,0:T(8,128)S(1)} collective-permute-done((f32[2,16,512]{2,1,0:T(8,128)S(1)}, f32[2,16,512]{2,1,0:T(8,128)S(1)}, u32[]{:S(2)}, u32[]{:S(2)}) %collective-permute-start.13) | collective-permute-done | bytes 65568 | tf_op jit(solution)/shard_map/ppermute | solution.py:32
  110.4 4.8 %collective-permute-start.19 = (f32[2,16,512]{2,1,0:T(8,128)S(1)}, f32[2,16,512]{2,1,0:T(8,128)S(1)}, u32[]{:S(2)}, u32[]{:S(2)}) collective-permute-start(f32[2,16,512]{2,1,0:T(8,128)S(1)} %add_add_fusion.1), channel_id=1, source_target_pairs={{0,256},{16,272},{32,288},{48,304},{64,320},{80,336},{96,352},{112... | collective-permute-start | bytes 196616 | tf_op jit(solution)/shard_map/ppermute | solution.py:32
  118.7 6.8 %collective-permute-done.20 = f32[2,16,512]{2,1,0:T(8,128)S(1)} collective-permute-done((f32[2,16,512]{2,1,0:T(8,128)S(1)}, f32[2,16,512]{2,1,0:T(8,128)S(1)}, u32[]{:S(2)}, u32[]{:S(2)}) %collective-permute-start.20) | collective-permute-done | bytes 65568 | tf_op jit(solution)/shard_map/ppermute | solution.py:32
  127.4 5.3 %collective-permute-start.22 = (f32[1]{0:T(128)}, f32[1]{0:T(128)}, u32[]{:S(2)}, u32[]{:S(2)}) collective-permute-start(f32[1]{0:T(128)} %bitcast.40), channel_id=1, source_target_pairs={{0,1},{1,0},{2,3},{3,2},{4,5},{5,4},{6,7},{7,6},{8,9},{9,8},{10,11... | collective-permute-start | bytes 20 | tf_op jit(solution)/shard_map/ppermute | solution.py:32
  133.5 9.2 %collective-permute-start.23 = (f32[1]{0:T(128)}, f32[1]{0:T(128)}, u32[]{:S(2)}, u32[]{:S(2)}) collective-permute-start(f32[1]{0:T(128)} %add.367), channel_id=1, source_target_pairs={{0,2},{1,3},{2,0},{3,1},{4,6},{5,7},{6,4},{7,5},{8,10},{9,11},{10,... | collective-permute-start | bytes 20 | tf_op jit(solution)/shard_map/ppermute | solution.py:32
  143.5 13.1 %collective-permute-start.24 = (f32[1]{0:T(128)}, f32[1]{0:T(128)}, u32[]{:S(2)}, u32[]{:S(2)}) collective-permute-start(f32[1]{0:T(128)} %add.368), channel_id=1, source_target_pairs={{0,4},{1,5},{2,6},{3,7},{4,0},{5,1},{6,2},{7,3},{8,12},{9,13},{10,... | collective-permute-start | bytes 20 | tf_op jit(solution)/shard_map/ppermute | solution.py:32
  157.4 3.2 %collective-permute-start.25 = (f32[1]{0:T(128)}, f32[1]{0:T(128)}, u32[]{:S(2)}, u32[]{:S(2)}) collective-permute-start(f32[1]{0:T(128)} %add.369), channel_id=1, source_target_pairs={{0,8},{1,9},{2,10},{3,11},{4,12},{5,13},{6,14},{7,15},{8,0},{9,1},... | collective-permute-start | bytes 20 | tf_op jit(solution)/shard_map/ppermute | solution.py:32
  (77 shorter events, 32.4 us)
Async XLA Ops:
  7.4 22.3 %collective-permute-start.7 = (f32[2,16,512]{2,1,0:T(8,128)S(1)}, f32[2,16,512]{2,1,0:T(8,128)S(1)}, u32[]{:S(2)}, u32[]{:S(2)}) collective-permute-start(f32[2,16,512]{2,1,0:T(8,128)S(1)} %pad_maximum_fusion.1), channel_id=1, source_target_pairs={{0,224},{16,240},{32,0},{48,16},{64,32},{80,48},{96,64},{112,80},{... | collective-permute-start | bytes 196616 | tf_op jit(solution)/shard_map/ppermute | solution.py:32
  13.6 21.2 %collective-permute-start.6 = (f32[2,16,512]{2,1,0:T(8,128)S(1)}, f32[2,16,512]{2,1,0:T(8,128)S(1)}, u32[]{:S(2)}, u32[]{:S(2)}) collective-permute-start(f32[2,16,512]{2,1,0:T(8,128)S(1)} %pad_maximum_fusion.1), channel_id=1, source_target_pairs={{0,192},{16,208},{32,224},{48,240},{64,0},{80,16},{96,32},{112,48}... | collective-permute-start | bytes 196616 | tf_op jit(solution)/shard_map/ppermute | solution.py:32
  18.7 25.0 %collective-permute-start.5 = (f32[2,16,512]{2,1,0:T(8,128)S(1)}, f32[2,16,512]{2,1,0:T(8,128)S(1)}, u32[]{:S(2)}, u32[]{:S(2)}) collective-permute-start(f32[2,16,512]{2,1,0:T(8,128)S(1)} %pad_maximum_fusion.1), channel_id=1, source_target_pairs={{0,160},{16,176},{32,192},{48,208},{64,224},{80,240},{96,0},{112,1... | collective-permute-start | bytes 196616 | tf_op jit(solution)/shard_map/ppermute | solution.py:32
  21.4 22.3 %collective-permute-start.4 = (f32[2,16,512]{2,1,0:T(8,128)S(1)}, f32[2,16,512]{2,1,0:T(8,128)S(1)}, u32[]{:S(2)}, u32[]{:S(2)}) collective-permute-start(f32[2,16,512]{2,1,0:T(8,128)S(1)} %pad_maximum_fusion.1), channel_id=1, source_target_pairs={{0,128},{16,144},{32,160},{48,176},{64,192},{80,208},{96,224},{112... | collective-permute-start | bytes 196616 | tf_op jit(solution)/shard_map/ppermute | solution.py:32
  27.8 15.9 %collective-permute-start.3 = (f32[2,16,512]{2,1,0:T(8,128)S(1)}, f32[2,16,512]{2,1,0:T(8,128)S(1)}, u32[]{:S(2)}, u32[]{:S(2)}) collective-permute-start(f32[2,16,512]{2,1,0:T(8,128)S(1)} %pad_maximum_fusion.1), channel_id=1, source_target_pairs={{0,96},{16,112},{32,128},{48,144},{64,160},{80,176},{96,192},{112,... | collective-permute-start | bytes 196616 | tf_op jit(solution)/shard_map/ppermute | solution.py:32
  29.8 14.0 %collective-permute-start.2 = (f32[2,16,512]{2,1,0:T(8,128)S(1)}, f32[2,16,512]{2,1,0:T(8,128)S(1)}, u32[]{:S(2)}, u32[]{:S(2)}) collective-permute-start(f32[2,16,512]{2,1,0:T(8,128)S(1)} %pad_maximum_fusion.1), channel_id=1, source_target_pairs={{0,64},{16,80},{32,96},{48,112},{64,128},{80,144},{96,160},{112,17... | collective-permute-start | bytes 196616 | tf_op jit(solution)/shard_map/ppermute | solution.py:32
  34.8 9.0 %collective-permute-start.1 = (f32[2,16,512]{2,1,0:T(8,128)S(1)}, f32[2,16,512]{2,1,0:T(8,128)S(1)}, u32[]{:S(2)}, u32[]{:S(2)}) collective-permute-start(f32[2,16,512]{2,1,0:T(8,128)S(1)} %pad_maximum_fusion.1), channel_id=1, source_target_pairs={{0,32},{16,48},{32,64},{48,80},{64,96},{80,112},{96,128},{112,144}... | collective-permute-start | bytes 196616 | tf_op jit(solution)/shard_map/ppermute | solution.py:32
  44.0 16.1 %collective-permute-start.10 = (f32[2,16,512]{2,1,0:T(8,128)S(1)}, f32[2,16,512]{2,1,0:T(8,128)S(1)}, u32[]{:S(2)}, u32[]{:S(2)}) collective-permute-start(f32[2,16,512]{2,1,0:T(8,128)S(1)} %pad_maximum_fusion.2), channel_id=1, source_target_pairs={{0,768},{16,784},{32,800},{48,816},{64,832},{80,848},{96,864},{112... | collective-permute-start | bytes 196616 | tf_op jit(solution)/shard_map/ppermute | solution.py:32
  49.0 11.1 %collective-permute-start.9 = (f32[2,16,512]{2,1,0:T(8,128)S(1)}, f32[2,16,512]{2,1,0:T(8,128)S(1)}, u32[]{:S(2)}, u32[]{:S(2)}) collective-permute-start(f32[2,16,512]{2,1,0:T(8,128)S(1)} %pad_maximum_fusion.2), channel_id=1, source_target_pairs={{0,512},{16,528},{32,544},{48,560},{64,576},{80,592},{96,608},{112... | collective-permute-start | bytes 196616 | tf_op jit(solution)/shard_map/ppermute | solution.py:32
  54.0 11.9 %collective-permute-start.8 = (f32[2,16,512]{2,1,0:T(8,128)S(1)}, f32[2,16,512]{2,1,0:T(8,128)S(1)}, u32[]{:S(2)}, u32[]{:S(2)}) collective-permute-start(f32[2,16,512]{2,1,0:T(8,128)S(1)} %pad_maximum_fusion.2), channel_id=1, source_target_pairs={{0,256},{16,272},{32,288},{48,304},{64,320},{80,336},{96,352},{112... | collective-permute-start | bytes 196616 | tf_op jit(solution)/shard_map/ppermute | solution.py:32
  77.0 18.0 %collective-permute-start.18 = (f32[2,16,512]{2,1,0:T(8,128)S(1)}, f32[2,16,512]{2,1,0:T(8,128)S(1)}, u32[]{:S(2)}, u32[]{:S(2)}) collective-permute-start(f32[2,16,512]{2,1,0:T(8,128)S(1)} %fusion.36), channel_id=1, source_target_pairs={{0,224},{16,240},{32,0},{48,16},{64,32},{80,48},{96,64},{112,80},{... | collective-permute-start | bytes 196616 | tf_op jit(solution)/shard_map/ppermute | solution.py:32
  79.6 20.6 %collective-permute-start.17 = (f32[2,16,512]{2,1,0:T(8,128)S(1)}, f32[2,16,512]{2,1,0:T(8,128)S(1)}, u32[]{:S(2)}, u32[]{:S(2)}) collective-permute-start(f32[2,16,512]{2,1,0:T(8,128)S(1)} %fusion.36), channel_id=1, source_target_pairs={{0,192},{16,208},{32,224},{48,240},{64,0},{80,16},{96,32},{112,48}... | collective-permute-start | bytes 196616 | tf_op jit(solution)/shard_map/ppermute | solution.py:32
  81.5 21.4 %collective-permute-start.16 = (f32[2,16,512]{2,1,0:T(8,128)S(1)}, f32[2,16,512]{2,1,0:T(8,128)S(1)}, u32[]{:S(2)}, u32[]{:S(2)}) collective-permute-start(f32[2,16,512]{2,1,0:T(8,128)S(1)} %fusion.36), channel_id=1, source_target_pairs={{0,160},{16,176},{32,192},{48,208},{64,224},{80,240},{96,0},{112,1... | collective-permute-start | bytes 196616 | tf_op jit(solution)/shard_map/ppermute | solution.py:32
  87.9 15.0 %collective-permute-start.15 = (f32[2,16,512]{2,1,0:T(8,128)S(1)}, f32[2,16,512]{2,1,0:T(8,128)S(1)}, u32[]{:S(2)}, u32[]{:S(2)}) collective-permute-start(f32[2,16,512]{2,1,0:T(8,128)S(1)} %fusion.36), channel_id=1, source_target_pairs={{0,128},{16,144},{32,160},{48,176},{64,192},{80,208},{96,224},{112... | collective-permute-start | bytes 196616 | tf_op jit(solution)/shard_map/ppermute | solution.py:32
  91.2 12.1 %collective-permute-start.14 = (f32[2,16,512]{2,1,0:T(8,128)S(1)}, f32[2,16,512]{2,1,0:T(8,128)S(1)}, u32[]{:S(2)}, u32[]{:S(2)}) collective-permute-start(f32[2,16,512]{2,1,0:T(8,128)S(1)} %fusion.36), channel_id=1, source_target_pairs={{0,96},{16,112},{32,128},{48,144},{64,160},{80,176},{96,192},{112,... | collective-permute-start | bytes 196616 | tf_op jit(solution)/shard_map/ppermute | solution.py:32
  95.0 9.4 %collective-permute-start.12 = (f32[2,16,512]{2,1,0:T(8,128)S(1)}, f32[2,16,512]{2,1,0:T(8,128)S(1)}, u32[]{:S(2)}, u32[]{:S(2)}) collective-permute-start(f32[2,16,512]{2,1,0:T(8,128)S(1)} %fusion.36), channel_id=1, source_target_pairs={{0,32},{16,48},{32,64},{48,80},{64,96},{80,112},{96,128},{112,144}... | collective-permute-start | bytes 196616 | tf_op jit(solution)/shard_map/ppermute | solution.py:32
  100.1 8.3 %collective-permute-start.13 = (f32[2,16,512]{2,1,0:T(8,128)S(1)}, f32[2,16,512]{2,1,0:T(8,128)S(1)}, u32[]{:S(2)}, u32[]{:S(2)}) collective-permute-start(f32[2,16,512]{2,1,0:T(8,128)S(1)} %fusion.36), channel_id=1, source_target_pairs={{0,64},{16,80},{32,96},{48,112},{64,128},{80,144},{96,160},{112,17... | collective-permute-start | bytes 196616 | tf_op jit(solution)/shard_map/ppermute | solution.py:32
  108.5 10.1 %collective-permute-start.21 = (f32[2,16,512]{2,1,0:T(8,128)S(1)}, f32[2,16,512]{2,1,0:T(8,128)S(1)}, u32[]{:S(2)}, u32[]{:S(2)}) collective-permute-start(f32[2,16,512]{2,1,0:T(8,128)S(1)} %add_add_fusion.1), channel_id=1, source_target_pairs={{0,768},{16,784},{32,800},{48,816},{64,832},{80,848},{96,864},{112... | collective-permute-start | bytes 196616 | tf_op jit(solution)/shard_map/ppermute | solution.py:32
  110.4 8.3 %collective-permute-start.19 = (f32[2,16,512]{2,1,0:T(8,128)S(1)}, f32[2,16,512]{2,1,0:T(8,128)S(1)}, u32[]{:S(2)}, u32[]{:S(2)}) collective-permute-start(f32[2,16,512]{2,1,0:T(8,128)S(1)} %add_add_fusion.1), channel_id=1, source_target_pairs={{0,256},{16,272},{32,288},{48,304},{64,320},{80,336},{96,352},{112... | collective-permute-start | bytes 196616 | tf_op jit(solution)/shard_map/ppermute | solution.py:32
  115.2 10.2 %collective-permute-start.20 = (f32[2,16,512]{2,1,0:T(8,128)S(1)}, f32[2,16,512]{2,1,0:T(8,128)S(1)}, u32[]{:S(2)}, u32[]{:S(2)}) collective-permute-start(f32[2,16,512]{2,1,0:T(8,128)S(1)} %add_add_fusion.1), channel_id=1, source_target_pairs={{0,512},{16,528},{32,544},{48,560},{64,576},{80,592},{96,608},{112... | collective-permute-start | bytes 196616 | tf_op jit(solution)/shard_map/ppermute | solution.py:32
  127.4 5.5 %collective-permute-start.22 = (f32[1]{0:T(128)}, f32[1]{0:T(128)}, u32[]{:S(2)}, u32[]{:S(2)}) collective-permute-start(f32[1]{0:T(128)} %bitcast.40), channel_id=1, source_target_pairs={{0,1},{1,0},{2,3},{3,2},{4,5},{5,4},{6,7},{7,6},{8,9},{9,8},{10,11... | collective-permute-start | bytes 20 | tf_op jit(solution)/shard_map/ppermute | solution.py:32
  133.5 9.4 %collective-permute-start.23 = (f32[1]{0:T(128)}, f32[1]{0:T(128)}, u32[]{:S(2)}, u32[]{:S(2)}) collective-permute-start(f32[1]{0:T(128)} %add.367), channel_id=1, source_target_pairs={{0,2},{1,3},{2,0},{3,1},{4,6},{5,7},{6,4},{7,5},{8,10},{9,11},{10,... | collective-permute-start | bytes 20 | tf_op jit(solution)/shard_map/ppermute | solution.py:32
  143.5 13.3 %collective-permute-start.24 = (f32[1]{0:T(128)}, f32[1]{0:T(128)}, u32[]{:S(2)}, u32[]{:S(2)}) collective-permute-start(f32[1]{0:T(128)} %add.368), channel_id=1, source_target_pairs={{0,4},{1,5},{2,6},{3,7},{4,0},{5,1},{6,2},{7,3},{8,12},{9,13},{10,... | collective-permute-start | bytes 20 | tf_op jit(solution)/shard_map/ppermute | solution.py:32
  157.4 5.4 %collective-permute-start.25 = (f32[1]{0:T(128)}, f32[1]{0:T(128)}, u32[]{:S(2)}, u32[]{:S(2)}) collective-permute-start(f32[1]{0:T(128)} %add.369), channel_id=1, source_target_pairs={{0,8},{1,9},{2,10},{3,11},{4,12},{5,13},{6,14},{7,15},{8,0},{9,1},... | collective-permute-start | bytes 20 | tf_op jit(solution)/shard_map/ppermute | solution.py:32
  (9 other events, 210.7 us)

commit v4 on v3

--- a/solution.py
+++ b/solution.py
@@ -33,27 +33,40 @@
     return got
 
 
-def carried_scan(ends, heads, rates, steps, axis, n, groups):
+def fused_scan(pieces, rates, steps, axis, n):
+    ends, heads, w_in, a_in, a_up, w_free, a_free = pieces
     index = lax.axis_index(axis)
-    power = lambda k: jnp.exp(-rates * (steps * k.astype(jnp.float32)))
-    incoming = jnp.zeros_like(ends)
-    upper = jnp.zeros_like(heads)
-    total, btotal = ends, heads
-    for stride, size in levels_of(n, groups):
-        r = (index // stride) % size
-        p = index % stride
-        got = level_gather(jnp.stack([total, btotal]), axis, n, stride, size)
-        new_total = power((size - 1 - r) * stride) * total
-        new_btotal = power(r * stride) * btotal
-        for q, pair in zip(range(1, size), got):
-            rq = (r - q) % size
-            lower = q <= r
-            incoming = incoming + jnp.where(lower, power((q - 1) * stride + p) * pair[0], 0.0)
-            upper = upper + jnp.where(lower, 0.0, power((size - q) * stride - p - 1) * pair[1])
-            new_total = new_total + power((size - 1 - rq) * stride) * pair[0]
-            new_btotal = new_btotal + power(rq * stride) * pair[1]
-        total, btotal = new_total, new_btotal
-    return incoming, upper
+    power = lambda k: jnp.exp(-rates * (steps * jnp.asarray(k).astype(jnp.float32)))
+    a_both = steps * power(1)
+    zeros = jnp.zeros_like(ends)
+    incoming, upper = zeros, zeros
+    group = jnp.stack([ends, heads, w_in, a_in, a_up, zeros, zeros, w_free, a_free])
+    size = 1
+    while size < n:
+        partner = lax.ppermute(group, axis, [(i, i ^ size) for i in range(n)])
+        high = (index // size) % 2 == 1
+        low_g = jnp.where(high, partner, group)
+        high_g = jnp.where(high, group, partner)
+        f_l, b_l, wa_l, wb_l, wc_l, u_l, v_l, zw_l, za_l = low_g
+        f_h, b_h, wa_h, wb_h, wc_h, u_h, v_h, zw_h, za_h = high_g
+        step = power(size)
+        spread = size * power(size - 1)
+        at = index % size
+        incoming = incoming + jnp.where(high, power(at) * f_l, 0.0)
+        upper = upper + jnp.where(high, 0.0, power(size - 1 - at) * b_h)
+        group = jnp.stack([
+            step * f_l + f_h,
+            b_l + step * b_h,
+            wa_l + step * wa_h,
+            wb_l + step * wb_h,
+            step * wc_l + wc_h,
+            step * u_l + (u_h + f_l * spread),
+            (v_l + b_h * spread) + step * v_h,
+            zw_l + zw_h + f_l * wa_h,
+            za_l + za_h + f_l * wb_h + b_h * wc_l + a_both * (b_h * u_l + f_l * v_h),
+        ])
+        size *= 2
+    return incoming, upper, group[7], group[8]
 
 
 def group_sum(x, axis, n, groups):
@@ -84,7 +97,6 @@
 
     ends = jnp.sum(jnp.exp(-rate * (steps - 1.0 - where)) * source[:, None, :], axis=0)
     heads = mixing * jnp.sum(falling * drive[:, None, :], axis=0)
-    incoming, upper = carried_scan(ends, heads, decay_rate, steps, "ctx", peers, CTX_GROUPS)
 
     row = jnp.arange(steps)[:, None]
     col = jnp.arange(steps)[None, :]
@@ -104,17 +116,14 @@
     a_free = jnp.sum(adjoint0 * previous0, axis=0)
     a_in = jnp.sum(adjoint0 * falling, axis=0)
     a_up = jnp.sum(shrunk * previous0, axis=0)
-    a_both = steps * jnp.exp(-decay_rate * steps)
-    grad_w = w_free + incoming * w_in
-    grad_a = a_free + incoming * a_in + upper * a_up + incoming * upper * a_both
+    pieces = (ends, heads, w_in, a_in, a_up, w_free, a_free)
+    incoming, upper, grad_mixing, grad_decay = fused_scan(pieces, decay_rate, steps, "ctx", peers)
 
     states = states0 + grown * incoming[None]
     adjoint = adjoint0 + shrunk * upper[None]
     mixed = jnp.sum(mixing[None] * states, axis=1)
     grad_source = jnp.sum(adjoint, axis=1)
 
-    sums = group_sum(jnp.stack([grad_w, grad_a]), "ctx", peers, CTX_GROUPS)
-    grad_mixing, grad_decay = sums[0], sums[1]
     raw_residue = grad_mixing * norm_factor
     raw_lograte = decay_rate * (
         grad_mixing * residues * decay * decay / norm_factor - decay * grad_decay

time: 166 us -> 163 us (0.982)
  the two profiles are of different devices: /device:TPU:2 before, /device:TPU:48 now
where the time goes in v4:
time: 163 us
  waiting for transfers between devices  67.3 us (41%)
  starting transfers between devices  58.5 us (36%)
  other arithmetic  16.6 us (10%)
  matrix products  12.2 us (7%)
  between operations  5.62 us (3%)
  local copies, waits for them, and re-layouts  2.44 us (1%)
    ppermute x6, waiting for transfers between devices, fused_scan(): partner = lax.ppermute(group, axis, [(i, i ^ size) for i in range(n)])  64.5 us
    ppermute x4, starting transfers between devices, level_gather(): got.append(lax.ppermute(x, axis, perm))  30.8 us
    ppermute x6, starting transfers between devices, fused_scan(): partner = lax.ppermute(group, axis, [(i, i ^ size) for i in range(n)])  27.7 us
    dot_general x1, matrix products, local(): jnp.dot(upper_tri, fallen, precision=HIGHEST).reshape(rising.shape)  9 us
    reduce_sum x1, other arithmetic, local(): grad_source = jnp.sum(adjoint, axis=1)  4.98 us
  transfers between devices with their start and end apart: 10, of which 10 were waited for; matrix products, arithmetic and copies ran while one was open for 0% of the time, Pallas kernels for 0%

profile of v4, /device:TPU:48, one launch (start us, length us, event | category | flops | bytes accessed | tf_op | source)
XLA Modules:
  0.0 162.6 jit_solution(17227661192063939110)
XLA Ops:
  0.7 1.2 convert_multiply_fusion.1
  3.7 1.2 bitcast_multiply_fusion.1
  4.9 3.2 %fusion.1 = f32[128,16,512]{2,0,1:T(8,128)S(1)} fusion(f32[16,512,128]{2,1,0:T(8,128)S(1)} %bitcast.949, f32[16,512]{1,0:T(8,128)S(1)} %get-tuple-element.47), kind=kOutput, calls=%fused_computation.16 | convolution fusion | flops 1612726272 | bytes 8421376 | tf_op jit(solution)/shard_map/dot_general | solution.py:108
  8.1 2.3 %fusion = f32[128,8192]{0,1:T(8,128)S(1)} fusion(f32[128,512]{0,1:T(8,128)S(1)} %copy.41, f32[8192]{0:T(1024)S(1)} %bitcast.953, f32[8192]{0:T(1024)S(1)} %bitcast.954), kind=kLoop, calls=%fused_computation.1 | loop fusion | flops 3145728 | bytes 4521984 | tf_op jit(solution)/shard_map/mul | solution.py:107
  10.5 9.0 %multiply_reduce_fusion.1 = (f32[16,512]{1,0:T(8,128)S(1)}, f32[16,512]{1,0:T(8,128)S(1)}, f32[16,512]{1,0:T(8,128)S(1)}, f32[16,512]{1,0:T(8,128)S(1)}, f32[16,...) fusion(f32[127,16,512]{2,0,1:T(8,128)S(1)} %bitcast.948, ...), kind=kOutput, calls=%fused_computation.5 | convolution fusion | flops 1631543296 | bytes 17565184 | tf_op jit(solution)/shard_map/dot_general | solution.py:109
  19.6 1.9 %collective-permute-start = (f32[9,16,512]{2,1,0:T(8,128)S(1)}, f32[9,16,512]{2,1,0:T(8,128)S(1)}, u32[]{:S(2)}, u32[]{:S(2)}) collective-permute-start(f32[9,16,512]{2,1,0:T(8,128)S(1)} %constant_dynamic-update-slice_fusion), channel_id=1, source_target_pairs={{0,16},{16,0},{32,48},{48,32},{64,80},{80,64},{96,112},{112,96},{1... | collective-permute-start | bytes 884744 | tf_op jit(solution)/shard_map/ppermute | solution.py:46
  21.5 1.5 collective-permute-done
  23.3 2.2 %collective-permute-start.1 = (f32[9,16,512]{2,1,0:T(8,128)S(1)}, f32[9,16,512]{2,1,0:T(8,128)S(1)}, u32[]{:S(2)}, u32[]{:S(2)}) collective-permute-start(f32[9,16,512]{2,1,0:T(8,128)S(1)} %constant_dynamic-update-slice_fusion.8), channel_id=1, source_target_pairs={{0,32},{16,48},{32,0},{48,16},{64,96},{80,112},{96,64},{112,80},{1... | collective-permute-start | bytes 884744 | tf_op jit(solution)/shard_map/ppermute | solution.py:46
  25.6 8.7 %collective-permute-done.1 = f32[9,16,512]{2,1,0:T(8,128)S(1)} collective-permute-done((f32[9,16,512]{2,1,0:T(8,128)S(1)}, f32[9,16,512]{2,1,0:T(8,128)S(1)}, u32[]{:S(2)}, u32[]{:S(2)}) %collective-permute-start.1) | collective-permute-done | bytes 294944 | tf_op jit(solution)/shard_map/ppermute | solution.py:46
  34.6 13.3 %collective-permute-start.2 = (f32[9,16,512]{2,1,0:T(8,128)S(1)}, f32[9,16,512]{2,1,0:T(8,128)S(1)}, u32[]{:S(2)}, u32[]{:S(2)}) collective-permute-start(f32[9,16,512]{2,1,0:T(8,128)S(1)} %constant_dynamic-update-slice_fusion.17), channel_id=1, source_target_pairs={{0,64},{16,80},{32,96},{48,112},{64,0},{80,16},{96,32},{112,48},{1... | collective-permute-start | bytes 884744 | tf_op jit(solution)/shard_map/ppermute | solution.py:46
  47.9 13.1 %collective-permute-done.2 = f32[9,16,512]{2,1,0:T(8,128)S(1)} collective-permute-done((f32[9,16,512]{2,1,0:T(8,128)S(1)}, f32[9,16,512]{2,1,0:T(8,128)S(1)}, u32[]{:S(2)}, u32[]{:S(2)}) %collective-permute-start.2) | collective-permute-done | bytes 294944 | tf_op jit(solution)/shard_map/ppermute | solution.py:46
  61.3 1.9 %collective-permute-start.3 = (f32[9,16,512]{2,1,0:T(8,128)S(1)}, f32[9,16,512]{2,1,0:T(8,128)S(1)}, u32[]{:S(2)}, u32[]{:S(2)}) collective-permute-start(f32[9,16,512]{2,1,0:T(8,128)S(1)} %constant_dynamic-update-slice_fusion.26), channel_id=1, source_target_pairs={{0,128},{16,144},{32,160},{48,176},{64,192},{80,208},{96,224},{112... | collective-permute-start | bytes 884744 | tf_op jit(solution)/shard_map/ppermute | solution.py:46
  63.2 15.7 %collective-permute-done.3 = f32[9,16,512]{2,1,0:T(8,128)S(1)} collective-permute-done((f32[9,16,512]{2,1,0:T(8,128)S(1)}, f32[9,16,512]{2,1,0:T(8,128)S(1)}, u32[]{:S(2)}, u32[]{:S(2)}) %collective-permute-start.3) | collective-permute-done | bytes 294944 | tf_op jit(solution)/shard_map/ppermute | solution.py:46
  79.2 1.9 %collective-permute-start.4 = (f32[9,16,512]{2,1,0:T(8,128)S(1)}, f32[9,16,512]{2,1,0:T(8,128)}, u32[]{:S(2)}, u32[]{:S(2)}) collective-permute-start(f32[9,16,512]{2,1,0:T(8,128)S(1)} %constant_dynamic-update-slice_fusion.35), channel_id=1, source_target_pairs={{0,256},{16,272},{32,288},{48,304},{64,320},{80,336},{96,352},{112... | collective-permute-start | bytes 884744 | tf_op jit(solution)/shard_map/ppermute | solution.py:46
  81.2 10.9 %collective-permute-done.4 = f32[9,16,512]{2,1,0:T(8,128)} collective-permute-done((f32[9,16,512]{2,1,0:T(8,128)S(1)}, f32[9,16,512]{2,1,0:T(8,128)}, u32[]{:S(2)}, u32[]{:S(2)}) %collective-permute-start.4) | collective-permute-done | bytes 294944 | tf_op jit(solution)/shard_map/ppermute | solution.py:46
  93.4 6.4 %collective-permute-start.5 = (f32[9,16,512]{2,1,0:T(8,128)S(1)}, f32[9,16,512]{2,1,0:T(8,128)}, u32[]{:S(2)}, u32[]{:S(2)}) collective-permute-start(f32[9,16,512]{2,1,0:T(8,128)S(1)} %constant_dynamic-update-slice_fusion.44), channel_id=1, source_target_pairs={{0,512},{16,528},{32,544},{48,560},{64,576},{80,592},{96,608},{112... | collective-permute-start | bytes 884744 | tf_op jit(solution)/shard_map/ppermute | solution.py:46
  99.9 14.6 %collective-permute-done.5 = f32[9,16,512]{2,1,0:T(8,128)} collective-permute-done((f32[9,16,512]{2,1,0:T(8,128)S(1)}, f32[9,16,512]{2,1,0:T(8,128)}, u32[]{:S(2)}, u32[]{:S(2)}) %collective-permute-start.5) | collective-permute-done | bytes 294944 | tf_op jit(solution)/shard_map/ppermute | solution.py:46
  114.6 1.0 broadcast_select_fusion.1
  117.0 5.0 %add_reduce_fusion = (f32[128,512]{1,0:T(8,128)S(1)}, f32[128,512]{1,0:T(8,128)S(1)}) fusion(f32[128,16,512]{2,0,1:T(8,128)} %get-tuple-element.50, f32[16,512]{1,0:T(8,128)S(1)} %select_add_fusion, f32[128]{0:T(128)S(1)} %get-tuple-element.53, f32[16,512]{1,0:T(8,128)S(1)} %copy-done, f32[16,512]{1,0:T(8,128)S(1)} %get-tuple-element.47, ...), kind=kLoop, calls=%fused_computation.3 | loop fusion | flops 11403264 | bytes 9077760 | tf_op jit(solution)/shard_map/reduce_sum | solution.py:125
  124.8 5.3 %collective-permute-start.6 = (f32[1]{0:T(128)}, f32[1]{0:T(128)}, u32[]{:S(2)}, u32[]{:S(2)}) collective-permute-start(f32[1]{0:T(128)} %bitcast.139), channel_id=1, source_target_pairs={{0,1},{1,0},{2,3},{3,2},{4,5},{5,4},{6,7},{7,6},{8,9},{9,8},{10,11... | collective-permute-start | bytes 20 | tf_op jit(solution)/shard_map/ppermute | solution.py:32
  131.0 9.2 %collective-permute-start.7 = (f32[1]{0:T(128)}, f32[1]{0:T(128)}, u32[]{:S(2)}, u32[]{:S(2)}) collective-permute-start(f32[1]{0:T(128)} %add.523), channel_id=1, source_target_pairs={{0,2},{1,3},{2,0},{3,1},{4,6},{5,7},{6,4},{7,5},{8,10},{9,11},{10,... | collective-permute-start | bytes 20 | tf_op jit(solution)/shard_map/ppermute | solution.py:32
  141.0 13.1 %collective-permute-start.8 = (f32[1]{0:T(128)}, f32[1]{0:T(128)}, u32[]{:S(2)}, u32[]{:S(2)}) collective-permute-start(f32[1]{0:T(128)} %add.524), channel_id=1, source_target_pairs={{0,4},{1,5},{2,6},{3,7},{4,0},{5,1},{6,2},{7,3},{8,12},{9,13},{10,... | collective-permute-start | bytes 20 | tf_op jit(solution)/shard_map/ppermute | solution.py:32
  155.0 3.2 %collective-permute-start.9 = (f32[1]{0:T(128)}, f32[1]{0:T(128)}, u32[]{:S(2)}, u32[]{:S(2)}) collective-permute-start(f32[1]{0:T(128)} %add.525), channel_id=1, source_target_pairs={{0,8},{1,9},{2,10},{3,11},{4,12},{5,13},{6,14},{7,15},{8,0},{9,1},... | collective-permute-start | bytes 20 | tf_op jit(solution)/shard_map/ppermute | solution.py:32
  158.2 2.2 %collective-permute-done.9 = f32[1]{0:T(128)} collective-permute-done((f32[1]{0:T(128)}, f32[1]{0:T(128)}, u32[]{:S(2)}, u32[]{:S(2)}) %collective-permute-start.9) | collective-permute-done | bytes 36 | tf_op jit(solution)/shard_map/ppermute | solution.py:32
  (92 shorter events, 8.9 us)
Async XLA Ops:
  8.1 11.4 %copy-start.1 = (f32[128,16,512]{2,0,1:T(8,128)}, f32[128,16,512]{2,0,1:T(8,128)S(1)}, u32[]{:S(2)}) copy-start(f32[128,16,512]{2,0,1:T(8,128)S(1)} %fusion.1) | copy-start | bytes 12582916
  8.1 2.4 %copy-start = (f32[16,512]{1,0:T(8,128)S(1)}, f32[16,512]{1,0:T(8,128)}, u32[]{:S(2)}) copy-start(f32[16,512]{1,0:T(8,128)} %param.11) | copy-start | bytes 98308
  19.6 3.5 %collective-permute-start = (f32[9,16,512]{2,1,0:T(8,128)S(1)}, f32[9,16,512]{2,1,0:T(8,128)S(1)}, u32[]{:S(2)}, u32[]{:S(2)}) collective-permute-start(f32[9,16,512]{2,1,0:T(8,128)S(1)} %constant_dynamic-update-slice_fusion), channel_id=1, source_target_pairs={{0,16},{16,0},{32,48},{48,32},{64,80},{80,64},{96,112},{112,96},{1... | collective-permute-start | bytes 884744 | tf_op jit(solution)/shard_map/ppermute | solution.py:46
  23.3 10.9 %collective-permute-start.1 = (f32[9,16,512]{2,1,0:T(8,128)S(1)}, f32[9,16,512]{2,1,0:T(8,128)S(1)}, u32[]{:S(2)}, u32[]{:S(2)}) collective-permute-start(f32[9,16,512]{2,1,0:T(8,128)S(1)} %constant_dynamic-update-slice_fusion.8), channel_id=1, source_target_pairs={{0,32},{16,48},{32,0},{48,16},{64,96},{80,112},{96,64},{112,80},{1... | collective-permute-start | bytes 884744 | tf_op jit(solution)/shard_map/ppermute | solution.py:46
  34.6 26.4 %collective-permute-start.2 = (f32[9,16,512]{2,1,0:T(8,128)S(1)}, f32[9,16,512]{2,1,0:T(8,128)S(1)}, u32[]{:S(2)}, u32[]{:S(2)}) collective-permute-start(f32[9,16,512]{2,1,0:T(8,128)S(1)} %constant_dynamic-update-slice_fusion.17), channel_id=1, source_target_pairs={{0,64},{16,80},{32,96},{48,112},{64,0},{80,16},{96,32},{112,48},{1... | collective-permute-start | bytes 884744 | tf_op jit(solution)/shard_map/ppermute | solution.py:46
  61.0 54.6 %copy-start.6 = (f32[16,512]{1,0:T(8,128)S(1)}, f32[16,512]{1,0:T(8,128)}, u32[]{:S(2)}) copy-start(f32[16,512]{1,0:T(8,128)} %param.10) | copy-start | bytes 98308
  61.3 17.7 %collective-permute-start.3 = (f32[9,16,512]{2,1,0:T(8,128)S(1)}, f32[9,16,512]{2,1,0:T(8,128)S(1)}, u32[]{:S(2)}, u32[]{:S(2)}) collective-permute-start(f32[9,16,512]{2,1,0:T(8,128)S(1)} %constant_dynamic-update-slice_fusion.26), channel_id=1, source_target_pairs={{0,128},{16,144},{32,160},{48,176},{64,192},{80,208},{96,224},{112... | collective-permute-start | bytes 884744 | tf_op jit(solution)/shard_map/ppermute | solution.py:46
  79.2 12.9 %collective-permute-start.4 = (f32[9,16,512]{2,1,0:T(8,128)S(1)}, f32[9,16,512]{2,1,0:T(8,128)}, u32[]{:S(2)}, u32[]{:S(2)}) collective-permute-start(f32[9,16,512]{2,1,0:T(8,128)S(1)} %constant_dynamic-update-slice_fusion.35), channel_id=1, source_target_pairs={{0,256},{16,272},{32,288},{48,304},{64,320},{80,336},{96,352},{112... | collective-permute-start | bytes 884744 | tf_op jit(solution)/shard_map/ppermute | solution.py:46
  93.4 21.2 %collective-permute-start.5 = (f32[9,16,512]{2,1,0:T(8,128)S(1)}, f32[9,16,512]{2,1,0:T(8,128)}, u32[]{:S(2)}, u32[]{:S(2)}) collective-permute-start(f32[9,16,512]{2,1,0:T(8,128)S(1)} %constant_dynamic-update-slice_fusion.44), channel_id=1, source_target_pairs={{0,512},{16,528},{32,544},{48,560},{64,576},{80,592},{96,608},{112... | collective-permute-start | bytes 884744 | tf_op jit(solution)/shard_map/ppermute | solution.py:46
  117.0 5.0 %copy-start.2 = (bf16[128,512]{1,0:T(8,128)(2,1)S(1)}, bf16[128,512]{1,0:T(8,128)(2,1)}, u32[]{:S(2)}) copy-start(bf16[128,512]{1,0:T(8,128)(2,1)} %param.9) | copy-start | bytes 393220
  117.0 5.0 %copy-start.3 = (bf16[128,512]{1,0:T(8,128)(2,1)S(1)}, bf16[128,512]{1,0:T(8,128)(2,1)}, u32[]{:S(2)}) copy-start(bf16[128,512]{1,0:T(8,128)(2,1)} %param.6) | copy-start | bytes 393220
  117.0 5.8 %copy-start.4 = (bf16[128,512]{1,0:T(8,128)(2,1)S(1)}, bf16[128,512]{1,0:T(8,128)(2,1)}, u32[]{:S(2)}) copy-start(bf16[128,512]{1,0:T(8,128)(2,1)} %param.8) | copy-start | bytes 393220
  117.0 5.8 %copy-start.5 = (bf16[128,512]{1,0:T(8,128)(2,1)S(1)}, bf16[128,512]{1,0:T(8,128)(2,1)}, u32[]{:S(2)}) copy-start(bf16[128,512]{1,0:T(8,128)(2,1)} %param.7) | copy-start | bytes 393220
  124.8 5.4 %collective-permute-start.6 = (f32[1]{0:T(128)}, f32[1]{0:T(128)}, u32[]{:S(2)}, u32[]{:S(2)}) collective-permute-start(f32[1]{0:T(128)} %bitcast.139), channel_id=1, source_target_pairs={{0,1},{1,0},{2,3},{3,2},{4,5},{5,4},{6,7},{7,6},{8,9},{9,8},{10,11... | collective-permute-start | bytes 20 | tf_op jit(solution)/shard_map/ppermute | solution.py:32
  131.0 9.3 %collective-permute-start.7 = (f32[1]{0:T(128)}, f32[1]{0:T(128)}, u32[]{:S(2)}, u32[]{:S(2)}) collective-permute-start(f32[1]{0:T(128)} %add.523), channel_id=1, source_target_pairs={{0,2},{1,3},{2,0},{3,1},{4,6},{5,7},{6,4},{7,5},{8,10},{9,11},{10,... | collective-permute-start | bytes 20 | tf_op jit(solution)/shard_map/ppermute | solution.py:32
  141.0 13.3 %collective-permute-start.8 = (f32[1]{0:T(128)}, f32[1]{0:T(128)}, u32[]{:S(2)}, u32[]{:S(2)}) collective-permute-start(f32[1]{0:T(128)} %add.524), channel_id=1, source_target_pairs={{0,4},{1,5},{2,6},{3,7},{4,0},{5,1},{6,2},{7,3},{8,12},{9,13},{10,... | collective-permute-start | bytes 20 | tf_op jit(solution)/shard_map/ppermute | solution.py:32
  155.0 5.4 %collective-permute-start.9 = (f32[1]{0:T(128)}, f32[1]{0:T(128)}, u32[]{:S(2)}, u32[]{:S(2)}) collective-permute-start(f32[1]{0:T(128)} %add.525), channel_id=1, source_target_pairs={{0,8},{1,9},{2,10},{3,11},{4,12},{5,13},{6,14},{7,15},{8,0},{9,1},... | collective-permute-start | bytes 20 | tf_op jit(solution)/shard_map/ppermute | solution.py:32

commit v5 on v4

--- a/solution.py
+++ b/solution.py
@@ -40,23 +40,34 @@
     a_both = steps * power(1)
     zeros = jnp.zeros_like(ends)
     incoming, upper = zeros, zeros
-    group = jnp.stack([ends, heads, w_in, a_in, a_up, zeros, zeros, w_free, a_free])
+    carry = jnp.stack([ends, heads])
+    group = jnp.stack([w_in, a_in, a_up, zeros, zeros, w_free, a_free])
+    sizes = []
     size = 1
     while size < n:
-        partner = lax.ppermute(group, axis, [(i, i ^ size) for i in range(n)])
+        sizes.append(size)
+        size *= 2
+    pairs_of = lambda size: [(i, i ^ size) for i in range(n)]
+    carry_partner = lax.ppermute(carry, axis, pairs_of(1)) if sizes else None
+    for k, size in enumerate(sizes):
         high = (index // size) % 2 == 1
-        low_g = jnp.where(high, partner, group)
-        high_g = jnp.where(high, group, partner)
-        f_l, b_l, wa_l, wb_l, wc_l, u_l, v_l, zw_l, za_l = low_g
-        f_h, b_h, wa_h, wb_h, wc_h, u_h, v_h, zw_h, za_h = high_g
+        f_l, b_l = jnp.where(high, carry_partner, carry)
+        f_h, b_h = jnp.where(high, carry, carry_partner)
         step = power(size)
         spread = size * power(size - 1)
         at = index % size
         incoming = incoming + jnp.where(high, power(at) * f_l, 0.0)
         upper = upper + jnp.where(high, 0.0, power(size - 1 - at) * b_h)
+        carry = jnp.stack([step * f_l + f_h, b_l + step * b_h])
+        partner = lax.ppermute(group, axis, pairs_of(size))
+        if k + 1 < len(sizes):
+            carry_partner = lax.ppermute(carry, axis, pairs_of(sizes[k + 1]))
+            partner, carry_partner = lax.optimization_barrier((partner, carry_partner))
+        low_g = jnp.where(high, partner, group)
+        high_g = jnp.where(high, group, partner)
+        wa_l, wb_l, wc_l, u_l, v_l, zw_l, za_l = low_g
+        wa_h, wb_h, wc_h, u_h, v_h, zw_h, za_h = high_g
         group = jnp.stack([
-            step * f_l + f_h,
-            b_l + step * b_h,
             wa_l + step * wa_h,
             wb_l + step * wb_h,
             step * wc_l + wc_h,
@@ -65,8 +76,7 @@
             zw_l + zw_h + f_l * wa_h,
             za_l + za_h + f_l * wb_h + b_h * wc_l + a_both * (b_h * u_l + f_l * v_h),
         ])
-        size *= 2
-    return incoming, upper, group[7], group[8]
+    return incoming, upper, group[5], group[6]
 
 
 def group_sum(x, axis, n, groups):

time: 163 us -> 155 us (0.951)
  the two profiles are of different devices: /device:TPU:48 before, /device:TPU:126 now
where the time goes in v5:
time: 155 us; the launch traced here: 154 us
  starting transfers between devices  73.6 us (47%)
  waiting for transfers between devices  46.1 us (30%)
  other arithmetic  14.1 us (9%)
  matrix products  12.2 us (8%)
  between operations  5.49 us (4%)
  local copies, waits for them, and re-layouts  2.44 us (2%)
    ppermute x4, starting transfers between devices, level_gather(): got.append(lax.ppermute(x, axis, perm))  33.9 us
    ppermute x5, waiting for transfers between devices, fused_scan(): carry_partner = lax.ppermute(carry, axis, pairs_of(sizes[k + 1]))  23.4 us
    ppermute x6, starting transfers between devices, fused_scan(): partner = lax.ppermute(group, axis, pairs_of(size))  20.3 us
    ppermute x6, waiting for transfers between devices, fused_scan(): partner = lax.ppermute(group, axis, pairs_of(size))  19.3 us
    ppermute x5, starting transfers between devices, fused_scan(): carry_partner = lax.ppermute(carry, axis, pairs_of(sizes[k + 1]))  17.4 us
    dot_general x1, matrix products, local(): jnp.dot(upper_tri, fallen, precision=HIGHEST).reshape(rising.shape)  8.99 us
    reduce_sum x1, other arithmetic, local(): grad_source = jnp.sum(adjoint, axis=1)  4.39 us
    ppermute x4, waiting for transfers between devices, level_gather(): got.append(lax.ppermute(x, axis, perm))  3.34 us
  transfers between devices with their start and end apart: 16, of which 13 were waited for; matrix products, arithmetic and copies ran while one was open for 0% of the time, Pallas kernels for 0%

profile of v5, /device:TPU:126, one launch (start us, length us, event | category | flops | bytes accessed | tf_op | source)
XLA Modules:
  0.0 153.8 jit_solution(5248498797126903297)
XLA Ops:
  4.9 3.2 %fusion.1 = f32[128,16,512]{2,0,1:T(8,128)S(1)} fusion(f32[16,512,128]{2,1,0:T(8,128)S(1)} %bitcast.901, f32[16,512]{1,0:T(8,128)S(1)} %get-tuple-element.87), kind=kOutput, calls=%fused_computation.16 | convolution fusion | flops 1612726272 | bytes 8421376 | tf_op jit(solution)/shard_map/dot_general | solution.py:118
  10.5 9.0 %multiply_reduce_fusion.1 = (f32[16,512]{1,0:T(8,128)S(1)}, f32[16,512]{1,0:T(8,128)S(1)}, f32[16,512]{1,0:T(8,128)S(1)}, f32[16,512]{1,0:T(8,128)S(1)}, f32[16,...) fusion(f32[127,16,512]{2,0,1:T(8,128)S(1)} %bitcast.900, ...), kind=kOutput, calls=%fused_computation.5 | convolution fusion | flops 1631543296 | bytes 17565184 | tf_op jit(solution)/shard_map/dot_general | solution.py:119
  24.0 3.1 %collective-permute-start.2 = (f32[2,16,512]{2,1,0:T(8,128)S(1)}, f32[2,16,512]{2,1,0:T(8,128)S(1)}, u32[]{:S(2)}, u32[]{:S(2)}) collective-permute-start(f32[2,16,512]{2,1,0:T(8,128)S(1)} %pad_maximum_fusion.2), channel_id=1, source_target_pairs={{0,32},{16,48},{32,0},{48,16},{64,96},{80,112},{96,64},{112,80},{1... | collective-permute-start | bytes 196616 | tf_op jit(solution)/shard_map/ppermute | solution.py:64
  27.2 3.0 %collective-permute-done.2 = f32[2,16,512]{2,1,0:T(8,128)S(1)} collective-permute-done((f32[2,16,512]{2,1,0:T(8,128)S(1)}, f32[2,16,512]{2,1,0:T(8,128)S(1)}, u32[]{:S(2)}, u32[]{:S(2)}) %collective-permute-start.2) | collective-permute-done | bytes 65568 | tf_op jit(solution)/shard_map/ppermute | solution.py:64
  30.4 3.1 %collective-permute-start.3 = (f32[7,16,512]{2,1,0:T(8,128)S(1)}, f32[7,16,512]{2,1,0:T(8,128)S(1)}, u32[]{:S(2)}, u32[]{:S(2)}) collective-permute-start(f32[7,16,512]{2,1,0:T(8,128)S(1)} %constant_dynamic-update-slice_fusion.6), channel_id=1, source_target_pairs={{0,32},{16,48},{32,0},{48,16},{64,96},{80,112},{96,64},{112,80},{1... | collective-permute-start | bytes 688136 | tf_op jit(solution)/shard_map/ppermute | solution.py:62
  33.6 3.8 %collective-permute-start.4 = (f32[2,16,512]{2,1,0:T(8,128)S(1)}, f32[2,16,512]{2,1,0:T(8,128)S(1)}, u32[]{:S(2)}, u32[]{:S(2)}) collective-permute-start(f32[2,16,512]{2,1,0:T(8,128)S(1)} %pad_maximum_fusion.3), channel_id=1, source_target_pairs={{0,64},{16,80},{32,96},{48,112},{64,0},{80,16},{96,32},{112,48},{1... | collective-permute-start | bytes 196616 | tf_op jit(solution)/shard_map/ppermute | solution.py:64
  37.5 3.2 %collective-permute-done.4 = f32[2,16,512]{2,1,0:T(8,128)S(1)} collective-permute-done((f32[2,16,512]{2,1,0:T(8,128)S(1)}, f32[2,16,512]{2,1,0:T(8,128)S(1)}, u32[]{:S(2)}, u32[]{:S(2)}) %collective-permute-start.4) | collective-permute-done | bytes 65568 | tf_op jit(solution)/shard_map/ppermute | solution.py:64
  40.9 3.9 %collective-permute-start.5 = (f32[7,16,512]{2,1,0:T(8,128)S(1)}, f32[7,16,512]{2,1,0:T(8,128)S(1)}, u32[]{:S(2)}, u32[]{:S(2)}) collective-permute-start(f32[7,16,512]{2,1,0:T(8,128)S(1)} %constant_dynamic-update-slice_fusion.13), channel_id=1, source_target_pairs={{0,64},{16,80},{32,96},{48,112},{64,0},{80,16},{96,32},{112,48},{1... | collective-permute-start | bytes 688136 | tf_op jit(solution)/shard_map/ppermute | solution.py:62
  44.8 2.9 %collective-permute-start.6 = (f32[2,16,512]{2,1,0:T(8,128)S(1)}, f32[2,16,512]{2,1,0:T(8,128)S(1)}, u32[]{:S(2)}, u32[]{:S(2)}) collective-permute-start(f32[2,16,512]{2,1,0:T(8,128)S(1)} %pad_maximum_fusion.4), channel_id=1, source_target_pairs={{0,128},{16,144},{32,160},{48,176},{64,192},{80,208},{96,224},{112... | collective-permute-start | bytes 196616 | tf_op jit(solution)/shard_map/ppermute | solution.py:64
  47.8 7.7 %collective-permute-done.6 = f32[2,16,512]{2,1,0:T(8,128)S(1)} collective-permute-done((f32[2,16,512]{2,1,0:T(8,128)S(1)}, f32[2,16,512]{2,1,0:T(8,128)S(1)}, u32[]{:S(2)}, u32[]{:S(2)}) %collective-permute-start.6) | collective-permute-done | bytes 65568 | tf_op jit(solution)/shard_map/ppermute | solution.py:64
  57.0 3.0 %collective-permute-start.7 = (f32[7,16,512]{2,1,0:T(8,128)S(1)}, f32[7,16,512]{2,1,0:T(8,128)S(1)}, u32[]{:S(2)}, u32[]{:S(2)}) collective-permute-start(f32[7,16,512]{2,1,0:T(8,128)S(1)} %constant_dynamic-update-slice_fusion.20), channel_id=1, source_target_pairs={{0,128},{16,144},{32,160},{48,176},{64,192},{80,208},{96,224},{112... | collective-permute-start | bytes 688136 | tf_op jit(solution)/shard_map/ppermute | solution.py:62
  60.1 4.2 %collective-permute-start.8 = (f32[2,16,512]{2,1,0:T(8,128)S(1)}, f32[2,16,512]{2,1,0:T(8,128)S(1)}, u32[]{:S(2)}, u32[]{:S(2)}) collective-permute-start(f32[2,16,512]{2,1,0:T(8,128)S(1)} %pad_maximum_fusion.5), channel_id=1, source_target_pairs={{0,256},{16,272},{32,288},{48,304},{64,320},{80,336},{96,352},{112... | collective-permute-start | bytes 196616 | tf_op jit(solution)/shard_map/ppermute | solution.py:64
  64.4 2.8 %collective-permute-done.8 = f32[2,16,512]{2,1,0:T(8,128)S(1)} collective-permute-done((f32[2,16,512]{2,1,0:T(8,128)S(1)}, f32[2,16,512]{2,1,0:T(8,128)S(1)}, u32[]{:S(2)}, u32[]{:S(2)}) %collective-permute-start.8) | collective-permute-done | bytes 65568 | tf_op jit(solution)/shard_map/ppermute | solution.py:64
  67.2 4.8 %collective-permute-done.7 = f32[7,16,512]{2,1,0:T(8,128)S(1)} collective-permute-done((f32[7,16,512]{2,1,0:T(8,128)S(1)}, f32[7,16,512]{2,1,0:T(8,128)S(1)}, u32[]{:S(2)}, u32[]{:S(2)}) %collective-permute-start.7) | collective-permute-done | bytes 229408 | tf_op jit(solution)/shard_map/ppermute | solution.py:62
  72.3 4.2 %collective-permute-start.9 = (f32[7,16,512]{2,1,0:T(8,128)S(1)}, f32[7,16,512]{2,1,0:T(8,128)S(1)}, u32[]{:S(2)}, u32[]{:S(2)}) collective-permute-start(f32[7,16,512]{2,1,0:T(8,128)S(1)} %constant_dynamic-update-slice_fusion.27), channel_id=1, source_target_pairs={{0,256},{16,272},{32,288},{48,304},{64,320},{80,336},{96,352},{112... | collective-permute-start | bytes 688136 | tf_op jit(solution)/shard_map/ppermute | solution.py:62
  76.5 3.3 %collective-permute-start.10 = (f32[2,16,512]{2,1,0:T(8,128)S(1)}, f32[2,16,512]{2,1,0:T(8,128)S(1)}, u32[]{:S(2)}, u32[]{:S(2)}) collective-permute-start(f32[2,16,512]{2,1,0:T(8,128)S(1)} %pad_maximum_fusion), channel_id=1, source_target_pairs={{0,512},{16,528},{32,544},{48,560},{64,576},{80,592},{96,608},{112... | collective-permute-start | bytes 196616 | tf_op jit(solution)/shard_map/ppermute | solution.py:64
  79.9 6.7 %collective-permute-done.10 = f32[2,16,512]{2,1,0:T(8,128)S(1)} collective-permute-done((f32[2,16,512]{2,1,0:T(8,128)S(1)}, f32[2,16,512]{2,1,0:T(8,128)S(1)}, u32[]{:S(2)}, u32[]{:S(2)}) %collective-permute-start.10) | collective-permute-done | bytes 65568 | tf_op jit(solution)/shard_map/ppermute | solution.py:64
  86.9 3.7 %collective-permute-start.11 = (f32[7,16,512]{2,1,0:T(8,128)S(1)}, f32[7,16,512]{2,1,0:T(8,128)S(1)}, u32[]{:S(2)}, u32[]{:S(2)}) collective-permute-start(f32[7,16,512]{2,1,0:T(8,128)S(1)} %constant_dynamic-update-slice_fusion.34), channel_id=1, source_target_pairs={{0,512},{16,528},{32,544},{48,560},{64,576},{80,592},{96,608},{112... | collective-permute-start | bytes 688136 | tf_op jit(solution)/shard_map/ppermute | solution.py:62
  90.7 13.1 %collective-permute-done.11 = f32[7,16,512]{2,1,0:T(8,128)S(1)} collective-permute-done((f32[7,16,512]{2,1,0:T(8,128)S(1)}, f32[7,16,512]{2,1,0:T(8,128)S(1)}, u32[]{:S(2)}, u32[]{:S(2)}) %collective-permute-start.11) | collective-permute-done | bytes 229408 | tf_op jit(solution)/shard_map/ppermute | solution.py:62
  105.2 4.4 %add_reduce_fusion = (f32[128,512]{1,0:T(8,128)S(1)}, f32[128,512]{1,0:T(8,128)S(1)}) fusion(f32[128,16,512]{2,0,1:T(8,128)} %get-tuple-element.90, f32[16,512]{1,0:T(8,128)S(1)} %select_add_fusion, f32[128]{0:T(128)S(1)} %get-tuple-element.93, f32[16,512]{1,0:T(8,128)S(1)} %copy-done, f32[16,512]{1,0:T(8,128)S(1)} %get-tuple-element.87, ...), kind=kLoop, calls=%fused_computation.3 | loop fusion | flops 11403264 | bytes 9077760 | tf_op jit(solution)/shard_map/reduce_sum | solution.py:135
  112.5 8.4 %collective-permute-start.12 = (f32[1]{0:T(128)}, f32[1]{0:T(128)}, u32[]{:S(2)}, u32[]{:S(2)}) collective-permute-start(f32[1]{0:T(128)} %bitcast.139), channel_id=1, source_target_pairs={{0,1},{1,0},{2,3},{3,2},{4,5},{5,4},{6,7},{7,6},{8,9},{9,8},{10,11... | collective-permute-start | bytes 20 | tf_op jit(solution)/shard_map/ppermute | solution.py:32
  121.9 9.1 %collective-permute-start.13 = (f32[1]{0:T(128)}, f32[1]{0:T(128)}, u32[]{:S(2)}, u32[]{:S(2)}) collective-permute-start(f32[1]{0:T(128)} %add.523), channel_id=1, source_target_pairs={{0,2},{1,3},{2,0},{3,1},{4,6},{5,7},{6,4},{7,5},{8,10},{9,11},{10,... | collective-permute-start | bytes 20 | tf_op jit(solution)/shard_map/ppermute | solution.py:32
  132.0 13.2 %collective-permute-start.14 = (f32[1]{0:T(128)}, f32[1]{0:T(128)}, u32[]{:S(2)}, u32[]{:S(2)}) collective-permute-start(f32[1]{0:T(128)} %add.524), channel_id=1, source_target_pairs={{0,4},{1,5},{2,6},{3,7},{4,0},{5,1},{6,2},{7,3},{8,12},{9,13},{10,... | collective-permute-start | bytes 20 | tf_op jit(solution)/shard_map/ppermute | solution.py:32
  146.1 3.2 %collective-permute-start.15 = (f32[1]{0:T(128)}, f32[1]{0:T(128)}, u32[]{:S(2)}, u32[]{:S(2)}) collective-permute-start(f32[1]{0:T(128)} %add.525), channel_id=1, source_target_pairs={{0,8},{1,9},{2,10},{3,11},{4,12},{5,13},{6,14},{7,15},{8,0},{9,1},... | collective-permute-start | bytes 20 | tf_op jit(solution)/shard_map/ppermute | solution.py:32
  (111 shorter events, 21.2 us)
Async XLA Ops:
  8.1 11.4 %copy-start.1 = (f32[128,16,512]{2,0,1:T(8,128)}, f32[128,16,512]{2,0,1:T(8,128)S(1)}, u32[]{:S(2)}) copy-start(f32[128,16,512]{2,0,1:T(8,128)S(1)} %fusion.1) | copy-start | bytes 12582916
  8.1 2.4 %copy-start = (f32[16,512]{1,0:T(8,128)S(1)}, f32[16,512]{1,0:T(8,128)}, u32[]{:S(2)}) copy-start(f32[16,512]{1,0:T(8,128)} %param.11) | copy-start | bytes 98308
  19.5 4.4 %collective-permute-start = (f32[2,16,512]{2,1,0:T(8,128)S(1)}, f32[2,16,512]{2,1,0:T(8,128)S(1)}, u32[]{:S(2)}, u32[]{:S(2)}) collective-permute-start(f32[2,16,512]{2,1,0:T(8,128)S(1)} %pad_maximum_fusion.1), channel_id=1, source_target_pairs={{0,16},{16,0},{32,48},{48,32},{64,80},{80,64},{96,112},{112,96},{1... | collective-permute-start | bytes 196616 | tf_op jit(solution)/shard_map/ppermute | solution.py:51
  21.5 8.7 %collective-permute-start.1 = (f32[7,16,512]{2,1,0:T(8,128)S(1)}, f32[7,16,512]{2,1,0:T(8,128)S(1)}, u32[]{:S(2)}, u32[]{:S(2)}) collective-permute-start(f32[7,16,512]{2,1,0:T(8,128)S(1)} %constant_dynamic-update-slice_fusion), channel_id=1, source_target_pairs={{0,16},{16,0},{32,48},{48,32},{64,80},{80,64},{96,112},{112,96},{1... | collective-permute-start | bytes 688136 | tf_op jit(solution)/shard_map/ppermute | solution.py:62
  24.0 6.2 %collective-permute-start.2 = (f32[2,16,512]{2,1,0:T(8,128)S(1)}, f32[2,16,512]{2,1,0:T(8,128)S(1)}, u32[]{:S(2)}, u32[]{:S(2)}) collective-permute-start(f32[2,16,512]{2,1,0:T(8,128)S(1)} %pad_maximum_fusion.2), channel_id=1, source_target_pairs={{0,32},{16,48},{32,0},{48,16},{64,96},{80,112},{96,64},{112,80},{1... | collective-permute-start | bytes 196616 | tf_op jit(solution)/shard_map/ppermute | solution.py:64
  30.4 10.3 %collective-permute-start.3 = (f32[7,16,512]{2,1,0:T(8,128)S(1)}, f32[7,16,512]{2,1,0:T(8,128)S(1)}, u32[]{:S(2)}, u32[]{:S(2)}) collective-permute-start(f32[7,16,512]{2,1,0:T(8,128)S(1)} %constant_dynamic-update-slice_fusion.6), channel_id=1, source_target_pairs={{0,32},{16,48},{32,0},{48,16},{64,96},{80,112},{96,64},{112,80},{1... | collective-permute-start | bytes 688136 | tf_op jit(solution)/shard_map/ppermute | solution.py:62
  33.6 7.1 %collective-permute-start.4 = (f32[2,16,512]{2,1,0:T(8,128)S(1)}, f32[2,16,512]{2,1,0:T(8,128)S(1)}, u32[]{:S(2)}, u32[]{:S(2)}) collective-permute-start(f32[2,16,512]{2,1,0:T(8,128)S(1)} %pad_maximum_fusion.3), channel_id=1, source_target_pairs={{0,64},{16,80},{32,96},{48,112},{64,0},{80,16},{96,32},{112,48},{1... | collective-permute-start | bytes 196616 | tf_op jit(solution)/shard_map/ppermute | solution.py:64
  40.9 15.9 %collective-permute-start.5 = (f32[7,16,512]{2,1,0:T(8,128)S(1)}, f32[7,16,512]{2,1,0:T(8,128)S(1)}, u32[]{:S(2)}, u32[]{:S(2)}) collective-permute-start(f32[7,16,512]{2,1,0:T(8,128)S(1)} %constant_dynamic-update-slice_fusion.13), channel_id=1, source_target_pairs={{0,64},{16,80},{32,96},{48,112},{64,0},{80,16},{96,32},{112,48},{1... | collective-permute-start | bytes 688136 | tf_op jit(solution)/shard_map/ppermute | solution.py:62
  44.8 10.7 %collective-permute-start.6 = (f32[2,16,512]{2,1,0:T(8,128)S(1)}, f32[2,16,512]{2,1,0:T(8,128)S(1)}, u32[]{:S(2)}, u32[]{:S(2)}) collective-permute-start(f32[2,16,512]{2,1,0:T(8,128)S(1)} %pad_maximum_fusion.4), channel_id=1, source_target_pairs={{0,128},{16,144},{32,160},{48,176},{64,192},{80,208},{96,224},{112... | collective-permute-start | bytes 196616 | tf_op jit(solution)/shard_map/ppermute | solution.py:64
  56.8 47.0 %copy-start.7 = (f32[16,512]{1,0:T(8,128)S(1)}, f32[16,512]{1,0:T(8,128)}, u32[]{:S(2)}) copy-start(f32[16,512]{1,0:T(8,128)} %param.10) | copy-start | bytes 98308
  57.0 15.0 %collective-permute-start.7 = (f32[7,16,512]{2,1,0:T(8,128)S(1)}, f32[7,16,512]{2,1,0:T(8,128)S(1)}, u32[]{:S(2)}, u32[]{:S(2)}) collective-permute-start(f32[7,16,512]{2,1,0:T(8,128)S(1)} %constant_dynamic-update-slice_fusion.20), channel_id=1, source_target_pairs={{0,128},{16,144},{32,160},{48,176},{64,192},{80,208},{96,224},{112... | collective-permute-start | bytes 688136 | tf_op jit(solution)/shard_map/ppermute | solution.py:62
  60.1 7.1 %collective-permute-start.8 = (f32[2,16,512]{2,1,0:T(8,128)S(1)}, f32[2,16,512]{2,1,0:T(8,128)S(1)}, u32[]{:S(2)}, u32[]{:S(2)}) collective-permute-start(f32[2,16,512]{2,1,0:T(8,128)S(1)} %pad_maximum_fusion.5), channel_id=1, source_target_pairs={{0,256},{16,272},{32,288},{48,304},{64,320},{80,336},{96,352},{112... | collective-permute-start | bytes 196616 | tf_op jit(solution)/shard_map/ppermute | solution.py:64
  72.3 14.5 %collective-permute-start.9 = (f32[7,16,512]{2,1,0:T(8,128)S(1)}, f32[7,16,512]{2,1,0:T(8,128)S(1)}, u32[]{:S(2)}, u32[]{:S(2)}) collective-permute-start(f32[7,16,512]{2,1,0:T(8,128)S(1)} %constant_dynamic-update-slice_fusion.27), channel_id=1, source_target_pairs={{0,256},{16,272},{32,288},{48,304},{64,320},{80,336},{96,352},{112... | collective-permute-start | bytes 688136 | tf_op jit(solution)/shard_map/ppermute | solution.py:62
  76.5 10.1 %collective-permute-start.10 = (f32[2,16,512]{2,1,0:T(8,128)S(1)}, f32[2,16,512]{2,1,0:T(8,128)S(1)}, u32[]{:S(2)}, u32[]{:S(2)}) collective-permute-start(f32[2,16,512]{2,1,0:T(8,128)S(1)} %pad_maximum_fusion), channel_id=1, source_target_pairs={{0,512},{16,528},{32,544},{48,560},{64,576},{80,592},{96,608},{112... | collective-permute-start | bytes 196616 | tf_op jit(solution)/shard_map/ppermute | solution.py:64
  79.9 25.3 %copy-start.2 = (f32[128,16,512]{2,0,1:T(8,128)S(1)}, f32[128,16,512]{2,0,1:T(8,128)}, u32[]{:S(2)}) copy-start(f32[128,16,512]{2,0,1:T(8,128)} %copy-done.1) | copy-start | bytes 12582916
  86.9 16.9 %collective-permute-start.11 = (f32[7,16,512]{2,1,0:T(8,128)S(1)}, f32[7,16,512]{2,1,0:T(8,128)S(1)}, u32[]{:S(2)}, u32[]{:S(2)}) collective-permute-start(f32[7,16,512]{2,1,0:T(8,128)S(1)} %constant_dynamic-update-slice_fusion.34), channel_id=1, source_target_pairs={{0,512},{16,528},{32,544},{48,560},{64,576},{80,592},{96,608},{112... | collective-permute-start | bytes 688136 | tf_op jit(solution)/shard_map/ppermute | solution.py:62
  105.2 4.4 %copy-start.3 = (bf16[128,512]{1,0:T(8,128)(2,1)S(1)}, bf16[128,512]{1,0:T(8,128)(2,1)}, u32[]{:S(2)}) copy-start(bf16[128,512]{1,0:T(8,128)(2,1)} %param.9) | copy-start | bytes 393220
  105.2 4.4 %copy-start.4 = (bf16[128,512]{1,0:T(8,128)(2,1)S(1)}, bf16[128,512]{1,0:T(8,128)(2,1)}, u32[]{:S(2)}) copy-start(bf16[128,512]{1,0:T(8,128)(2,1)} %param.6) | copy-start | bytes 393220
  105.2 5.2 %copy-start.5 = (bf16[128,512]{1,0:T(8,128)(2,1)S(1)}, bf16[128,512]{1,0:T(8,128)(2,1)}, u32[]{:S(2)}) copy-start(bf16[128,512]{1,0:T(8,128)(2,1)} %param.8) | copy-start | bytes 393220
  105.2 5.2 %copy-start.6 = (bf16[128,512]{1,0:T(8,128)(2,1)S(1)}, bf16[128,512]{1,0:T(8,128)(2,1)}, u32[]{:S(2)}) copy-start(bf16[128,512]{1,0:T(8,128)(2,1)} %param.7) | copy-start | bytes 393220
  112.5 8.8 %collective-permute-start.12 = (f32[1]{0:T(128)}, f32[1]{0:T(128)}, u32[]{:S(2)}, u32[]{:S(2)}) collective-permute-start(f32[1]{0:T(128)} %bitcast.139), channel_id=1, source_target_pairs={{0,1},{1,0},{2,3},{3,2},{4,5},{5,4},{6,7},{7,6},{8,9},{9,8},{10,11... | collective-permute-start | bytes 20 | tf_op jit(solution)/shard_map/ppermute | solution.py:32
  121.9 9.4 %collective-permute-start.13 = (f32[1]{0:T(128)}, f32[1]{0:T(128)}, u32[]{:S(2)}, u32[]{:S(2)}) collective-permute-start(f32[1]{0:T(128)} %add.523), channel_id=1, source_target_pairs={{0,2},{1,3},{2,0},{3,1},{4,6},{5,7},{6,4},{7,5},{8,10},{9,11},{10,... | collective-permute-start | bytes 20 | tf_op jit(solution)/shard_map/ppermute | solution.py:32
  132.0 13.5 %collective-permute-start.14 = (f32[1]{0:T(128)}, f32[1]{0:T(128)}, u32[]{:S(2)}, u32[]{:S(2)}) collective-permute-start(f32[1]{0:T(128)} %add.524), channel_id=1, source_target_pairs={{0,4},{1,5},{2,6},{3,7},{4,0},{5,1},{6,2},{7,3},{8,12},{9,13},{10,... | collective-permute-start | bytes 20 | tf_op jit(solution)/shard_map/ppermute | solution.py:32
  146.1 5.5 %collective-permute-start.15 = (f32[1]{0:T(128)}, f32[1]{0:T(128)}, u32[]{:S(2)}, u32[]{:S(2)}) collective-permute-start(f32[1]{0:T(128)} %add.525), channel_id=1, source_target_pairs={{0,8},{1,9},{2,10},{3,11},{4,12},{5,13},{6,14},{7,15},{8,0},{9,1},... | collective-permute-start | bytes 20 | tf_op jit(solution)/shard_map/ppermute | solution.py:32

commit v6 on v5

--- a/solution.py
+++ b/solution.py
@@ -104,8 +104,9 @@
     where = jnp.arange(steps, dtype=jnp.float32)[:, None, None]
     rising = jnp.exp(rate * where)
     falling = jnp.exp(-rate * where)
+    whole = jnp.exp(-decay_rate * steps)
 
-    ends = jnp.sum(jnp.exp(-rate * (steps - 1.0 - where)) * source[:, None, :], axis=0)
+    ends = jnp.sum((jnp.exp(-decay_rate * (steps - 1.0))[None] * rising) * source[:, None, :], axis=0)
     heads = mixing * jnp.sum(falling * drive[:, None, :], axis=0)
 
     row = jnp.arange(steps)[:, None]
@@ -118,8 +119,8 @@
     states0 = falling * jnp.dot(lower_tri, climbed, precision=HIGHEST).reshape(rising.shape)
     adjoint0 = rising * jnp.dot(upper_tri, fallen, precision=HIGHEST).reshape(rising.shape)
 
-    grown = jnp.exp(-rate * (where + 1.0))
-    shrunk = jnp.exp(-rate * (steps - where))
+    grown = falling * decay[None]
+    shrunk = rising * whole[None]
     previous0 = jnp.concatenate([jnp.zeros_like(states0[:1]), states0[:-1]], axis=0)
     w_free = jnp.sum(drive[:, None, :] * states0, axis=0)
     w_in = jnp.sum(drive[:, None, :] * grown, axis=0)

time: 155 us -> 150 us (0.968)
  waiting for transfers between devices: 46.1 us -> 39.9 us
  starting transfers between devices: 73.6 us -> 75.3 us
    ppermute x6, waiting for transfers between devices: 19.3 us -> 13.7 us  [fused_scan(): partner = lax.ppermute(group, axis, pairs_of(size))]
    ppermute x6, starting transfers between devices: 20.3 us -> 22 us  [fused_scan(): partner = lax.ppermute(group, axis, pairs_of(size))]
  transfers between devices with their start and end apart: 16 -> 16, of which waited for: 13 -> 13; matrix products, arithmetic and copies ran while one was open for 0% -> 3% of each run, Pallas kernels for 0% -> 0%
where the time goes in v6:
time: 150 us; the launch traced here: 149 us
  starting transfers between devices  75.3 us (50%)
  waiting for transfers between devices  39.9 us (27%)
  other arithmetic  14.3 us (10%)
  matrix products  11.5 us (8%)
  between operations  5.49 us (4%)
  local copies, waits for them, and re-layouts  2.45 us (2%)
    ppermute x4, starting transfers between devices, level_gather(): got.append(lax.ppermute(x, axis, perm))  34 us
    ppermute x5, waiting for transfers between devices, fused_scan(): carry_partner = lax.ppermute(carry, axis, pairs_of(sizes[k + 1]))  23.5 us
    ppermute x6, starting transfers between devices, fused_scan(): partner = lax.ppermute(group, axis, pairs_of(size))  22 us
    ppermute x5, starting transfers between devices, fused_scan(): carry_partner = lax.ppermute(carry, axis, pairs_of(sizes[k + 1]))  17.4 us
    ppermute x6, waiting for transfers between devices, fused_scan(): partner = lax.ppermute(group, axis, pairs_of(size))  13.7 us
    dot_general x1, matrix products, local(): jnp.dot(upper_tri, fallen, precision=HIGHEST).reshape(rising.shape)  8.28 us
    reduce_sum x1, other arithmetic, local(): grad_source = jnp.sum(adjoint, axis=1)  3.4 us
    dot_general x1, matrix products, local(): jnp.dot(lower_tri, climbed, precision=HIGHEST).reshape(rising.shape)  3.21 us
  transfers between devices with their start and end apart: 16, of which 13 were waited for; matrix products, arithmetic and copies ran while one was open for 3% of the time, Pallas kernels for 0%

profile of v6, /device:TPU:126, one launch (start us, length us, event | category | flops | bytes accessed | tf_op | source)
XLA Modules:
  0.0 149.0 jit_solution(18066238191226732366)
XLA Ops:
  4.9 3.2 %fusion.4 = f32[128,16,512]{2,0,1:T(8,128)S(1)} fusion(f32[16,512,128]{2,1,0:T(8,128)S(1)} %bitcast.901, f32[16,512]{1,0:T(8,128)S(1)} %get-tuple-element.89), kind=kOutput, calls=%fused_computation.17 | convolution fusion | flops 1612726272 | bytes 8421376 | tf_op jit(solution)/shard_map/dot_general | solution.py:119
  10.4 8.3 %multiply_reduce_fusion.1 = (f32[16,512]{1,0:T(8,128)S(1)}, f32[16,512]{1,0:T(8,128)S(1)}, f32[16,512]{1,0:T(8,128)S(1)}, f32[16,512]{1,0:T(8,128)S(1)}, f32[16,...) fusion(f32[127,16,512]{2,0,1:T(8,128)S(1)} %bitcast.900, ...), kind=kOutput, calls=%fused_computation.5 | convolution fusion | flops 1631543296 | bytes 17661952 | tf_op jit(solution)/shard_map/dot_general | solution.py:120
  23.3 3.1 %collective-permute-start.2 = (f32[2,16,512]{2,1,0:T(8,128)S(1)}, f32[2,16,512]{2,1,0:T(8,128)S(1)}, u32[]{:S(2)}, u32[]{:S(2)}) collective-permute-start(f32[2,16,512]{2,1,0:T(8,128)S(1)} %pad_maximum_fusion.2), channel_id=1, source_target_pairs={{0,32},{16,48},{32,0},{48,16},{64,96},{80,112},{96,64},{112,80},{1... | collective-permute-start | bytes 196616 | tf_op jit(solution)/shard_map/ppermute | solution.py:64
  26.4 3.0 %collective-permute-done.2 = f32[2,16,512]{2,1,0:T(8,128)S(1)} collective-permute-done((f32[2,16,512]{2,1,0:T(8,128)S(1)}, f32[2,16,512]{2,1,0:T(8,128)S(1)}, u32[]{:S(2)}, u32[]{:S(2)}) %collective-permute-start.2) | collective-permute-done | bytes 65568 | tf_op jit(solution)/shard_map/ppermute | solution.py:64
  29.7 3.1 %collective-permute-start.3 = (f32[7,16,512]{2,1,0:T(8,128)S(1)}, f32[7,16,512]{2,1,0:T(8,128)S(1)}, u32[]{:S(2)}, u32[]{:S(2)}) collective-permute-start(f32[7,16,512]{2,1,0:T(8,128)S(1)} %constant_dynamic-update-slice_fusion.6), channel_id=1, source_target_pairs={{0,32},{16,48},{32,0},{48,16},{64,96},{80,112},{96,64},{112,80},{1... | collective-permute-start | bytes 688136 | tf_op jit(solution)/shard_map/ppermute | solution.py:62
  32.9 3.8 %collective-permute-start.4 = (f32[2,16,512]{2,1,0:T(8,128)S(1)}, f32[2,16,512]{2,1,0:T(8,128)S(1)}, u32[]{:S(2)}, u32[]{:S(2)}) collective-permute-start(f32[2,16,512]{2,1,0:T(8,128)S(1)} %pad_maximum_fusion.3), channel_id=1, source_target_pairs={{0,64},{16,80},{32,96},{48,112},{64,0},{80,16},{96,32},{112,48},{1... | collective-permute-start | bytes 196616 | tf_op jit(solution)/shard_map/ppermute | solution.py:64
  36.7 3.2 %collective-permute-done.4 = f32[2,16,512]{2,1,0:T(8,128)S(1)} collective-permute-done((f32[2,16,512]{2,1,0:T(8,128)S(1)}, f32[2,16,512]{2,1,0:T(8,128)S(1)}, u32[]{:S(2)}, u32[]{:S(2)}) %collective-permute-start.4) | collective-permute-done | bytes 65568 | tf_op jit(solution)/shard_map/ppermute | solution.py:64
  40.2 3.9 %collective-permute-start.5 = (f32[7,16,512]{2,1,0:T(8,128)S(1)}, f32[7,16,512]{2,1,0:T(8,128)S(1)}, u32[]{:S(2)}, u32[]{:S(2)}) collective-permute-start(f32[7,16,512]{2,1,0:T(8,128)S(1)} %constant_dynamic-update-slice_fusion.13), channel_id=1, source_target_pairs={{0,64},{16,80},{32,96},{48,112},{64,0},{80,16},{96,32},{112,48},{1... | collective-permute-start | bytes 688136 | tf_op jit(solution)/shard_map/ppermute | solution.py:62
  44.1 2.9 %collective-permute-start.6 = (f32[2,16,512]{2,1,0:T(8,128)S(1)}, f32[2,16,512]{2,1,0:T(8,128)S(1)}, u32[]{:S(2)}, u32[]{:S(2)}) collective-permute-start(f32[2,16,512]{2,1,0:T(8,128)S(1)} %pad_maximum_fusion.4), channel_id=1, source_target_pairs={{0,128},{16,144},{32,160},{48,176},{64,192},{80,208},{96,224},{112... | collective-permute-start | bytes 196616 | tf_op jit(solution)/shard_map/ppermute | solution.py:64
  47.1 7.7 %collective-permute-done.6 = f32[2,16,512]{2,1,0:T(8,128)S(1)} collective-permute-done((f32[2,16,512]{2,1,0:T(8,128)S(1)}, f32[2,16,512]{2,1,0:T(8,128)S(1)}, u32[]{:S(2)}, u32[]{:S(2)}) %collective-permute-start.6) | collective-permute-done | bytes 65568 | tf_op jit(solution)/shard_map/ppermute | solution.py:64
  56.3 3.0 %collective-permute-start.7 = (f32[7,16,512]{2,1,0:T(8,128)S(1)}, f32[7,16,512]{2,1,0:T(8,128)S(1)}, u32[]{:S(2)}, u32[]{:S(2)}) collective-permute-start(f32[7,16,512]{2,1,0:T(8,128)S(1)} %constant_dynamic-update-slice_fusion.20), channel_id=1, source_target_pairs={{0,128},{16,144},{32,160},{48,176},{64,192},{80,208},{96,224},{112... | collective-permute-start | bytes 688136 | tf_op jit(solution)/shard_map/ppermute | solution.py:62
  59.4 4.2 %collective-permute-start.8 = (f32[2,16,512]{2,1,0:T(8,128)S(1)}, f32[2,16,512]{2,1,0:T(8,128)S(1)}, u32[]{:S(2)}, u32[]{:S(2)}) collective-permute-start(f32[2,16,512]{2,1,0:T(8,128)S(1)} %pad_maximum_fusion.5), channel_id=1, source_target_pairs={{0,256},{16,272},{32,288},{48,304},{64,320},{80,336},{96,352},{112... | collective-permute-start | bytes 196616 | tf_op jit(solution)/shard_map/ppermute | solution.py:64
  63.6 2.8 %collective-permute-done.8 = f32[2,16,512]{2,1,0:T(8,128)S(1)} collective-permute-done((f32[2,16,512]{2,1,0:T(8,128)S(1)}, f32[2,16,512]{2,1,0:T(8,128)S(1)}, u32[]{:S(2)}, u32[]{:S(2)}) %collective-permute-start.8) | collective-permute-done | bytes 65568 | tf_op jit(solution)/shard_map/ppermute | solution.py:64
  66.5 4.8 %collective-permute-done.7 = f32[7,16,512]{2,1,0:T(8,128)S(1)} collective-permute-done((f32[7,16,512]{2,1,0:T(8,128)S(1)}, f32[7,16,512]{2,1,0:T(8,128)S(1)}, u32[]{:S(2)}, u32[]{:S(2)}) %collective-permute-start.7) | collective-permute-done | bytes 229408 | tf_op jit(solution)/shard_map/ppermute | solution.py:62
  71.5 4.3 %collective-permute-start.9 = (f32[7,16,512]{2,1,0:T(8,128)S(1)}, f32[7,16,512]{2,1,0:T(8,128)S(1)}, u32[]{:S(2)}, u32[]{:S(2)}) collective-permute-start(f32[7,16,512]{2,1,0:T(8,128)S(1)} %constant_dynamic-update-slice_fusion.27), channel_id=1, source_target_pairs={{0,256},{16,272},{32,288},{48,304},{64,320},{80,336},{96,352},{112... | collective-permute-start | bytes 688136 | tf_op jit(solution)/shard_map/ppermute | solution.py:62
  76.0 3.3 %collective-permute-start.10 = (f32[2,16,512]{2,1,0:T(8,128)S(1)}, f32[2,16,512]{2,1,0:T(8,128)S(1)}, u32[]{:S(2)}, u32[]{:S(2)}) collective-permute-start(f32[2,16,512]{2,1,0:T(8,128)S(1)} %pad_maximum_fusion), channel_id=1, source_target_pairs={{0,512},{16,528},{32,544},{48,560},{64,576},{80,592},{96,608},{112... | collective-permute-start | bytes 196616 | tf_op jit(solution)/shard_map/ppermute | solution.py:64
  79.3 6.8 %collective-permute-done.10 = f32[2,16,512]{2,1,0:T(8,128)S(1)} collective-permute-done((f32[2,16,512]{2,1,0:T(8,128)S(1)}, f32[2,16,512]{2,1,0:T(8,128)S(1)}, u32[]{:S(2)}, u32[]{:S(2)}) %collective-permute-start.10) | collective-permute-done | bytes 65568 | tf_op jit(solution)/shard_map/ppermute | solution.py:64
  87.9 5.3 %collective-permute-start.11 = (f32[7,16,512]{2,1,0:T(8,128)S(1)}, f32[7,16,512]{2,1,0:T(8,128)S(1)}, u32[]{:S(2)}, u32[]{:S(2)}) collective-permute-start(f32[7,16,512]{2,1,0:T(8,128)S(1)} %constant_dynamic-update-slice_fusion.34), channel_id=1, source_target_pairs={{0,512},{16,528},{32,544},{48,560},{64,576},{80,592},{96,608},{112... | collective-permute-start | bytes 688136 | tf_op jit(solution)/shard_map/ppermute | solution.py:62
  93.3 3.4 %add_reduce_fusion = f32[128,512]{1,0:T(8,128)S(1)} fusion(f32[128,16,512]{2,0,1:T(8,128)} %get-tuple-element.91, f32[16,512]{1,0:T(8,128)S(1)} %select_add_fusion, f32[16,512]{1,0:T(8,128)S(1)} %get-tuple-element.87, f32[16,512]{1,0:T(8,128)S(1)} %copy-done), kind=kLoop, calls=%fused_computation.3 | loop fusion | flops 6225920 | bytes 4554752 | tf_op jit(solution)/shard_map/reduce_sum | solution.py:136
  97.5 6.0 %collective-permute-done.11 = f32[7,16,512]{2,1,0:T(8,128)S(1)} collective-permute-done((f32[7,16,512]{2,1,0:T(8,128)S(1)}, f32[7,16,512]{2,1,0:T(8,128)S(1)}, u32[]{:S(2)}, u32[]{:S(2)}) %collective-permute-start.11) | collective-permute-done | bytes 229408 | tf_op jit(solution)/shard_map/ppermute | solution.py:62
  108.2 8.5 %collective-permute-start.12 = (f32[1]{0:T(128)}, f32[1]{0:T(128)}, u32[]{:S(2)}, u32[]{:S(2)}) collective-permute-start(f32[1]{0:T(128)} %bitcast.139), channel_id=1, source_target_pairs={{0,1},{1,0},{2,3},{3,2},{4,5},{5,4},{6,7},{7,6},{8,9},{9,8},{10,11... | collective-permute-start | bytes 20 | tf_op jit(solution)/shard_map/ppermute | solution.py:32
  117.5 9.1 %collective-permute-start.13 = (f32[1]{0:T(128)}, f32[1]{0:T(128)}, u32[]{:S(2)}, u32[]{:S(2)}) collective-permute-start(f32[1]{0:T(128)} %add.510), channel_id=1, source_target_pairs={{0,2},{1,3},{2,0},{3,1},{4,6},{5,7},{6,4},{7,5},{8,10},{9,11},{10,... | collective-permute-start | bytes 20 | tf_op jit(solution)/shard_map/ppermute | solution.py:32
  127.4 13.2 %collective-permute-start.14 = (f32[1]{0:T(128)}, f32[1]{0:T(128)}, u32[]{:S(2)}, u32[]{:S(2)}) collective-permute-start(f32[1]{0:T(128)} %add.511), channel_id=1, source_target_pairs={{0,4},{1,5},{2,6},{3,7},{4,0},{5,1},{6,2},{7,3},{8,12},{9,13},{10,... | collective-permute-start | bytes 20 | tf_op jit(solution)/shard_map/ppermute | solution.py:32
  141.4 3.2 %collective-permute-start.15 = (f32[1]{0:T(128)}, f32[1]{0:T(128)}, u32[]{:S(2)}, u32[]{:S(2)}) collective-permute-start(f32[1]{0:T(128)} %add.512), channel_id=1, source_target_pairs={{0,8},{1,9},{2,10},{3,11},{4,12},{5,13},{6,14},{7,15},{8,0},{9,1},... | collective-permute-start | bytes 20 | tf_op jit(solution)/shard_map/ppermute | solution.py:32
  (110 shorter events, 23.3 us)
Async XLA Ops:
  8.1 10.7 %copy-start.1 = (f32[128,16,512]{2,0,1:T(8,128)}, f32[128,16,512]{2,0,1:T(8,128)S(1)}, u32[]{:S(2)}) copy-start(f32[128,16,512]{2,0,1:T(8,128)S(1)} %fusion.4) | copy-start | bytes 12582916
  8.1 2.4 %copy-start = (f32[16,512]{1,0:T(8,128)S(1)}, f32[16,512]{1,0:T(8,128)}, u32[]{:S(2)}) copy-start(f32[16,512]{1,0:T(8,128)} %param.11) | copy-start | bytes 98308
  18.8 4.4 %collective-permute-start = (f32[2,16,512]{2,1,0:T(8,128)S(1)}, f32[2,16,512]{2,1,0:T(8,128)S(1)}, u32[]{:S(2)}, u32[]{:S(2)}) collective-permute-start(f32[2,16,512]{2,1,0:T(8,128)S(1)} %pad_maximum_fusion.1), channel_id=1, source_target_pairs={{0,16},{16,0},{32,48},{48,32},{64,80},{80,64},{96,112},{112,96},{1... | collective-permute-start | bytes 196616 | tf_op jit(solution)/shard_map/ppermute | solution.py:51
  20.8 8.7 %collective-permute-start.1 = (f32[7,16,512]{2,1,0:T(8,128)S(1)}, f32[7,16,512]{2,1,0:T(8,128)S(1)}, u32[]{:S(2)}, u32[]{:S(2)}) collective-permute-start(f32[7,16,512]{2,1,0:T(8,128)S(1)} %constant_dynamic-update-slice_fusion), channel_id=1, source_target_pairs={{0,16},{16,0},{32,48},{48,32},{64,80},{80,64},{96,112},{112,96},{1... | collective-permute-start | bytes 688136 | tf_op jit(solution)/shard_map/ppermute | solution.py:62
  23.3 6.2 %collective-permute-start.2 = (f32[2,16,512]{2,1,0:T(8,128)S(1)}, f32[2,16,512]{2,1,0:T(8,128)S(1)}, u32[]{:S(2)}, u32[]{:S(2)}) collective-permute-start(f32[2,16,512]{2,1,0:T(8,128)S(1)} %pad_maximum_fusion.2), channel_id=1, source_target_pairs={{0,32},{16,48},{32,0},{48,16},{64,96},{80,112},{96,64},{112,80},{1... | collective-permute-start | bytes 196616 | tf_op jit(solution)/shard_map/ppermute | solution.py:64
  29.7 10.3 %collective-permute-start.3 = (f32[7,16,512]{2,1,0:T(8,128)S(1)}, f32[7,16,512]{2,1,0:T(8,128)S(1)}, u32[]{:S(2)}, u32[]{:S(2)}) collective-permute-start(f32[7,16,512]{2,1,0:T(8,128)S(1)} %constant_dynamic-update-slice_fusion.6), channel_id=1, source_target_pairs={{0,32},{16,48},{32,0},{48,16},{64,96},{80,112},{96,64},{112,80},{1... | collective-permute-start | bytes 688136 | tf_op jit(solution)/shard_map/ppermute | solution.py:62
  32.9 7.1 %collective-permute-start.4 = (f32[2,16,512]{2,1,0:T(8,128)S(1)}, f32[2,16,512]{2,1,0:T(8,128)S(1)}, u32[]{:S(2)}, u32[]{:S(2)}) collective-permute-start(f32[2,16,512]{2,1,0:T(8,128)S(1)} %pad_maximum_fusion.3), channel_id=1, source_target_pairs={{0,64},{16,80},{32,96},{48,112},{64,0},{80,16},{96,32},{112,48},{1... | collective-permute-start | bytes 196616 | tf_op jit(solution)/shard_map/ppermute | solution.py:64
  40.2 15.9 %collective-permute-start.5 = (f32[7,16,512]{2,1,0:T(8,128)S(1)}, f32[7,16,512]{2,1,0:T(8,128)S(1)}, u32[]{:S(2)}, u32[]{:S(2)}) collective-permute-start(f32[7,16,512]{2,1,0:T(8,128)S(1)} %constant_dynamic-update-slice_fusion.13), channel_id=1, source_target_pairs={{0,64},{16,80},{32,96},{48,112},{64,0},{80,16},{96,32},{112,48},{1... | collective-permute-start | bytes 688136 | tf_op jit(solution)/shard_map/ppermute | solution.py:62
  44.1 10.7 %collective-permute-start.6 = (f32[2,16,512]{2,1,0:T(8,128)S(1)}, f32[2,16,512]{2,1,0:T(8,128)S(1)}, u32[]{:S(2)}, u32[]{:S(2)}) collective-permute-start(f32[2,16,512]{2,1,0:T(8,128)S(1)} %pad_maximum_fusion.4), channel_id=1, source_target_pairs={{0,128},{16,144},{32,160},{48,176},{64,192},{80,208},{96,224},{112... | collective-permute-start | bytes 196616 | tf_op jit(solution)/shard_map/ppermute | solution.py:64
  56.3 15.0 %collective-permute-start.7 = (f32[7,16,512]{2,1,0:T(8,128)S(1)}, f32[7,16,512]{2,1,0:T(8,128)S(1)}, u32[]{:S(2)}, u32[]{:S(2)}) collective-permute-start(f32[7,16,512]{2,1,0:T(8,128)S(1)} %constant_dynamic-update-slice_fusion.20), channel_id=1, source_target_pairs={{0,128},{16,144},{32,160},{48,176},{64,192},{80,208},{96,224},{112... | collective-permute-start | bytes 688136 | tf_op jit(solution)/shard_map/ppermute | solution.py:62
  59.4 7.1 %collective-permute-start.8 = (f32[2,16,512]{2,1,0:T(8,128)S(1)}, f32[2,16,512]{2,1,0:T(8,128)S(1)}, u32[]{:S(2)}, u32[]{:S(2)}) collective-permute-start(f32[2,16,512]{2,1,0:T(8,128)S(1)} %pad_maximum_fusion.5), channel_id=1, source_target_pairs={{0,256},{16,272},{32,288},{48,304},{64,320},{80,336},{96,352},{112... | collective-permute-start | bytes 196616 | tf_op jit(solution)/shard_map/ppermute | solution.py:64
  71.4 25.2 %copy-start.3 = (bf16[128,512]{1,0:T(8,128)(2,1)S(1)}, bf16[128,512]{1,0:T(8,128)(2,1)}, u32[]{:S(2)}) copy-start(bf16[128,512]{1,0:T(8,128)(2,1)} %param.8) | copy-start | bytes 393220
  71.4 25.2 %copy-start.4 = (bf16[128,512]{1,0:T(8,128)(2,1)S(1)}, bf16[128,512]{1,0:T(8,128)(2,1)}, u32[]{:S(2)}) copy-start(bf16[128,512]{1,0:T(8,128)(2,1)} %param.7) | copy-start | bytes 393220
  71.5 16.1 %collective-permute-start.9 = (f32[7,16,512]{2,1,0:T(8,128)S(1)}, f32[7,16,512]{2,1,0:T(8,128)S(1)}, u32[]{:S(2)}, u32[]{:S(2)}) collective-permute-start(f32[7,16,512]{2,1,0:T(8,128)S(1)} %constant_dynamic-update-slice_fusion.27), channel_id=1, source_target_pairs={{0,256},{16,272},{32,288},{48,304},{64,320},{80,336},{96,352},{112... | collective-permute-start | bytes 688136 | tf_op jit(solution)/shard_map/ppermute | solution.py:62
  76.0 10.2 %collective-permute-start.10 = (f32[2,16,512]{2,1,0:T(8,128)S(1)}, f32[2,16,512]{2,1,0:T(8,128)S(1)}, u32[]{:S(2)}, u32[]{:S(2)}) collective-permute-start(f32[2,16,512]{2,1,0:T(8,128)S(1)} %pad_maximum_fusion), channel_id=1, source_target_pairs={{0,512},{16,528},{32,544},{48,560},{64,576},{80,592},{96,608},{112... | collective-permute-start | bytes 196616 | tf_op jit(solution)/shard_map/ppermute | solution.py:64
  79.3 24.2 %copy-start.7 = (f32[16,512]{1,0:T(8,128)S(1)}, f32[16,512]{1,0:T(8,128)}, u32[]{:S(2)}) copy-start(f32[16,512]{1,0:T(8,128)} %param.10) | copy-start | bytes 98308
  87.8 17.0 %copy-start.2 = (f32[128,16,512]{2,0,1:T(8,128)S(1)}, f32[128,16,512]{2,0,1:T(8,128)}, u32[]{:S(2)}) copy-start(f32[128,16,512]{2,0,1:T(8,128)} %copy-done.1) | copy-start | bytes 12582916
  87.9 15.5 %collective-permute-start.11 = (f32[7,16,512]{2,1,0:T(8,128)S(1)}, f32[7,16,512]{2,1,0:T(8,128)S(1)}, u32[]{:S(2)}, u32[]{:S(2)}) collective-permute-start(f32[7,16,512]{2,1,0:T(8,128)S(1)} %constant_dynamic-update-slice_fusion.34), channel_id=1, source_target_pairs={{0,512},{16,528},{32,544},{48,560},{64,576},{80,592},{96,608},{112... | collective-permute-start | bytes 688136 | tf_op jit(solution)/shard_map/ppermute | solution.py:62
  96.7 9.4 %copy-start.5 = (bf16[128,512]{1,0:T(8,128)(2,1)S(1)}, bf16[128,512]{1,0:T(8,128)(2,1)}, u32[]{:S(2)}) copy-start(bf16[128,512]{1,0:T(8,128)(2,1)} %param.9) | copy-start | bytes 393220
  96.7 9.4 %copy-start.6 = (bf16[128,512]{1,0:T(8,128)(2,1)S(1)}, bf16[128,512]{1,0:T(8,128)(2,1)}, u32[]{:S(2)}) copy-start(bf16[128,512]{1,0:T(8,128)(2,1)} %param.6) | copy-start | bytes 393220
  108.2 8.7 %collective-permute-start.12 = (f32[1]{0:T(128)}, f32[1]{0:T(128)}, u32[]{:S(2)}, u32[]{:S(2)}) collective-permute-start(f32[1]{0:T(128)} %bitcast.139), channel_id=1, source_target_pairs={{0,1},{1,0},{2,3},{3,2},{4,5},{5,4},{6,7},{7,6},{8,9},{9,8},{10,11... | collective-permute-start | bytes 20 | tf_op jit(solution)/shard_map/ppermute | solution.py:32
  117.5 9.3 %collective-permute-start.13 = (f32[1]{0:T(128)}, f32[1]{0:T(128)}, u32[]{:S(2)}, u32[]{:S(2)}) collective-permute-start(f32[1]{0:T(128)} %add.510), channel_id=1, source_target_pairs={{0,2},{1,3},{2,0},{3,1},{4,6},{5,7},{6,4},{7,5},{8,10},{9,11},{10,... | collective-permute-start | bytes 20 | tf_op jit(solution)/shard_map/ppermute | solution.py:32
  127.4 13.4 %collective-permute-start.14 = (f32[1]{0:T(128)}, f32[1]{0:T(128)}, u32[]{:S(2)}, u32[]{:S(2)}) collective-permute-start(f32[1]{0:T(128)} %add.511), channel_id=1, source_target_pairs={{0,4},{1,5},{2,6},{3,7},{4,0},{5,1},{6,2},{7,3},{8,12},{9,13},{10,... | collective-permute-start | bytes 20 | tf_op jit(solution)/shard_map/ppermute | solution.py:32
  141.4 5.4 %collective-permute-start.15 = (f32[1]{0:T(128)}, f32[1]{0:T(128)}, u32[]{:S(2)}, u32[]{:S(2)}) collective-permute-start(f32[1]{0:T(128)} %add.512), channel_id=1, source_target_pairs={{0,8},{1,9},{2,10},{3,11},{4,12},{5,13},{6,14},{7,15},{8,0},{9,1},... | collective-permute-start | bytes 20 | tf_op jit(solution)/shard_map/ppermute | solution.py:32

commit v7 on v6

--- a/solution.py
+++ b/solution.py
@@ -8,7 +8,7 @@
 WIDTH = 8192
 MODES = 16
 
-HIGHEST = lax.Precision.HIGHEST
+PRECISION = lax.Precision.HIGH
 CTX_GROUPS = (2, 8, 4)
 CHAN_GROUPS = (2, 2, 2, 2)
 
@@ -116,8 +116,8 @@
     flat = (steps, modes * columns)
     climbed = (rising * source[:, None, :]).reshape(flat)
     fallen = (falling * (mixing[None] * drive[:, None, :])).reshape(flat)
-    states0 = falling * jnp.dot(lower_tri, climbed, precision=HIGHEST).reshape(rising.shape)
-    adjoint0 = rising * jnp.dot(upper_tri, fallen, precision=HIGHEST).reshape(rising.shape)
+    states0 = falling * jnp.dot(lower_tri, climbed, precision=PRECISION).reshape(rising.shape)
+    adjoint0 = rising * jnp.dot(upper_tri, fallen, precision=PRECISION).reshape(rising.shape)
 
     grown = falling * decay[None]
     shrunk = rising * whole[None]

time: 150 us -> 148 us (0.987)
  matrix products: 11.5 us -> 9.47 us
    dot_general x2, matrix products: 11.5 us -> 9.47 us  [the longest x1 7.36 us: local(): jnp.dot(upper_tri, fallen, precision=PRECISION).reshape(rising.shape)]
where the time goes in v7:
time: 148 us; the launch traced here: 147 us
  starting transfers between devices  75.2 us (51%)
  waiting for transfers between devices  40 us (27%)
  other arithmetic  14.3 us (10%)
  matrix products  9.47 us (6%)
  between operations  5.49 us (4%)
  local copies, waits for them, and re-layouts  2.45 us (2%)
    ppermute x4, starting transfers between devices, level_gather(): got.append(lax.ppermute(x, axis, perm))  33.9 us
    ppermute x5, waiting for transfers between devices, fused_scan(): carry_partner = lax.ppermute(carry, axis, pairs_of(sizes[k + 1]))  23.5 us
    ppermute x6, starting transfers between devices, fused_scan(): partner = lax.ppermute(group, axis, pairs_of(size))  22 us
    ppermute x5, starting transfers between devices, fused_scan(): carry_partner = lax.ppermute(carry, axis, pairs_of(sizes[k + 1]))  17.4 us
    ppermute x6, waiting for transfers between devices, fused_scan(): partner = lax.ppermute(group, axis, pairs_of(size))  13.8 us
    dot_general x1, matrix products, local(): jnp.dot(upper_tri, fallen, precision=PRECISION).reshape(rising.shape)  7.36 us
    reduce_sum x1, other arithmetic, local(): grad_source = jnp.sum(adjoint, axis=1)  3.4 us
  transfers between devices with their start and end apart: 16, of which 13 were waited for; matrix products, arithmetic and copies ran while one was open for 3% of the time, Pallas kernels for 0%

profile of v7, /device:TPU:126, one launch (start us, length us, event | category | flops | bytes accessed | tf_op | source)
XLA Modules:
  0.0 146.9 jit_solution(16036845378949027427)
XLA Ops:
  9.3 7.4 %multiply_reduce_fusion.1 = (f32[16,512]{1,0:T(8,128)S(1)}, f32[16,512]{1,0:T(8,128)S(1)}, f32[16,512]{1,0:T(8,128)S(1)}, f32[16,512]{1,0:T(8,128)S(1)}, f32[16,...) fusion(f32[127,16,512]{2,0,1:T(8,128)S(1)} %bitcast.900, ...), kind=kOutput, calls=%fused_computation.5 | convolution fusion | flops 826236928 | bytes 17661952 | tf_op jit(solution)/shard_map/dot_general | solution.py:120
  18.7 2.4 %collective-permute-start.1 = (f32[7,16,512]{2,1,0:T(8,128)S(1)}, f32[7,16,512]{2,1,0:T(8,128)S(1)}, u32[]{:S(2)}, u32[]{:S(2)}) collective-permute-start(f32[7,16,512]{2,1,0:T(8,128)S(1)} %constant_dynamic-update-slice_fusion), channel_id=1, source_target_pairs={{0,16},{16,0},{32,48},{48,32},{64,80},{80,64},{96,112},{112,96},{1... | collective-permute-start | bytes 688136 | tf_op jit(solution)/shard_map/ppermute | solution.py:62
  21.3 3.1 %collective-permute-start.2 = (f32[2,16,512]{2,1,0:T(8,128)S(1)}, f32[2,16,512]{2,1,0:T(8,128)S(1)}, u32[]{:S(2)}, u32[]{:S(2)}) collective-permute-start(f32[2,16,512]{2,1,0:T(8,128)S(1)} %pad_maximum_fusion.2), channel_id=1, source_target_pairs={{0,32},{16,48},{32,0},{48,16},{64,96},{80,112},{96,64},{112,80},{1... | collective-permute-start | bytes 196616 | tf_op jit(solution)/shard_map/ppermute | solution.py:64
  24.4 3.0 %collective-permute-done.2 = f32[2,16,512]{2,1,0:T(8,128)S(1)} collective-permute-done((f32[2,16,512]{2,1,0:T(8,128)S(1)}, f32[2,16,512]{2,1,0:T(8,128)S(1)}, u32[]{:S(2)}, u32[]{:S(2)}) %collective-permute-start.2) | collective-permute-done | bytes 65568 | tf_op jit(solution)/shard_map/ppermute | solution.py:64
  27.6 3.1 %collective-permute-start.3 = (f32[7,16,512]{2,1,0:T(8,128)S(1)}, f32[7,16,512]{2,1,0:T(8,128)S(1)}, u32[]{:S(2)}, u32[]{:S(2)}) collective-permute-start(f32[7,16,512]{2,1,0:T(8,128)S(1)} %constant_dynamic-update-slice_fusion.6), channel_id=1, source_target_pairs={{0,32},{16,48},{32,0},{48,16},{64,96},{80,112},{96,64},{112,80},{1... | collective-permute-start | bytes 688136 | tf_op jit(solution)/shard_map/ppermute | solution.py:62
  30.9 3.8 %collective-permute-start.4 = (f32[2,16,512]{2,1,0:T(8,128)S(1)}, f32[2,16,512]{2,1,0:T(8,128)S(1)}, u32[]{:S(2)}, u32[]{:S(2)}) collective-permute-start(f32[2,16,512]{2,1,0:T(8,128)S(1)} %pad_maximum_fusion.3), channel_id=1, source_target_pairs={{0,64},{16,80},{32,96},{48,112},{64,0},{80,16},{96,32},{112,48},{1... | collective-permute-start | bytes 196616 | tf_op jit(solution)/shard_map/ppermute | solution.py:64
  34.7 3.2 %collective-permute-done.4 = f32[2,16,512]{2,1,0:T(8,128)S(1)} collective-permute-done((f32[2,16,512]{2,1,0:T(8,128)S(1)}, f32[2,16,512]{2,1,0:T(8,128)S(1)}, u32[]{:S(2)}, u32[]{:S(2)}) %collective-permute-start.4) | collective-permute-done | bytes 65568 | tf_op jit(solution)/shard_map/ppermute | solution.py:64
  38.1 3.8 %collective-permute-start.5 = (f32[7,16,512]{2,1,0:T(8,128)S(1)}, f32[7,16,512]{2,1,0:T(8,128)S(1)}, u32[]{:S(2)}, u32[]{:S(2)}) collective-permute-start(f32[7,16,512]{2,1,0:T(8,128)S(1)} %constant_dynamic-update-slice_fusion.13), channel_id=1, source_target_pairs={{0,64},{16,80},{32,96},{48,112},{64,0},{80,16},{96,32},{112,48},{1... | collective-permute-start | bytes 688136 | tf_op jit(solution)/shard_map/ppermute | solution.py:62
  42.1 3.0 %collective-permute-start.6 = (f32[2,16,512]{2,1,0:T(8,128)S(1)}, f32[2,16,512]{2,1,0:T(8,128)S(1)}, u32[]{:S(2)}, u32[]{:S(2)}) collective-permute-start(f32[2,16,512]{2,1,0:T(8,128)S(1)} %pad_maximum_fusion.4), channel_id=1, source_target_pairs={{0,128},{16,144},{32,160},{48,176},{64,192},{80,208},{96,224},{112... | collective-permute-start | bytes 196616 | tf_op jit(solution)/shard_map/ppermute | solution.py:64
  45.1 7.7 %collective-permute-done.6 = f32[2,16,512]{2,1,0:T(8,128)S(1)} collective-permute-done((f32[2,16,512]{2,1,0:T(8,128)S(1)}, f32[2,16,512]{2,1,0:T(8,128)S(1)}, u32[]{:S(2)}, u32[]{:S(2)}) %collective-permute-start.6) | collective-permute-done | bytes 65568 | tf_op jit(solution)/shard_map/ppermute | solution.py:64
  54.3 3.0 %collective-permute-start.7 = (f32[7,16,512]{2,1,0:T(8,128)S(1)}, f32[7,16,512]{2,1,0:T(8,128)S(1)}, u32[]{:S(2)}, u32[]{:S(2)}) collective-permute-start(f32[7,16,512]{2,1,0:T(8,128)S(1)} %constant_dynamic-update-slice_fusion.20), channel_id=1, source_target_pairs={{0,128},{16,144},{32,160},{48,176},{64,192},{80,208},{96,224},{112... | collective-permute-start | bytes 688136 | tf_op jit(solution)/shard_map/ppermute | solution.py:62
  57.4 4.2 %collective-permute-start.8 = (f32[2,16,512]{2,1,0:T(8,128)S(1)}, f32[2,16,512]{2,1,0:T(8,128)S(1)}, u32[]{:S(2)}, u32[]{:S(2)}) collective-permute-start(f32[2,16,512]{2,1,0:T(8,128)S(1)} %pad_maximum_fusion.5), channel_id=1, source_target_pairs={{0,256},{16,272},{32,288},{48,304},{64,320},{80,336},{96,352},{112... | collective-permute-start | bytes 196616 | tf_op jit(solution)/shard_map/ppermute | solution.py:64
  61.6 2.8 %collective-permute-done.8 = f32[2,16,512]{2,1,0:T(8,128)S(1)} collective-permute-done((f32[2,16,512]{2,1,0:T(8,128)S(1)}, f32[2,16,512]{2,1,0:T(8,128)S(1)}, u32[]{:S(2)}, u32[]{:S(2)}) %collective-permute-start.8) | collective-permute-done | bytes 65568 | tf_op jit(solution)/shard_map/ppermute | solution.py:64
  64.4 4.8 %collective-permute-done.7 = f32[7,16,512]{2,1,0:T(8,128)S(1)} collective-permute-done((f32[7,16,512]{2,1,0:T(8,128)S(1)}, f32[7,16,512]{2,1,0:T(8,128)S(1)}, u32[]{:S(2)}, u32[]{:S(2)}) %collective-permute-start.7) | collective-permute-done | bytes 229408 | tf_op jit(solution)/shard_map/ppermute | solution.py:62
  69.5 4.3 %collective-permute-start.9 = (f32[7,16,512]{2,1,0:T(8,128)S(1)}, f32[7,16,512]{2,1,0:T(8,128)S(1)}, u32[]{:S(2)}, u32[]{:S(2)}) collective-permute-start(f32[7,16,512]{2,1,0:T(8,128)S(1)} %constant_dynamic-update-slice_fusion.27), channel_id=1, source_target_pairs={{0,256},{16,272},{32,288},{48,304},{64,320},{80,336},{96,352},{112... | collective-permute-start | bytes 688136 | tf_op jit(solution)/shard_map/ppermute | solution.py:62
  73.9 3.3 %collective-permute-start.10 = (f32[2,16,512]{2,1,0:T(8,128)S(1)}, f32[2,16,512]{2,1,0:T(8,128)S(1)}, u32[]{:S(2)}, u32[]{:S(2)}) collective-permute-start(f32[2,16,512]{2,1,0:T(8,128)S(1)} %pad_maximum_fusion), channel_id=1, source_target_pairs={{0,512},{16,528},{32,544},{48,560},{64,576},{80,592},{96,608},{112... | collective-permute-start | bytes 196616 | tf_op jit(solution)/shard_map/ppermute | solution.py:64
  77.3 6.8 %collective-permute-done.10 = f32[2,16,512]{2,1,0:T(8,128)S(1)} collective-permute-done((f32[2,16,512]{2,1,0:T(8,128)S(1)}, f32[2,16,512]{2,1,0:T(8,128)S(1)}, u32[]{:S(2)}, u32[]{:S(2)}) %collective-permute-start.10) | collective-permute-done | bytes 65568 | tf_op jit(solution)/shard_map/ppermute | solution.py:64
  85.9 5.2 %collective-permute-start.11 = (f32[7,16,512]{2,1,0:T(8,128)S(1)}, f32[7,16,512]{2,1,0:T(8,128)S(1)}, u32[]{:S(2)}, u32[]{:S(2)}) collective-permute-start(f32[7,16,512]{2,1,0:T(8,128)S(1)} %constant_dynamic-update-slice_fusion.34), channel_id=1, source_target_pairs={{0,512},{16,528},{32,544},{48,560},{64,576},{80,592},{96,608},{112... | collective-permute-start | bytes 688136 | tf_op jit(solution)/shard_map/ppermute | solution.py:62
  91.3 3.4 %add_reduce_fusion = f32[128,512]{1,0:T(8,128)S(1)} fusion(f32[128,16,512]{2,0,1:T(8,128)} %get-tuple-element.91, f32[16,512]{1,0:T(8,128)S(1)} %select_add_fusion, f32[16,512]{1,0:T(8,128)S(1)} %get-tuple-element.87, f32[16,512]{1,0:T(8,128)S(1)} %copy-done), kind=kLoop, calls=%fused_computation.3 | loop fusion | flops 6225920 | bytes 4554752 | tf_op jit(solution)/shard_map/reduce_sum | solution.py:136
  95.5 6.0 %collective-permute-done.11 = f32[7,16,512]{2,1,0:T(8,128)S(1)} collective-permute-done((f32[7,16,512]{2,1,0:T(8,128)S(1)}, f32[7,16,512]{2,1,0:T(8,128)S(1)}, u32[]{:S(2)}, u32[]{:S(2)}) %collective-permute-start.11) | collective-permute-done | bytes 229408 | tf_op jit(solution)/shard_map/ppermute | solution.py:62
  106.2 8.4 %collective-permute-start.12 = (f32[1]{0:T(128)}, f32[1]{0:T(128)}, u32[]{:S(2)}, u32[]{:S(2)}) collective-permute-start(f32[1]{0:T(128)} %bitcast.139), channel_id=1, source_target_pairs={{0,1},{1,0},{2,3},{3,2},{4,5},{5,4},{6,7},{7,6},{8,9},{9,8},{10,11... | collective-permute-start | bytes 20 | tf_op jit(solution)/shard_map/ppermute | solution.py:32
  115.4 9.1 %collective-permute-start.13 = (f32[1]{0:T(128)}, f32[1]{0:T(128)}, u32[]{:S(2)}, u32[]{:S(2)}) collective-permute-start(f32[1]{0:T(128)} %add.510), channel_id=1, source_target_pairs={{0,2},{1,3},{2,0},{3,1},{4,6},{5,7},{6,4},{7,5},{8,10},{9,11},{10,... | collective-permute-start | bytes 20 | tf_op jit(solution)/shard_map/ppermute | solution.py:32
  125.4 13.1 %collective-permute-start.14 = (f32[1]{0:T(128)}, f32[1]{0:T(128)}, u32[]{:S(2)}, u32[]{:S(2)}) collective-permute-start(f32[1]{0:T(128)} %add.511), channel_id=1, source_target_pairs={{0,4},{1,5},{2,6},{3,7},{4,0},{5,1},{6,2},{7,3},{8,12},{9,13},{10,... | collective-permute-start | bytes 20 | tf_op jit(solution)/shard_map/ppermute | solution.py:32
  139.3 3.2 %collective-permute-start.15 = (f32[1]{0:T(128)}, f32[1]{0:T(128)}, u32[]{:S(2)}, u32[]{:S(2)}) collective-permute-start(f32[1]{0:T(128)} %add.512), channel_id=1, source_target_pairs={{0,8},{1,9},{2,10},{3,11},{4,12},{5,13},{6,14},{7,15},{8,0},{9,1},... | collective-permute-start | bytes 20 | tf_op jit(solution)/shard_map/ppermute | solution.py:32
  (110 shorter events, 23.0 us)
Async XLA Ops:
  7.0 9.7 %copy-start.1 = (f32[128,16,512]{2,0,1:T(8,128)}, f32[128,16,512]{2,0,1:T(8,128)S(1)}, u32[]{:S(2)}) copy-start(f32[128,16,512]{2,0,1:T(8,128)S(1)} %fusion.4) | copy-start | bytes 12582916
  7.0 2.4 %copy-start = (f32[16,512]{1,0:T(8,128)S(1)}, f32[16,512]{1,0:T(8,128)}, u32[]{:S(2)}) copy-start(f32[16,512]{1,0:T(8,128)} %param.11) | copy-start | bytes 98308
  16.7 4.4 %collective-permute-start = (f32[2,16,512]{2,1,0:T(8,128)S(1)}, f32[2,16,512]{2,1,0:T(8,128)S(1)}, u32[]{:S(2)}, u32[]{:S(2)}) collective-permute-start(f32[2,16,512]{2,1,0:T(8,128)S(1)} %pad_maximum_fusion.1), channel_id=1, source_target_pairs={{0,16},{16,0},{32,48},{48,32},{64,80},{80,64},{96,112},{112,96},{1... | collective-permute-start | bytes 196616 | tf_op jit(solution)/shard_map/ppermute | solution.py:51
  18.7 8.7 %collective-permute-start.1 = (f32[7,16,512]{2,1,0:T(8,128)S(1)}, f32[7,16,512]{2,1,0:T(8,128)S(1)}, u32[]{:S(2)}, u32[]{:S(2)}) collective-permute-start(f32[7,16,512]{2,1,0:T(8,128)S(1)} %constant_dynamic-update-slice_fusion), channel_id=1, source_target_pairs={{0,16},{16,0},{32,48},{48,32},{64,80},{80,64},{96,112},{112,96},{1... | collective-permute-start | bytes 688136 | tf_op jit(solution)/shard_map/ppermute | solution.py:62
  21.3 6.2 %collective-permute-start.2 = (f32[2,16,512]{2,1,0:T(8,128)S(1)}, f32[2,16,512]{2,1,0:T(8,128)S(1)}, u32[]{:S(2)}, u32[]{:S(2)}) collective-permute-start(f32[2,16,512]{2,1,0:T(8,128)S(1)} %pad_maximum_fusion.2), channel_id=1, source_target_pairs={{0,32},{16,48},{32,0},{48,16},{64,96},{80,112},{96,64},{112,80},{1... | collective-permute-start | bytes 196616 | tf_op jit(solution)/shard_map/ppermute | solution.py:64
  27.6 10.3 %collective-permute-start.3 = (f32[7,16,512]{2,1,0:T(8,128)S(1)}, f32[7,16,512]{2,1,0:T(8,128)S(1)}, u32[]{:S(2)}, u32[]{:S(2)}) collective-permute-start(f32[7,16,512]{2,1,0:T(8,128)S(1)} %constant_dynamic-update-slice_fusion.6), channel_id=1, source_target_pairs={{0,32},{16,48},{32,0},{48,16},{64,96},{80,112},{96,64},{112,80},{1... | collective-permute-start | bytes 688136 | tf_op jit(solution)/shard_map/ppermute | solution.py:62
  30.9 7.1 %collective-permute-start.4 = (f32[2,16,512]{2,1,0:T(8,128)S(1)}, f32[2,16,512]{2,1,0:T(8,128)S(1)}, u32[]{:S(2)}, u32[]{:S(2)}) collective-permute-start(f32[2,16,512]{2,1,0:T(8,128)S(1)} %pad_maximum_fusion.3), channel_id=1, source_target_pairs={{0,64},{16,80},{32,96},{48,112},{64,0},{80,16},{96,32},{112,48},{1... | collective-permute-start | bytes 196616 | tf_op jit(solution)/shard_map/ppermute | solution.py:64
  38.1 15.9 %collective-permute-start.5 = (f32[7,16,512]{2,1,0:T(8,128)S(1)}, f32[7,16,512]{2,1,0:T(8,128)S(1)}, u32[]{:S(2)}, u32[]{:S(2)}) collective-permute-start(f32[7,16,512]{2,1,0:T(8,128)S(1)} %constant_dynamic-update-slice_fusion.13), channel_id=1, source_target_pairs={{0,64},{16,80},{32,96},{48,112},{64,0},{80,16},{96,32},{112,48},{1... | collective-permute-start | bytes 688136 | tf_op jit(solution)/shard_map/ppermute | solution.py:62
  42.1 10.7 %collective-permute-start.6 = (f32[2,16,512]{2,1,0:T(8,128)S(1)}, f32[2,16,512]{2,1,0:T(8,128)S(1)}, u32[]{:S(2)}, u32[]{:S(2)}) collective-permute-start(f32[2,16,512]{2,1,0:T(8,128)S(1)} %pad_maximum_fusion.4), channel_id=1, source_target_pairs={{0,128},{16,144},{32,160},{48,176},{64,192},{80,208},{96,224},{112... | collective-permute-start | bytes 196616 | tf_op jit(solution)/shard_map/ppermute | solution.py:64
  54.3 15.0 %collective-permute-start.7 = (f32[7,16,512]{2,1,0:T(8,128)S(1)}, f32[7,16,512]{2,1,0:T(8,128)S(1)}, u32[]{:S(2)}, u32[]{:S(2)}) collective-permute-start(f32[7,16,512]{2,1,0:T(8,128)S(1)} %constant_dynamic-update-slice_fusion.20), channel_id=1, source_target_pairs={{0,128},{16,144},{32,160},{48,176},{64,192},{80,208},{96,224},{112... | collective-permute-start | bytes 688136 | tf_op jit(solution)/shard_map/ppermute | solution.py:62
  57.4 7.1 %collective-permute-start.8 = (f32[2,16,512]{2,1,0:T(8,128)S(1)}, f32[2,16,512]{2,1,0:T(8,128)S(1)}, u32[]{:S(2)}, u32[]{:S(2)}) collective-permute-start(f32[2,16,512]{2,1,0:T(8,128)S(1)} %pad_maximum_fusion.5), channel_id=1, source_target_pairs={{0,256},{16,272},{32,288},{48,304},{64,320},{80,336},{96,352},{112... | collective-permute-start | bytes 196616 | tf_op jit(solution)/shard_map/ppermute | solution.py:64
  69.4 25.2 %copy-start.3 = (bf16[128,512]{1,0:T(8,128)(2,1)S(1)}, bf16[128,512]{1,0:T(8,128)(2,1)}, u32[]{:S(2)}) copy-start(bf16[128,512]{1,0:T(8,128)(2,1)} %param.8) | copy-start | bytes 393220
  69.4 25.2 %copy-start.4 = (bf16[128,512]{1,0:T(8,128)(2,1)S(1)}, bf16[128,512]{1,0:T(8,128)(2,1)}, u32[]{:S(2)}) copy-start(bf16[128,512]{1,0:T(8,128)(2,1)} %param.7) | copy-start | bytes 393220
  69.5 16.2 %collective-permute-start.9 = (f32[7,16,512]{2,1,0:T(8,128)S(1)}, f32[7,16,512]{2,1,0:T(8,128)S(1)}, u32[]{:S(2)}, u32[]{:S(2)}) collective-permute-start(f32[7,16,512]{2,1,0:T(8,128)S(1)} %constant_dynamic-update-slice_fusion.27), channel_id=1, source_target_pairs={{0,256},{16,272},{32,288},{48,304},{64,320},{80,336},{96,352},{112... | collective-permute-start | bytes 688136 | tf_op jit(solution)/shard_map/ppermute | solution.py:62
  73.9 10.2 %collective-permute-start.10 = (f32[2,16,512]{2,1,0:T(8,128)S(1)}, f32[2,16,512]{2,1,0:T(8,128)S(1)}, u32[]{:S(2)}, u32[]{:S(2)}) collective-permute-start(f32[2,16,512]{2,1,0:T(8,128)S(1)} %pad_maximum_fusion), channel_id=1, source_target_pairs={{0,512},{16,528},{32,544},{48,560},{64,576},{80,592},{96,608},{112... | collective-permute-start | bytes 196616 | tf_op jit(solution)/shard_map/ppermute | solution.py:64
  77.3 24.2 %copy-start.7 = (f32[16,512]{1,0:T(8,128)S(1)}, f32[16,512]{1,0:T(8,128)}, u32[]{:S(2)}) copy-start(f32[16,512]{1,0:T(8,128)} %param.10) | copy-start | bytes 98308
  85.8 17.1 %copy-start.2 = (f32[128,16,512]{2,0,1:T(8,128)S(1)}, f32[128,16,512]{2,0,1:T(8,128)}, u32[]{:S(2)}) copy-start(f32[128,16,512]{2,0,1:T(8,128)} %copy-done.1) | copy-start | bytes 12582916
  85.9 15.6 %collective-permute-start.11 = (f32[7,16,512]{2,1,0:T(8,128)S(1)}, f32[7,16,512]{2,1,0:T(8,128)S(1)}, u32[]{:S(2)}, u32[]{:S(2)}) collective-permute-start(f32[7,16,512]{2,1,0:T(8,128)S(1)} %constant_dynamic-update-slice_fusion.34), channel_id=1, source_target_pairs={{0,512},{16,528},{32,544},{48,560},{64,576},{80,592},{96,608},{112... | collective-permute-start | bytes 688136 | tf_op jit(solution)/shard_map/ppermute | solution.py:62
  94.7 9.5 %copy-start.5 = (bf16[128,512]{1,0:T(8,128)(2,1)S(1)}, bf16[128,512]{1,0:T(8,128)(2,1)}, u32[]{:S(2)}) copy-start(bf16[128,512]{1,0:T(8,128)(2,1)} %param.9) | copy-start | bytes 393220
  94.7 9.5 %copy-start.6 = (bf16[128,512]{1,0:T(8,128)(2,1)S(1)}, bf16[128,512]{1,0:T(8,128)(2,1)}, u32[]{:S(2)}) copy-start(bf16[128,512]{1,0:T(8,128)(2,1)} %param.6) | copy-start | bytes 393220
  106.2 8.6 %collective-permute-start.12 = (f32[1]{0:T(128)}, f32[1]{0:T(128)}, u32[]{:S(2)}, u32[]{:S(2)}) collective-permute-start(f32[1]{0:T(128)} %bitcast.139), channel_id=1, source_target_pairs={{0,1},{1,0},{2,3},{3,2},{4,5},{5,4},{6,7},{7,6},{8,9},{9,8},{10,11... | collective-permute-start | bytes 20 | tf_op jit(solution)/shard_map/ppermute | solution.py:32
  115.4 9.3 %collective-permute-start.13 = (f32[1]{0:T(128)}, f32[1]{0:T(128)}, u32[]{:S(2)}, u32[]{:S(2)}) collective-permute-start(f32[1]{0:T(128)} %add.510), channel_id=1, source_target_pairs={{0,2},{1,3},{2,0},{3,1},{4,6},{5,7},{6,4},{7,5},{8,10},{9,11},{10,... | collective-permute-start | bytes 20 | tf_op jit(solution)/shard_map/ppermute | solution.py:32
  125.4 13.3 %collective-permute-start.14 = (f32[1]{0:T(128)}, f32[1]{0:T(128)}, u32[]{:S(2)}, u32[]{:S(2)}) collective-permute-start(f32[1]{0:T(128)} %add.511), channel_id=1, source_target_pairs={{0,4},{1,5},{2,6},{3,7},{4,0},{5,1},{6,2},{7,3},{8,12},{9,13},{10,... | collective-permute-start | bytes 20 | tf_op jit(solution)/shard_map/ppermute | solution.py:32
  139.3 5.4 %collective-permute-start.15 = (f32[1]{0:T(128)}, f32[1]{0:T(128)}, u32[]{:S(2)}, u32[]{:S(2)}) collective-permute-start(f32[1]{0:T(128)} %add.512), channel_id=1, source_target_pairs={{0,8},{1,9},{2,10},{3,11},{4,12},{5,13},{6,14},{7,15},{8,0},{9,1},... | collective-permute-start | bytes 20 | tf_op jit(solution)/shard_map/ppermute | solution.py:32

commit v8 on v7

--- a/solution.py
+++ b/solution.py
@@ -33,7 +33,7 @@
     return got
 
 
-def fused_scan(pieces, rates, steps, axis, n):
+def fused_scan(pieces, rates, steps, axis, n, hide):
     ends, heads, w_in, a_in, a_up, w_free, a_free = pieces
     index = lax.axis_index(axis)
     power = lambda k: jnp.exp(-rates * (steps * jnp.asarray(k).astype(jnp.float32)))
@@ -63,6 +63,9 @@
         if k + 1 < len(sizes):
             carry_partner = lax.ppermute(carry, axis, pairs_of(sizes[k + 1]))
             partner, carry_partner = lax.optimization_barrier((partner, carry_partner))
+        else:
+            hidden = hide(incoming, upper)
+            partner, hidden = lax.optimization_barrier((partner, hidden))
         low_g = jnp.where(high, partner, group)
         high_g = jnp.where(high, group, partner)
         wa_l, wb_l, wc_l, u_l, v_l, zw_l, za_l = low_g
@@ -76,7 +79,7 @@
             zw_l + zw_h + f_l * wa_h,
             za_l + za_h + f_l * wb_h + b_h * wc_l + a_both * (b_h * u_l + f_l * v_h),
         ])
-    return incoming, upper, group[5], group[6]
+    return hidden, group[5], group[6]
 
 
 def group_sum(x, axis, n, groups):
@@ -128,12 +131,21 @@
     a_in = jnp.sum(adjoint0 * falling, axis=0)
     a_up = jnp.sum(shrunk * previous0, axis=0)
     pieces = (ends, heads, w_in, a_in, a_up, w_free, a_free)
-    incoming, upper, grad_mixing, grad_decay = fused_scan(pieces, decay_rate, steps, "ctx", peers)
 
-    states = states0 + grown * incoming[None]
-    adjoint = adjoint0 + shrunk * upper[None]
-    mixed = jnp.sum(mixing[None] * states, axis=1)
-    grad_source = jnp.sum(adjoint, axis=1)
+    def finish(incoming, upper):
+        states = states0 + grown * incoming[None]
+        adjoint = adjoint0 + shrunk * upper[None]
+        mixed = jnp.sum(mixing[None] * states, axis=1)
+        grad_source = jnp.sum(adjoint, axis=1)
+        return (
+            (query * mixed).astype(jnp.bfloat16),
+            (upstream * mixed).astype(jnp.bfloat16),
+            (grad_source * values).astype(jnp.bfloat16),
+            (grad_source * keyed).astype(jnp.bfloat16),
+        )
+
+    outs, grad_mixing, grad_decay = fused_scan(pieces, decay_rate, steps, "ctx", peers, finish)
+    output, grad_query, grad_key, grad_value = outs
 
     raw_residue = grad_mixing * norm_factor
     raw_lograte = decay_rate * (
@@ -147,10 +159,6 @@
     at = lax.axis_index("ctx") * width
     own_residue = lax.dynamic_slice_in_dim(raw_residue, at, width, axis=1)
     own_lograte = lax.dynamic_slice_in_dim(raw_lograte, at, width, axis=1)
-    output = (query * mixed).astype(jnp.bfloat16)
-    grad_query = (upstream * mixed).astype(jnp.bfloat16)
-    grad_key = (grad_source * values).astype(jnp.bfloat16)
-    grad_value = (grad_source * keyed).astype(jnp.bfloat16)
     return (output, grad_query, grad_key, grad_value, own_residue * scale, own_lograte * scale)
 
 

time: 148 us -> 145 us (0.980)
  waiting for transfers between devices: 40 us -> 37.9 us
    ppermute x6, waiting for transfers between devices: 13.8 us -> 11.7 us  [fused_scan(): partner = lax.ppermute(group, axis, pairs_of(size))]
  transfers between devices with their start and end apart: 16 -> 16, of which waited for: 13 -> 13; matrix products, arithmetic and copies ran while one was open for 3% -> 4% of each run, Pallas kernels for 0% -> 0%
where the time goes in v8:
time: 145 us
  starting transfers between devices  74.9 us (52%)
  waiting for transfers between devices  37.9 us (26%)
  other arithmetic  14.3 us (10%)
  matrix products  9.47 us (7%)
  between operations  5.46 us (4%)
  local copies, waits for them, and re-layouts  2.45 us (2%)
    ppermute x4, starting transfers between devices, level_gather(): got.append(lax.ppermute(x, axis, perm))  33.9 us
    ppermute x5, waiting for transfers between devices, fused_scan(): carry_partner = lax.ppermute(carry, axis, pairs_of(sizes[k + 1]))  23.5 us
    ppermute x6, starting transfers between devices, fused_scan(): partner = lax.ppermute(group, axis, pairs_of(size))  21.7 us
    ppermute x5, starting transfers between devices, fused_scan(): carry_partner = lax.ppermute(carry, axis, pairs_of(sizes[k + 1]))  17.4 us
    ppermute x6, waiting for transfers between devices, fused_scan(): partner = lax.ppermute(group, axis, pairs_of(size))  11.7 us
    dot_general x1, matrix products, local(): jnp.dot(upper_tri, fallen, precision=PRECISION).reshape(rising.shape)  7.36 us
    reduce_sum x1, other arithmetic, finish(): mixed = jnp.sum(mixing[None] * states, axis=1)  3.47 us
  transfers between devices with their start and end apart: 16, of which 13 were waited for; matrix products, arithmetic and copies ran while one was open for 4% of the time, Pallas kernels for 0%

profile of v8, /device:TPU:126, one launch (start us, length us, event | category | flops | bytes accessed | tf_op | source)
XLA Modules:
  0.0 144.5 jit_solution(732062954568828312)
XLA Ops:
  9.3 7.4 %multiply_reduce_fusion.3 = (f32[16,512]{1,0:T(8,128)S(1)}, f32[16,512]{1,0:T(8,128)S(1)}, f32[16,512]{1,0:T(8,128)S(1)}, f32[16,512]{1,0:T(8,128)S(1)}, f32[16,...) fusion(f32[127,16,512]{2,0,1:T(8,128)S(1)} %bitcast.900, ...), kind=kOutput, calls=%fused_computation.7 | convolution fusion | flops 826236928 | bytes 17661952 | tf_op jit(solution)/shard_map/dot_general | solution.py:123
  18.7 2.4 %collective-permute-start = (f32[7,16,512]{2,1,0:T(8,128)S(1)}, f32[7,16,512]{2,1,0:T(8,128)S(1)}, u32[]{:S(2)}, u32[]{:S(2)}) collective-permute-start(f32[7,16,512]{2,1,0:T(8,128)S(1)} %constant_dynamic-update-slice_fusion), channel_id=1, source_target_pairs={{0,16},{16,0},{32,48},{48,32},{64,80},{80,64},{96,112},{112,96},{1... | collective-permute-start | bytes 688136 | tf_op jit(solution)/shard_map/ppermute | solution.py:62
  21.3 3.1 %collective-permute-start.2 = (f32[2,16,512]{2,1,0:T(8,128)S(1)}, f32[2,16,512]{2,1,0:T(8,128)S(1)}, u32[]{:S(2)}, u32[]{:S(2)}) collective-permute-start(f32[2,16,512]{2,1,0:T(8,128)S(1)} %pad_maximum_fusion.2), channel_id=1, source_target_pairs={{0,32},{16,48},{32,0},{48,16},{64,96},{80,112},{96,64},{112,80},{1... | collective-permute-start | bytes 196616 | tf_op jit(solution)/shard_map/ppermute | solution.py:64
  24.4 3.0 %collective-permute-done.2 = f32[2,16,512]{2,1,0:T(8,128)S(1)} collective-permute-done((f32[2,16,512]{2,1,0:T(8,128)S(1)}, f32[2,16,512]{2,1,0:T(8,128)S(1)}, u32[]{:S(2)}, u32[]{:S(2)}) %collective-permute-start.2) | collective-permute-done | bytes 65568 | tf_op jit(solution)/shard_map/ppermute | solution.py:64
  27.6 3.1 %collective-permute-start.3 = (f32[7,16,512]{2,1,0:T(8,128)S(1)}, f32[7,16,512]{2,1,0:T(8,128)S(1)}, u32[]{:S(2)}, u32[]{:S(2)}) collective-permute-start(f32[7,16,512]{2,1,0:T(8,128)S(1)} %constant_dynamic-update-slice_fusion.6), channel_id=1, source_target_pairs={{0,32},{16,48},{32,0},{48,16},{64,96},{80,112},{96,64},{112,80},{1... | collective-permute-start | bytes 688136 | tf_op jit(solution)/shard_map/ppermute | solution.py:62
  30.9 3.8 %collective-permute-start.4 = (f32[2,16,512]{2,1,0:T(8,128)S(1)}, f32[2,16,512]{2,1,0:T(8,128)S(1)}, u32[]{:S(2)}, u32[]{:S(2)}) collective-permute-start(f32[2,16,512]{2,1,0:T(8,128)S(1)} %pad_maximum_fusion.3), channel_id=1, source_target_pairs={{0,64},{16,80},{32,96},{48,112},{64,0},{80,16},{96,32},{112,48},{1... | collective-permute-start | bytes 196616 | tf_op jit(solution)/shard_map/ppermute | solution.py:64
  34.7 3.2 %collective-permute-done.4 = f32[2,16,512]{2,1,0:T(8,128)S(1)} collective-permute-done((f32[2,16,512]{2,1,0:T(8,128)S(1)}, f32[2,16,512]{2,1,0:T(8,128)S(1)}, u32[]{:S(2)}, u32[]{:S(2)}) %collective-permute-start.4) | collective-permute-done | bytes 65568 | tf_op jit(solution)/shard_map/ppermute | solution.py:64
  38.1 3.8 %collective-permute-start.5 = (f32[7,16,512]{2,1,0:T(8,128)S(1)}, f32[7,16,512]{2,1,0:T(8,128)S(1)}, u32[]{:S(2)}, u32[]{:S(2)}) collective-permute-start(f32[7,16,512]{2,1,0:T(8,128)S(1)} %constant_dynamic-update-slice_fusion.13), channel_id=1, source_target_pairs={{0,64},{16,80},{32,96},{48,112},{64,0},{80,16},{96,32},{112,48},{1... | collective-permute-start | bytes 688136 | tf_op jit(solution)/shard_map/ppermute | solution.py:62
  42.1 3.0 %collective-permute-start.6 = (f32[2,16,512]{2,1,0:T(8,128)S(1)}, f32[2,16,512]{2,1,0:T(8,128)S(1)}, u32[]{:S(2)}, u32[]{:S(2)}) collective-permute-start(f32[2,16,512]{2,1,0:T(8,128)S(1)} %pad_maximum_fusion.4), channel_id=1, source_target_pairs={{0,128},{16,144},{32,160},{48,176},{64,192},{80,208},{96,224},{112... | collective-permute-start | bytes 196616 | tf_op jit(solution)/shard_map/ppermute | solution.py:64
  45.1 7.7 %collective-permute-done.6 = f32[2,16,512]{2,1,0:T(8,128)S(1)} collective-permute-done((f32[2,16,512]{2,1,0:T(8,128)S(1)}, f32[2,16,512]{2,1,0:T(8,128)S(1)}, u32[]{:S(2)}, u32[]{:S(2)}) %collective-permute-start.6) | collective-permute-done | bytes 65568 | tf_op jit(solution)/shard_map/ppermute | solution.py:64
  54.3 3.0 %collective-permute-start.7 = (f32[7,16,512]{2,1,0:T(8,128)S(1)}, f32[7,16,512]{2,1,0:T(8,128)S(1)}, u32[]{:S(2)}, u32[]{:S(2)}) collective-permute-start(f32[7,16,512]{2,1,0:T(8,128)S(1)} %constant_dynamic-update-slice_fusion.20), channel_id=1, source_target_pairs={{0,128},{16,144},{32,160},{48,176},{64,192},{80,208},{96,224},{112... | collective-permute-start | bytes 688136 | tf_op jit(solution)/shard_map/ppermute | solution.py:62
  57.4 4.2 %collective-permute-start.8 = (f32[2,16,512]{2,1,0:T(8,128)S(1)}, f32[2,16,512]{2,1,0:T(8,128)S(1)}, u32[]{:S(2)}, u32[]{:S(2)}) collective-permute-start(f32[2,16,512]{2,1,0:T(8,128)S(1)} %pad_maximum_fusion.5), channel_id=1, source_target_pairs={{0,256},{16,272},{32,288},{48,304},{64,320},{80,336},{96,352},{112... | collective-permute-start | bytes 196616 | tf_op jit(solution)/shard_map/ppermute | solution.py:64
  61.6 2.8 %collective-permute-done.8 = f32[2,16,512]{2,1,0:T(8,128)S(1)} collective-permute-done((f32[2,16,512]{2,1,0:T(8,128)S(1)}, f32[2,16,512]{2,1,0:T(8,128)S(1)}, u32[]{:S(2)}, u32[]{:S(2)}) %collective-permute-start.8) | collective-permute-done | bytes 65568 | tf_op jit(solution)/shard_map/ppermute | solution.py:64
  64.4 4.8 %collective-permute-done.7 = f32[7,16,512]{2,1,0:T(8,128)S(1)} collective-permute-done((f32[7,16,512]{2,1,0:T(8,128)S(1)}, f32[7,16,512]{2,1,0:T(8,128)S(1)}, u32[]{:S(2)}, u32[]{:S(2)}) %collective-permute-start.7) | collective-permute-done | bytes 229408 | tf_op jit(solution)/shard_map/ppermute | solution.py:62
  69.5 4.3 %collective-permute-start.9 = (f32[7,16,512]{2,1,0:T(8,128)S(1)}, f32[7,16,512]{2,1,0:T(8,128)S(1)}, u32[]{:S(2)}, u32[]{:S(2)}) collective-permute-start(f32[7,16,512]{2,1,0:T(8,128)S(1)} %constant_dynamic-update-slice_fusion.27), channel_id=1, source_target_pairs={{0,256},{16,272},{32,288},{48,304},{64,320},{80,336},{96,352},{112... | collective-permute-start | bytes 688136 | tf_op jit(solution)/shard_map/ppermute | solution.py:62
  73.9 3.3 %collective-permute-start.10 = (f32[2,16,512]{2,1,0:T(8,128)S(1)}, f32[2,16,512]{2,1,0:T(8,128)S(1)}, u32[]{:S(2)}, u32[]{:S(2)}) collective-permute-start(f32[2,16,512]{2,1,0:T(8,128)S(1)} %pad_maximum_fusion), channel_id=1, source_target_pairs={{0,512},{16,528},{32,544},{48,560},{64,576},{80,592},{96,608},{112... | collective-permute-start | bytes 196616 | tf_op jit(solution)/shard_map/ppermute | solution.py:64
  77.3 6.8 %collective-permute-done.10 = f32[2,16,512]{2,1,0:T(8,128)S(1)} collective-permute-done((f32[2,16,512]{2,1,0:T(8,128)S(1)}, f32[2,16,512]{2,1,0:T(8,128)S(1)}, u32[]{:S(2)}, u32[]{:S(2)}) %collective-permute-start.10) | collective-permute-done | bytes 65568 | tf_op jit(solution)/shard_map/ppermute | solution.py:64
  85.9 5.0 %collective-permute-start.11 = (f32[7,16,512]{2,1,0:T(8,128)S(1)}, f32[7,16,512]{2,1,0:T(8,128)S(1)}, u32[]{:S(2)}, u32[]{:S(2)}) collective-permute-start(f32[7,16,512]{2,1,0:T(8,128)S(1)} %constant_dynamic-update-slice_fusion.34), channel_id=1, source_target_pairs={{0,512},{16,528},{32,544},{48,560},{64,576},{80,592},{96,608},{112... | collective-permute-start | bytes 688136 | tf_op jit(solution)/shard_map/ppermute | solution.py:62
  91.0 3.5 %multiply_reduce_fusion = f32[128,512]{1,0:T(8,128)S(1)} fusion(f32[128,16,512]{2,0,1:T(8,128)} %copy-done.1, f32[16,512]{1,0:T(8,128)S(1)} %get-tuple-element.57, f32[16,512]{1,0:T(8,128)S(1)} %get-tuple-element.98, f32[16,512]{1,0:T(8,128)S(1)} %get-tuple-element.99, f32[16,512]{1,0:T(8,128)S(1)} %get-tuple-element.100), kind=kLoop, calls=%fused_computation.4 | loop fusion | flops 6225920 | bytes 4587520 | tf_op jit(solution)/shard_map/reduce_sum | solution.py:138
  97.2 4.0 %collective-permute-done.11 = f32[7,16,512]{2,1,0:T(8,128)S(1)} collective-permute-done((f32[7,16,512]{2,1,0:T(8,128)S(1)}, f32[7,16,512]{2,1,0:T(8,128)S(1)}, u32[]{:S(2)}, u32[]{:S(2)}) %collective-permute-start.11) | collective-permute-done | bytes 229408 | tf_op jit(solution)/shard_map/ppermute | solution.py:62
  103.9 8.4 %collective-permute-start.12 = (f32[1]{0:T(128)}, f32[1]{0:T(128)}, u32[]{:S(2)}, u32[]{:S(2)}) collective-permute-start(f32[1]{0:T(128)} %bitcast.139), channel_id=1, source_target_pairs={{0,1},{1,0},{2,3},{3,2},{4,5},{5,4},{6,7},{7,6},{8,9},{9,8},{10,11... | collective-permute-start | bytes 20 | tf_op jit(solution)/shard_map/ppermute | solution.py:32
  113.1 9.1 %collective-permute-start.13 = (f32[1]{0:T(128)}, f32[1]{0:T(128)}, u32[]{:S(2)}, u32[]{:S(2)}) collective-permute-start(f32[1]{0:T(128)} %add.510), channel_id=1, source_target_pairs={{0,2},{1,3},{2,0},{3,1},{4,6},{5,7},{6,4},{7,5},{8,10},{9,11},{10,... | collective-permute-start | bytes 20 | tf_op jit(solution)/shard_map/ppermute | solution.py:32
  123.0 13.1 %collective-permute-start.14 = (f32[1]{0:T(128)}, f32[1]{0:T(128)}, u32[]{:S(2)}, u32[]{:S(2)}) collective-permute-start(f32[1]{0:T(128)} %add.511), channel_id=1, source_target_pairs={{0,4},{1,5},{2,6},{3,7},{4,0},{5,1},{6,2},{7,3},{8,12},{9,13},{10,... | collective-permute-start | bytes 20 | tf_op jit(solution)/shard_map/ppermute | solution.py:32
  137.0 3.2 %collective-permute-start.15 = (f32[1]{0:T(128)}, f32[1]{0:T(128)}, u32[]{:S(2)}, u32[]{:S(2)}) collective-permute-start(f32[1]{0:T(128)} %add.512), channel_id=1, source_target_pairs={{0,8},{1,9},{2,10},{3,11},{4,12},{5,13},{6,14},{7,15},{8,0},{9,1},... | collective-permute-start | bytes 20 | tf_op jit(solution)/shard_map/ppermute | solution.py:32
  (111 shorter events, 22.9 us)
Async XLA Ops:
  7.0 9.7 %copy-start.1 = (f32[128,16,512]{2,0,1:T(8,128)}, f32[128,16,512]{2,0,1:T(8,128)S(1)}, u32[]{:S(2)}) copy-start(f32[128,16,512]{2,0,1:T(8,128)S(1)} %fusion.3) | copy-start | bytes 12582916
  7.0 2.4 %copy-start = (f32[16,512]{1,0:T(8,128)S(1)}, f32[16,512]{1,0:T(8,128)}, u32[]{:S(2)}) copy-start(f32[16,512]{1,0:T(8,128)} %param.11) | copy-start | bytes 98308
  16.7 4.4 %collective-permute-start.1 = (f32[2,16,512]{2,1,0:T(8,128)S(1)}, f32[2,16,512]{2,1,0:T(8,128)S(1)}, u32[]{:S(2)}, u32[]{:S(2)}) collective-permute-start(f32[2,16,512]{2,1,0:T(8,128)S(1)} %pad_maximum_fusion.1), channel_id=1, source_target_pairs={{0,16},{16,0},{32,48},{48,32},{64,80},{80,64},{96,112},{112,96},{1... | collective-permute-start | bytes 196616 | tf_op jit(solution)/shard_map/ppermute | solution.py:51
  18.7 8.7 %collective-permute-start = (f32[7,16,512]{2,1,0:T(8,128)S(1)}, f32[7,16,512]{2,1,0:T(8,128)S(1)}, u32[]{:S(2)}, u32[]{:S(2)}) collective-permute-start(f32[7,16,512]{2,1,0:T(8,128)S(1)} %constant_dynamic-update-slice_fusion), channel_id=1, source_target_pairs={{0,16},{16,0},{32,48},{48,32},{64,80},{80,64},{96,112},{112,96},{1... | collective-permute-start | bytes 688136 | tf_op jit(solution)/shard_map/ppermute | solution.py:62
  21.3 6.2 %collective-permute-start.2 = (f32[2,16,512]{2,1,0:T(8,128)S(1)}, f32[2,16,512]{2,1,0:T(8,128)S(1)}, u32[]{:S(2)}, u32[]{:S(2)}) collective-permute-start(f32[2,16,512]{2,1,0:T(8,128)S(1)} %pad_maximum_fusion.2), channel_id=1, source_target_pairs={{0,32},{16,48},{32,0},{48,16},{64,96},{80,112},{96,64},{112,80},{1... | collective-permute-start | bytes 196616 | tf_op jit(solution)/shard_map/ppermute | solution.py:64
  27.6 10.3 %collective-permute-start.3 = (f32[7,16,512]{2,1,0:T(8,128)S(1)}, f32[7,16,512]{2,1,0:T(8,128)S(1)}, u32[]{:S(2)}, u32[]{:S(2)}) collective-permute-start(f32[7,16,512]{2,1,0:T(8,128)S(1)} %constant_dynamic-update-slice_fusion.6), channel_id=1, source_target_pairs={{0,32},{16,48},{32,0},{48,16},{64,96},{80,112},{96,64},{112,80},{1... | collective-permute-start | bytes 688136 | tf_op jit(solution)/shard_map/ppermute | solution.py:62
  30.9 7.1 %collective-permute-start.4 = (f32[2,16,512]{2,1,0:T(8,128)S(1)}, f32[2,16,512]{2,1,0:T(8,128)S(1)}, u32[]{:S(2)}, u32[]{:S(2)}) collective-permute-start(f32[2,16,512]{2,1,0:T(8,128)S(1)} %pad_maximum_fusion.3), channel_id=1, source_target_pairs={{0,64},{16,80},{32,96},{48,112},{64,0},{80,16},{96,32},{112,48},{1... | collective-permute-start | bytes 196616 | tf_op jit(solution)/shard_map/ppermute | solution.py:64
  38.1 15.9 %collective-permute-start.5 = (f32[7,16,512]{2,1,0:T(8,128)S(1)}, f32[7,16,512]{2,1,0:T(8,128)S(1)}, u32[]{:S(2)}, u32[]{:S(2)}) collective-permute-start(f32[7,16,512]{2,1,0:T(8,128)S(1)} %constant_dynamic-update-slice_fusion.13), channel_id=1, source_target_pairs={{0,64},{16,80},{32,96},{48,112},{64,0},{80,16},{96,32},{112,48},{1... | collective-permute-start | bytes 688136 | tf_op jit(solution)/shard_map/ppermute | solution.py:62
  42.1 10.7 %collective-permute-start.6 = (f32[2,16,512]{2,1,0:T(8,128)S(1)}, f32[2,16,512]{2,1,0:T(8,128)S(1)}, u32[]{:S(2)}, u32[]{:S(2)}) collective-permute-start(f32[2,16,512]{2,1,0:T(8,128)S(1)} %pad_maximum_fusion.4), channel_id=1, source_target_pairs={{0,128},{16,144},{32,160},{48,176},{64,192},{80,208},{96,224},{112... | collective-permute-start | bytes 196616 | tf_op jit(solution)/shard_map/ppermute | solution.py:64
  54.3 15.0 %collective-permute-start.7 = (f32[7,16,512]{2,1,0:T(8,128)S(1)}, f32[7,16,512]{2,1,0:T(8,128)S(1)}, u32[]{:S(2)}, u32[]{:S(2)}) collective-permute-start(f32[7,16,512]{2,1,0:T(8,128)S(1)} %constant_dynamic-update-slice_fusion.20), channel_id=1, source_target_pairs={{0,128},{16,144},{32,160},{48,176},{64,192},{80,208},{96,224},{112... | collective-permute-start | bytes 688136 | tf_op jit(solution)/shard_map/ppermute | solution.py:62
  57.4 7.1 %collective-permute-start.8 = (f32[2,16,512]{2,1,0:T(8,128)S(1)}, f32[2,16,512]{2,1,0:T(8,128)S(1)}, u32[]{:S(2)}, u32[]{:S(2)}) collective-permute-start(f32[2,16,512]{2,1,0:T(8,128)S(1)} %pad_maximum_fusion.5), channel_id=1, source_target_pairs={{0,256},{16,272},{32,288},{48,304},{64,320},{80,336},{96,352},{112... | collective-permute-start | bytes 196616 | tf_op jit(solution)/shard_map/ppermute | solution.py:64
  69.5 25.0 %copy-start.3 = (bf16[128,512]{1,0:T(8,128)(2,1)S(1)}, bf16[128,512]{1,0:T(8,128)(2,1)}, u32[]{:S(2)}) copy-start(bf16[128,512]{1,0:T(8,128)(2,1)} %param.6) | copy-start | bytes 393220
  69.5 25.0 %copy-start.4 = (bf16[128,512]{1,0:T(8,128)(2,1)S(1)}, bf16[128,512]{1,0:T(8,128)(2,1)}, u32[]{:S(2)}) copy-start(bf16[128,512]{1,0:T(8,128)(2,1)} %param.9) | copy-start | bytes 393220
  69.5 16.2 %collective-permute-start.9 = (f32[7,16,512]{2,1,0:T(8,128)S(1)}, f32[7,16,512]{2,1,0:T(8,128)S(1)}, u32[]{:S(2)}, u32[]{:S(2)}) collective-permute-start(f32[7,16,512]{2,1,0:T(8,128)S(1)} %constant_dynamic-update-slice_fusion.27), channel_id=1, source_target_pairs={{0,256},{16,272},{32,288},{48,304},{64,320},{80,336},{96,352},{112... | collective-permute-start | bytes 688136 | tf_op jit(solution)/shard_map/ppermute | solution.py:62
  73.9 10.2 %collective-permute-start.10 = (f32[2,16,512]{2,1,0:T(8,128)S(1)}, f32[2,16,512]{2,1,0:T(8,128)S(1)}, u32[]{:S(2)}, u32[]{:S(2)}) collective-permute-start(f32[2,16,512]{2,1,0:T(8,128)S(1)} %pad_maximum_fusion), channel_id=1, source_target_pairs={{0,512},{16,528},{32,544},{48,560},{64,576},{80,592},{96,608},{112... | collective-permute-start | bytes 196616 | tf_op jit(solution)/shard_map/ppermute | solution.py:64
  77.3 18.0 %copy-start.2 = (f32[128,16,512]{2,0,1:T(8,128)S(1)}, f32[128,16,512]{2,0,1:T(8,128)}, u32[]{:S(2)}) copy-start(f32[128,16,512]{2,0,1:T(8,128)} %get-tuple-element.101) | copy-start | bytes 12582916
  85.9 15.3 %collective-permute-start.11 = (f32[7,16,512]{2,1,0:T(8,128)S(1)}, f32[7,16,512]{2,1,0:T(8,128)S(1)}, u32[]{:S(2)}, u32[]{:S(2)}) collective-permute-start(f32[7,16,512]{2,1,0:T(8,128)S(1)} %constant_dynamic-update-slice_fusion.34), channel_id=1, source_target_pairs={{0,512},{16,528},{32,544},{48,560},{64,576},{80,592},{96,608},{112... | collective-permute-start | bytes 688136 | tf_op jit(solution)/shard_map/ppermute | solution.py:62
  91.0 5.5 %copy-start.5 = (bf16[128,512]{1,0:T(8,128)(2,1)S(1)}, bf16[128,512]{1,0:T(8,128)(2,1)}, u32[]{:S(2)}) copy-start(bf16[128,512]{1,0:T(8,128)(2,1)} %param.8) | copy-start | bytes 393220
  91.0 5.5 %copy-start.6 = (bf16[128,512]{1,0:T(8,128)(2,1)S(1)}, bf16[128,512]{1,0:T(8,128)(2,1)}, u32[]{:S(2)}) copy-start(bf16[128,512]{1,0:T(8,128)(2,1)} %param.7) | copy-start | bytes 393220
  94.5 6.8 %copy-start.7 = (f32[16,512]{1,0:T(8,128)S(1)}, f32[16,512]{1,0:T(8,128)}, u32[]{:S(2)}) copy-start(f32[16,512]{1,0:T(8,128)} %param.10) | copy-start | bytes 98308
  103.9 8.6 %collective-permute-start.12 = (f32[1]{0:T(128)}, f32[1]{0:T(128)}, u32[]{:S(2)}, u32[]{:S(2)}) collective-permute-start(f32[1]{0:T(128)} %bitcast.139), channel_id=1, source_target_pairs={{0,1},{1,0},{2,3},{3,2},{4,5},{5,4},{6,7},{7,6},{8,9},{9,8},{10,11... | collective-permute-start | bytes 20 | tf_op jit(solution)/shard_map/ppermute | solution.py:32
  113.1 9.3 %collective-permute-start.13 = (f32[1]{0:T(128)}, f32[1]{0:T(128)}, u32[]{:S(2)}, u32[]{:S(2)}) collective-permute-start(f32[1]{0:T(128)} %add.510), channel_id=1, source_target_pairs={{0,2},{1,3},{2,0},{3,1},{4,6},{5,7},{6,4},{7,5},{8,10},{9,11},{10,... | collective-permute-start | bytes 20 | tf_op jit(solution)/shard_map/ppermute | solution.py:32
  123.0 13.3 %collective-permute-start.14 = (f32[1]{0:T(128)}, f32[1]{0:T(128)}, u32[]{:S(2)}, u32[]{:S(2)}) collective-permute-start(f32[1]{0:T(128)} %add.511), channel_id=1, source_target_pairs={{0,4},{1,5},{2,6},{3,7},{4,0},{5,1},{6,2},{7,3},{8,12},{9,13},{10,... | collective-permute-start | bytes 20 | tf_op jit(solution)/shard_map/ppermute | solution.py:32
  137.0 5.4 %collective-permute-start.15 = (f32[1]{0:T(128)}, f32[1]{0:T(128)}, u32[]{:S(2)}, u32[]{:S(2)}) collective-permute-start(f32[1]{0:T(128)} %add.512), channel_id=1, source_target_pairs={{0,8},{1,9},{2,10},{3,11},{4,12},{5,13},{6,14},{7,15},{8,0},{9,1},... | collective-permute-start | bytes 20 | tf_op jit(solution)/shard_map/ppermute | solution.py:32

commit v9 on v8

--- a/solution.py
+++ b/solution.py
@@ -40,8 +40,8 @@
     a_both = steps * power(1)
     zeros = jnp.zeros_like(ends)
     incoming, upper = zeros, zeros
-    carry = jnp.stack([ends, heads])
-    group = jnp.stack([w_in, a_in, a_up, zeros, zeros, w_free, a_free])
+    carry = jnp.stack([ends, heads, w_in, a_in, a_up])
+    group = jnp.stack([zeros, zeros, w_free, a_free])
     sizes = []
     size = 1
     while size < n:
@@ -51,14 +51,20 @@
     carry_partner = lax.ppermute(carry, axis, pairs_of(1)) if sizes else None
     for k, size in enumerate(sizes):
         high = (index // size) % 2 == 1
-        f_l, b_l = jnp.where(high, carry_partner, carry)
-        f_h, b_h = jnp.where(high, carry, carry_partner)
+        f_l, b_l, wa_l, wb_l, wc_l = jnp.where(high, carry_partner, carry)
+        f_h, b_h, wa_h, wb_h, wc_h = jnp.where(high, carry, carry_partner)
         step = power(size)
         spread = size * power(size - 1)
         at = index % size
         incoming = incoming + jnp.where(high, power(at) * f_l, 0.0)
         upper = upper + jnp.where(high, 0.0, power(size - 1 - at) * b_h)
-        carry = jnp.stack([step * f_l + f_h, b_l + step * b_h])
+        carry = jnp.stack([
+            step * f_l + f_h,
+            b_l + step * b_h,
+            wa_l + step * wa_h,
+            wb_l + step * wb_h,
+            step * wc_l + wc_h,
+        ])
         partner = lax.ppermute(group, axis, pairs_of(size))
         if k + 1 < len(sizes):
             carry_partner = lax.ppermute(carry, axis, pairs_of(sizes[k + 1]))
@@ -68,18 +74,15 @@
             partner, hidden = lax.optimization_barrier((partner, hidden))
         low_g = jnp.where(high, partner, group)
         high_g = jnp.where(high, group, partner)
-        wa_l, wb_l, wc_l, u_l, v_l, zw_l, za_l = low_g
-        wa_h, wb_h, wc_h, u_h, v_h, zw_h, za_h = high_g
+        u_l, v_l, zw_l, za_l = low_g
+        u_h, v_h, zw_h, za_h = high_g
         group = jnp.stack([
-            wa_l + step * wa_h,
-            wb_l + step * wb_h,
-            step * wc_l + wc_h,
             step * u_l + (u_h + f_l * spread),
             (v_l + b_h * spread) + step * v_h,
             zw_l + zw_h + f_l * wa_h,
             za_l + za_h + f_l * wb_h + b_h * wc_l + a_both * (b_h * u_l + f_l * v_h),
         ])
-    return hidden, group[5], group[6]
+    return hidden, group[2], group[3]
 
 
 def group_sum(x, axis, n, groups):

time: 145 us -> 163 us (1.12)
  the two profiles are of different devices: /device:TPU:126 before, /device:TPU:14 now
where the time goes in v9:
time: 163 us; the launch traced here: 162 us
  starting transfers between devices  84.4 us (52%)
  waiting for transfers between devices  44.6 us (27%)
  other arithmetic  15.6 us (10%)
  matrix products  9.48 us (6%)
  between operations  5.47 us (3%)
  local copies, waits for them, and re-layouts  2.44 us (1%)
    ppermute x6, waiting for transfers between devices, fused_scan(): partner = lax.ppermute(group, axis, pairs_of(size))  36 us
    ppermute x4, starting transfers between devices, level_gather(): got.append(lax.ppermute(x, axis, perm))  31.7 us
    ppermute x6, starting transfers between devices, fused_scan(): partner = lax.ppermute(group, axis, pairs_of(size))  27.4 us
    ppermute x5, starting transfers between devices, fused_scan(): carry_partner = lax.ppermute(carry, axis, pairs_of(sizes[k + 1]))  23.5 us
    dot_general x1, matrix products, local(): jnp.dot(upper_tri, fallen, precision=PRECISION).reshape(rising.shape)  7.38 us
    reduce_sum x1, other arithmetic, finish(): grad_source = jnp.sum(adjoint, axis=1)  5.07 us
    ppermute x5, waiting for transfers between devices, fused_scan(): carry_partner = lax.ppermute(carry, axis, pairs_of(sizes[k + 1]))  4.51 us
  transfers between devices with their start and end apart: 16, of which 13 were waited for; matrix products, arithmetic and copies ran while one was open for 1% of the time, Pallas kernels for 0%

profile of v9, /device:TPU:14, one launch (start us, length us, event | category | flops | bytes accessed | tf_op | source)
XLA Modules:
  0.0 162.0 jit_solution(1437193976097709654)
XLA Ops:
  5.7 2.1 %fusion.4 = f32[128,16,512]{2,0,1:T(8,128)S(1)} fusion(f32[16,512,128]{2,1,0:T(8,128)S(1)} %bitcast.887, f32[16,512]{1,0:T(8,128)S(1)} %get-tuple-element.104), kind=kOutput, calls=%fused_computation.17 | convolution fusion | flops 807419904 | bytes 8421376 | tf_op jit(solution)/shard_map/dot_general | solution.py:125
  7.8 2.3 %fusion = f32[128,8192]{0,1:T(8,128)S(1)} fusion(f32[128,512]{0,1:T(8,128)S(1)} %copy.47, f32[8192]{0:T(1024)S(1)} %bitcast.890, f32[8192]{0:T(1024)S(1)} %bitcast.891), kind=kLoop, calls=%fused_computation.1 | loop fusion | flops 3145728 | bytes 4521984 | tf_op jit(solution)/shard_map/mul | solution.py:124
  10.2 7.4 %multiply_reduce_fusion.1 = (f32[16,512]{1,0:T(8,128)S(1)}, f32[16,512]{1,0:T(8,128)S(1)}, f32[16,512]{1,0:T(8,128)S(1)}, f32[16,512]{1,0:T(8,128)S(1)}, f32[16,...) fusion(f32[127,16,512]{2,0,1:T(8,128)S(1)} %bitcast.886, ...), kind=kOutput, calls=%fused_computation.5 | convolution fusion | flops 826236928 | bytes 17661952 | tf_op jit(solution)/shard_map/dot_general | solution.py:126
  21.1 3.6 %collective-permute-start.2 = (f32[5,16,512]{2,1,0:T(8,128)S(1)}, f32[5,16,512]{2,1,0:T(8,128)S(1)}, u32[]{:S(2)}, u32[]{:S(2)}) collective-permute-start(f32[5,16,512]{2,1,0:T(8,128)S(1)} %constant_dynamic-update-slice_fusion.5), channel_id=1, source_target_pairs={{0,32},{16,48},{32,0},{48,16},{64,96},{80,112},{96,64},{112,80},{1... | collective-permute-start | bytes 491528 | tf_op jit(solution)/shard_map/ppermute | solution.py:70
  29.5 4.7 %collective-permute-start.4 = (f32[5,16,512]{2,1,0:T(8,128)S(1)}, f32[5,16,512]{2,1,0:T(8,128)S(1)}, u32[]{:S(2)}, u32[]{:S(2)}) collective-permute-start(f32[5,16,512]{2,1,0:T(8,128)S(1)} %constant_dynamic-update-slice_fusion.10), channel_id=1, source_target_pairs={{0,64},{16,80},{32,96},{48,112},{64,0},{80,16},{96,32},{112,48},{1... | collective-permute-start | bytes 491528 | tf_op jit(solution)/shard_map/ppermute | solution.py:70
  34.3 3.6 %collective-permute-start.3 = (f32[4,16,512]{2,1,0:T(8,128)S(1)}, f32[4,16,512]{2,1,0:T(8,128)S(1)}, u32[]{:S(2)}, u32[]{:S(2)}) collective-permute-start(f32[4,16,512]{2,1,0:T(8,128)S(1)} %pad_maximum_fusion.1), channel_id=1, source_target_pairs={{0,32},{16,48},{32,0},{48,16},{64,96},{80,112},{96,64},{112,80},{1... | collective-permute-start | bytes 393224 | tf_op jit(solution)/shard_map/ppermute | solution.py:68
  37.9 4.9 %collective-permute-done.3 = f32[4,16,512]{2,1,0:T(8,128)S(1)} collective-permute-done((f32[4,16,512]{2,1,0:T(8,128)S(1)}, f32[4,16,512]{2,1,0:T(8,128)S(1)}, u32[]{:S(2)}, u32[]{:S(2)}) %collective-permute-start.3) | collective-permute-done | bytes 131104 | tf_op jit(solution)/shard_map/ppermute | solution.py:68
  43.1 7.7 %collective-permute-start.6 = (f32[5,16,512]{2,1,0:T(8,128)S(1)}, f32[5,16,512]{2,1,0:T(8,128)S(1)}, u32[]{:S(2)}, u32[]{:S(2)}) collective-permute-start(f32[5,16,512]{2,1,0:T(8,128)S(1)} %constant_dynamic-update-slice_fusion.15), channel_id=1, source_target_pairs={{0,128},{16,144},{32,160},{48,176},{64,192},{80,208},{96,224},{112... | collective-permute-start | bytes 491528 | tf_op jit(solution)/shard_map/ppermute | solution.py:70
  52.7 10.2 %collective-permute-done.5 = f32[4,16,512]{2,1,0:T(8,128)S(1)} collective-permute-done((f32[4,16,512]{2,1,0:T(8,128)S(1)}, f32[4,16,512]{2,1,0:T(8,128)S(1)}, u32[]{:S(2)}, u32[]{:S(2)}) %collective-permute-start.5) | collective-permute-done | bytes 131104 | tf_op jit(solution)/shard_map/ppermute | solution.py:68
  63.2 4.2 %collective-permute-start.8 = (f32[5,16,512]{2,1,0:T(8,128)S(1)}, f32[5,16,512]{2,1,0:T(8,128)S(1)}, u32[]{:S(2)}, u32[]{:S(2)}) collective-permute-start(f32[5,16,512]{2,1,0:T(8,128)S(1)} %constant_dynamic-update-slice_fusion.20), channel_id=1, source_target_pairs={{0,256},{16,272},{32,288},{48,304},{64,320},{80,336},{96,352},{112... | collective-permute-start | bytes 491528 | tf_op jit(solution)/shard_map/ppermute | solution.py:70
  67.4 5.3 %collective-permute-start.7 = (f32[4,16,512]{2,1,0:T(8,128)S(1)}, f32[4,16,512]{2,1,0:T(8,128)S(1)}, u32[]{:S(2)}, u32[]{:S(2)}) collective-permute-start(f32[4,16,512]{2,1,0:T(8,128)S(1)} %pad_maximum_fusion.3), channel_id=1, source_target_pairs={{0,128},{16,144},{32,160},{48,176},{64,192},{80,208},{96,224},{112... | collective-permute-start | bytes 393224 | tf_op jit(solution)/shard_map/ppermute | solution.py:68
  72.7 8.4 %collective-permute-done.7 = f32[4,16,512]{2,1,0:T(8,128)S(1)} collective-permute-done((f32[4,16,512]{2,1,0:T(8,128)S(1)}, f32[4,16,512]{2,1,0:T(8,128)S(1)}, u32[]{:S(2)}, u32[]{:S(2)}) %collective-permute-start.7) | collective-permute-done | bytes 131104 | tf_op jit(solution)/shard_map/ppermute | solution.py:68
  81.4 3.3 %collective-permute-start.10 = (f32[5,16,512]{2,1,0:T(8,128)S(1)}, f32[5,16,512]{2,1,0:T(8,128)S(1)}, u32[]{:S(2)}, u32[]{:S(2)}) collective-permute-start(f32[5,16,512]{2,1,0:T(8,128)S(1)} %constant_dynamic-update-slice_fusion.25), channel_id=1, source_target_pairs={{0,512},{16,528},{32,544},{48,560},{64,576},{80,592},{96,608},{112... | collective-permute-start | bytes 491528 | tf_op jit(solution)/shard_map/ppermute | solution.py:70
  84.7 4.3 %collective-permute-start.9 = (f32[4,16,512]{2,1,0:T(8,128)S(1)}, f32[4,16,512]{2,1,0:T(8,128)S(1)}, u32[]{:S(2)}, u32[]{:S(2)}) collective-permute-start(f32[4,16,512]{2,1,0:T(8,128)S(1)} %pad_maximum_fusion.4), channel_id=1, source_target_pairs={{0,256},{16,272},{32,288},{48,304},{64,320},{80,336},{96,352},{112... | collective-permute-start | bytes 393224 | tf_op jit(solution)/shard_map/ppermute | solution.py:68
  89.1 5.5 %collective-permute-done.9 = f32[4,16,512]{2,1,0:T(8,128)S(1)} collective-permute-done((f32[4,16,512]{2,1,0:T(8,128)S(1)}, f32[4,16,512]{2,1,0:T(8,128)S(1)}, u32[]{:S(2)}, u32[]{:S(2)}) %collective-permute-start.9) | collective-permute-done | bytes 131104 | tf_op jit(solution)/shard_map/ppermute | solution.py:68
  94.6 3.3 %collective-permute-done.10 = f32[5,16,512]{2,1,0:T(8,128)S(1)} collective-permute-done((f32[5,16,512]{2,1,0:T(8,128)S(1)}, f32[5,16,512]{2,1,0:T(8,128)S(1)}, u32[]{:S(2)}, u32[]{:S(2)}) %collective-permute-start.10) | collective-permute-done | bytes 163872 | tf_op jit(solution)/shard_map/ppermute | solution.py:70
  98.2 5.1 %add_reduce_fusion = (f32[128,512]{1,0:T(8,128)S(1)}, f32[128,512]{1,0:T(8,128)S(1)}) fusion(f32[128,16,512]{2,0,1:T(8,128)} %get-tuple-element.106, f32[16,512]{1,0:T(8,128)S(1)} %select_add_fusion, f32[16,512]{1,0:T(8,128)S(1)} %get-tuple-element.101, f32[16,512]{1,0:T(8,128)S(1)} %copy-done, f32[128,16,512]{2,0,1:T(8,128)} %copy-done.1, ...), kind=kLoop, calls=%fused_computation.3 | loop fusion | flops 12451840 | bytes 9142272 | tf_op jit(solution)/shard_map/reduce_sum | solution.py:142
  104.1 10.3 %collective-permute-start.11 = (f32[4,16,512]{2,1,0:T(8,128)S(1)}, f32[4,16,512]{2,1,0:T(8,128)S(1)}, u32[]{:S(2)}, u32[]{:S(2)}) collective-permute-start(f32[4,16,512]{2,1,0:T(8,128)S(1)} %pad_maximum_fusion.5), channel_id=1, source_target_pairs={{0,512},{16,528},{32,544},{48,560},{64,576},{80,592},{96,608},{112... | collective-permute-start | bytes 393224 | tf_op jit(solution)/shard_map/ppermute | solution.py:68
  115.2 5.7 %collective-permute-done.11 = f32[4,16,512]{2,1,0:T(8,128)S(1)} collective-permute-done((f32[4,16,512]{2,1,0:T(8,128)S(1)}, f32[4,16,512]{2,1,0:T(8,128)S(1)}, u32[]{:S(2)}, u32[]{:S(2)}) %collective-permute-start.11) | collective-permute-done | bytes 131104 | tf_op jit(solution)/shard_map/ppermute | solution.py:68
  123.5 6.1 %collective-permute-start.12 = (f32[1]{0:T(128)}, f32[1]{0:T(128)}, u32[]{:S(2)}, u32[]{:S(2)}) collective-permute-start(f32[1]{0:T(128)} %bitcast.139), channel_id=1, source_target_pairs={{0,1},{1,0},{2,3},{3,2},{4,5},{5,4},{6,7},{7,6},{8,9},{9,8},{10,11... | collective-permute-start | bytes 20 | tf_op jit(solution)/shard_map/ppermute | solution.py:32
  130.5 9.2 %collective-permute-start.13 = (f32[1]{0:T(128)}, f32[1]{0:T(128)}, u32[]{:S(2)}, u32[]{:S(2)}) collective-permute-start(f32[1]{0:T(128)} %add.510), channel_id=1, source_target_pairs={{0,2},{1,3},{2,0},{3,1},{4,6},{5,7},{6,4},{7,5},{8,10},{9,11},{10,... | collective-permute-start | bytes 20 | tf_op jit(solution)/shard_map/ppermute | solution.py:32
  140.5 13.1 %collective-permute-start.14 = (f32[1]{0:T(128)}, f32[1]{0:T(128)}, u32[]{:S(2)}, u32[]{:S(2)}) collective-permute-start(f32[1]{0:T(128)} %add.511), channel_id=1, source_target_pairs={{0,4},{1,5},{2,6},{3,7},{4,0},{5,1},{6,2},{7,3},{8,12},{9,13},{10,... | collective-permute-start | bytes 20 | tf_op jit(solution)/shard_map/ppermute | solution.py:32
  154.4 3.2 %collective-permute-start.15 = (f32[1]{0:T(128)}, f32[1]{0:T(128)}, u32[]{:S(2)}, u32[]{:S(2)}) collective-permute-start(f32[1]{0:T(128)} %add.512), channel_id=1, source_target_pairs={{0,8},{1,9},{2,10},{3,11},{4,12},{5,13},{6,14},{7,15},{8,0},{9,1},... | collective-permute-start | bytes 20 | tf_op jit(solution)/shard_map/ppermute | solution.py:32
  157.6 2.2 %collective-permute-done.15 = f32[1]{0:T(128)} collective-permute-done((f32[1]{0:T(128)}, f32[1]{0:T(128)}, u32[]{:S(2)}, u32[]{:S(2)}) %collective-permute-start.15) | collective-permute-done | bytes 36 | tf_op jit(solution)/shard_map/ppermute | solution.py:32
  (105 shorter events, 20.8 us)
Async XLA Ops:
  7.8 9.8 %copy-start.1 = (f32[128,16,512]{2,0,1:T(8,128)}, f32[128,16,512]{2,0,1:T(8,128)S(1)}, u32[]{:S(2)}) copy-start(f32[128,16,512]{2,0,1:T(8,128)S(1)} %fusion.4) | copy-start | bytes 12582916
  7.8 2.4 %copy-start = (f32[16,512]{1,0:T(8,128)S(1)}, f32[16,512]{1,0:T(8,128)}, u32[]{:S(2)}) copy-start(f32[16,512]{1,0:T(8,128)} %param.11) | copy-start | bytes 98308
  17.6 3.3 %collective-permute-start.1 = (f32[5,16,512]{2,1,0:T(8,128)S(1)}, f32[5,16,512]{2,1,0:T(8,128)S(1)}, u32[]{:S(2)}, u32[]{:S(2)}) collective-permute-start(f32[5,16,512]{2,1,0:T(8,128)S(1)} %constant_dynamic-update-slice_fusion), channel_id=1, source_target_pairs={{0,16},{16,0},{32,48},{48,32},{64,80},{80,64},{96,112},{112,96},{1... | collective-permute-start | bytes 491528 | tf_op jit(solution)/shard_map/ppermute | solution.py:51
  21.1 8.1 %collective-permute-start.2 = (f32[5,16,512]{2,1,0:T(8,128)S(1)}, f32[5,16,512]{2,1,0:T(8,128)S(1)}, u32[]{:S(2)}, u32[]{:S(2)}) collective-permute-start(f32[5,16,512]{2,1,0:T(8,128)S(1)} %constant_dynamic-update-slice_fusion.5), channel_id=1, source_target_pairs={{0,32},{16,48},{32,0},{48,16},{64,96},{80,112},{96,64},{112,80},{1... | collective-permute-start | bytes 491528 | tf_op jit(solution)/shard_map/ppermute | solution.py:70
  24.7 3.2 %collective-permute-start = (f32[4,16,512]{2,1,0:T(8,128)S(1)}, f32[4,16,512]{2,1,0:T(8,128)S(1)}, u32[]{:S(2)}, u32[]{:S(2)}) collective-permute-start(f32[4,16,512]{2,1,0:T(8,128)S(1)} %pad_maximum_fusion), channel_id=1, source_target_pairs={{0,16},{16,0},{32,48},{48,32},{64,80},{80,64},{96,112},{112,96},{1... | collective-permute-start | bytes 393224 | tf_op jit(solution)/shard_map/ppermute | solution.py:68
  29.5 13.3 %collective-permute-start.4 = (f32[5,16,512]{2,1,0:T(8,128)S(1)}, f32[5,16,512]{2,1,0:T(8,128)S(1)}, u32[]{:S(2)}, u32[]{:S(2)}) collective-permute-start(f32[5,16,512]{2,1,0:T(8,128)S(1)} %constant_dynamic-update-slice_fusion.10), channel_id=1, source_target_pairs={{0,64},{16,80},{32,96},{48,112},{64,0},{80,16},{96,32},{112,48},{1... | collective-permute-start | bytes 491528 | tf_op jit(solution)/shard_map/ppermute | solution.py:70
  34.3 8.6 %collective-permute-start.3 = (f32[4,16,512]{2,1,0:T(8,128)S(1)}, f32[4,16,512]{2,1,0:T(8,128)S(1)}, u32[]{:S(2)}, u32[]{:S(2)}) collective-permute-start(f32[4,16,512]{2,1,0:T(8,128)S(1)} %pad_maximum_fusion.1), channel_id=1, source_target_pairs={{0,32},{16,48},{32,0},{48,16},{64,96},{80,112},{96,64},{112,80},{1... | collective-permute-start | bytes 393224 | tf_op jit(solution)/shard_map/ppermute | solution.py:68
  43.1 19.8 %collective-permute-start.6 = (f32[5,16,512]{2,1,0:T(8,128)S(1)}, f32[5,16,512]{2,1,0:T(8,128)S(1)}, u32[]{:S(2)}, u32[]{:S(2)}) collective-permute-start(f32[5,16,512]{2,1,0:T(8,128)S(1)} %constant_dynamic-update-slice_fusion.15), channel_id=1, source_target_pairs={{0,128},{16,144},{32,160},{48,176},{64,192},{80,208},{96,224},{112... | collective-permute-start | bytes 491528 | tf_op jit(solution)/shard_map/ppermute | solution.py:70
  50.8 12.1 %collective-permute-start.5 = (f32[4,16,512]{2,1,0:T(8,128)S(1)}, f32[4,16,512]{2,1,0:T(8,128)S(1)}, u32[]{:S(2)}, u32[]{:S(2)}) collective-permute-start(f32[4,16,512]{2,1,0:T(8,128)S(1)} %pad_maximum_fusion.2), channel_id=1, source_target_pairs={{0,64},{16,80},{32,96},{48,112},{64,0},{80,16},{96,32},{112,48},{1... | collective-permute-start | bytes 393224 | tf_op jit(solution)/shard_map/ppermute | solution.py:68
  63.2 18.0 %collective-permute-start.8 = (f32[5,16,512]{2,1,0:T(8,128)S(1)}, f32[5,16,512]{2,1,0:T(8,128)S(1)}, u32[]{:S(2)}, u32[]{:S(2)}) collective-permute-start(f32[5,16,512]{2,1,0:T(8,128)S(1)} %constant_dynamic-update-slice_fusion.20), channel_id=1, source_target_pairs={{0,256},{16,272},{32,288},{48,304},{64,320},{80,336},{96,352},{112... | collective-permute-start | bytes 491528 | tf_op jit(solution)/shard_map/ppermute | solution.py:70
  67.4 13.7 %collective-permute-start.7 = (f32[4,16,512]{2,1,0:T(8,128)S(1)}, f32[4,16,512]{2,1,0:T(8,128)S(1)}, u32[]{:S(2)}, u32[]{:S(2)}) collective-permute-start(f32[4,16,512]{2,1,0:T(8,128)S(1)} %pad_maximum_fusion.3), channel_id=1, source_target_pairs={{0,128},{16,144},{32,160},{48,176},{64,192},{80,208},{96,224},{112... | collective-permute-start | bytes 393224 | tf_op jit(solution)/shard_map/ppermute | solution.py:68
  81.4 16.5 %collective-permute-start.10 = (f32[5,16,512]{2,1,0:T(8,128)S(1)}, f32[5,16,512]{2,1,0:T(8,128)S(1)}, u32[]{:S(2)}, u32[]{:S(2)}) collective-permute-start(f32[5,16,512]{2,1,0:T(8,128)S(1)} %constant_dynamic-update-slice_fusion.25), channel_id=1, source_target_pairs={{0,512},{16,528},{32,544},{48,560},{64,576},{80,592},{96,608},{112... | collective-permute-start | bytes 491528 | tf_op jit(solution)/shard_map/ppermute | solution.py:70
  84.7 9.9 %collective-permute-start.9 = (f32[4,16,512]{2,1,0:T(8,128)S(1)}, f32[4,16,512]{2,1,0:T(8,128)S(1)}, u32[]{:S(2)}, u32[]{:S(2)}) collective-permute-start(f32[4,16,512]{2,1,0:T(8,128)S(1)} %pad_maximum_fusion.4), channel_id=1, source_target_pairs={{0,256},{16,272},{32,288},{48,304},{64,320},{80,336},{96,352},{112... | collective-permute-start | bytes 393224 | tf_op jit(solution)/shard_map/ppermute | solution.py:68
  98.2 5.1 %copy-start.2 = (bf16[128,512]{1,0:T(8,128)(2,1)S(1)}, bf16[128,512]{1,0:T(8,128)(2,1)}, u32[]{:S(2)}) copy-start(bf16[128,512]{1,0:T(8,128)(2,1)} %param.8) | copy-start | bytes 393220
  98.2 5.1 %copy-start.3 = (bf16[128,512]{1,0:T(8,128)(2,1)S(1)}, bf16[128,512]{1,0:T(8,128)(2,1)}, u32[]{:S(2)}) copy-start(bf16[128,512]{1,0:T(8,128)(2,1)} %param.7) | copy-start | bytes 393220
  98.2 16.2 %copy-start.4 = (bf16[128,512]{1,0:T(8,128)(2,1)S(1)}, bf16[128,512]{1,0:T(8,128)(2,1)}, u32[]{:S(2)}) copy-start(bf16[128,512]{1,0:T(8,128)(2,1)} %param.6) | copy-start | bytes 393220
  98.2 16.2 %copy-start.5 = (bf16[128,512]{1,0:T(8,128)(2,1)S(1)}, bf16[128,512]{1,0:T(8,128)(2,1)}, u32[]{:S(2)}) copy-start(bf16[128,512]{1,0:T(8,128)(2,1)} %param.9) | copy-start | bytes 393220
  98.2 22.7 %copy-start.6 = (f32[16,512]{1,0:T(8,128)S(1)}, f32[16,512]{1,0:T(8,128)}, u32[]{:S(2)}) copy-start(f32[16,512]{1,0:T(8,128)} %param.10) | copy-start | bytes 98308
  104.1 16.8 %collective-permute-start.11 = (f32[4,16,512]{2,1,0:T(8,128)S(1)}, f32[4,16,512]{2,1,0:T(8,128)S(1)}, u32[]{:S(2)}, u32[]{:S(2)}) collective-permute-start(f32[4,16,512]{2,1,0:T(8,128)S(1)} %pad_maximum_fusion.5), channel_id=1, source_target_pairs={{0,512},{16,528},{32,544},{48,560},{64,576},{80,592},{96,608},{112... | collective-permute-start | bytes 393224 | tf_op jit(solution)/shard_map/ppermute | solution.py:68
  123.5 6.3 %collective-permute-start.12 = (f32[1]{0:T(128)}, f32[1]{0:T(128)}, u32[]{:S(2)}, u32[]{:S(2)}) collective-permute-start(f32[1]{0:T(128)} %bitcast.139), channel_id=1, source_target_pairs={{0,1},{1,0},{2,3},{3,2},{4,5},{5,4},{6,7},{7,6},{8,9},{9,8},{10,11... | collective-permute-start | bytes 20 | tf_op jit(solution)/shard_map/ppermute | solution.py:32
  130.5 9.4 %collective-permute-start.13 = (f32[1]{0:T(128)}, f32[1]{0:T(128)}, u32[]{:S(2)}, u32[]{:S(2)}) collective-permute-start(f32[1]{0:T(128)} %add.510), channel_id=1, source_target_pairs={{0,2},{1,3},{2,0},{3,1},{4,6},{5,7},{6,4},{7,5},{8,10},{9,11},{10,... | collective-permute-start | bytes 20 | tf_op jit(solution)/shard_map/ppermute | solution.py:32
  140.5 13.3 %collective-permute-start.14 = (f32[1]{0:T(128)}, f32[1]{0:T(128)}, u32[]{:S(2)}, u32[]{:S(2)}) collective-permute-start(f32[1]{0:T(128)} %add.511), channel_id=1, source_target_pairs={{0,4},{1,5},{2,6},{3,7},{4,0},{5,1},{6,2},{7,3},{8,12},{9,13},{10,... | collective-permute-start | bytes 20 | tf_op jit(solution)/shard_map/ppermute | solution.py:32
  154.4 5.4 %collective-permute-start.15 = (f32[1]{0:T(128)}, f32[1]{0:T(128)}, u32[]{:S(2)}, u32[]{:S(2)}) collective-permute-start(f32[1]{0:T(128)} %add.512), channel_id=1, source_target_pairs={{0,8},{1,9},{2,10},{3,11},{4,12},{5,13},{6,14},{7,15},{8,0},{9,1},... | collective-permute-start | bytes 20 | tf_op jit(solution)/shard_map/ppermute | solution.py:32

commit v10 on v8

--- a/solution.py
+++ b/solution.py
@@ -10,7 +10,7 @@
 
 PRECISION = lax.Precision.HIGH
 CTX_GROUPS = (2, 8, 4)
-CHAN_GROUPS = (2, 2, 2, 2)
+CHAN_GROUPS = (2, 4, 2)
 
 
 def levels_of(n, groups):

time: 145 us -> 151 us (1.041)
  starting transfers between devices: 74.9 us -> 78.1 us
  waiting for transfers between devices: 37.9 us -> 39.8 us
    ppermute x4 -> x5, starting transfers between devices: 33.9 us -> 37.1 us  [level_gather(): got.append(lax.ppermute(x, axis, perm))]
    ppermute x4 -> x5, waiting for transfers between devices: 2.73 us -> 4.57 us  [level_gather(): got.append(lax.ppermute(x, axis, perm))]
  transfers between devices with their start and end apart: 16 -> 17, of which waited for: 13 -> 12; matrix products, arithmetic and copies ran while one was open for 4% -> 4% of each run, Pallas kernels for 0% -> 0%
where the time goes in v10:
time: 151 us; the launch traced here: 150 us
  starting transfers between devices  78.1 us (52%)
  waiting for transfers between devices  39.8 us (26%)
  other arithmetic  14.3 us (9%)
  matrix products  9.49 us (6%)
  between operations  6.12 us (4%)
  local copies, waits for them, and re-layouts  2.45 us (2%)
    ppermute x5, starting transfers between devices, level_gather(): got.append(lax.ppermute(x, axis, perm))  37.1 us
    ppermute x5, waiting for transfers between devices, fused_scan(): carry_partner = lax.ppermute(carry, axis, pairs_of(sizes[k + 1]))  23.5 us
    ppermute x6, starting transfers between devices, fused_scan(): partner = lax.ppermute(group, axis, pairs_of(size))  21.7 us
    ppermute x5, starting transfers between devices, fused_scan(): carry_partner = lax.ppermute(carry, axis, pairs_of(sizes[k + 1]))  17.4 us
    ppermute x6, waiting for transfers between devices, fused_scan(): partner = lax.ppermute(group, axis, pairs_of(size))  11.7 us
    dot_general x1, matrix products, local(): jnp.dot(upper_tri, fallen, precision=PRECISION).reshape(rising.shape)  7.38 us
    ppermute x5, waiting for transfers between devices, level_gather(): got.append(lax.ppermute(x, axis, perm))  4.57 us
    reduce_sum x1, other arithmetic, finish(): mixed = jnp.sum(mixing[None] * states, axis=1)  3.47 us
  transfers between devices with their start and end apart: 17, of which 12 were waited for; matrix products, arithmetic and copies ran while one was open for 4% of the time, Pallas kernels for 0%

profile of v10, /device:TPU:126, one launch (start us, length us, event | category | flops | bytes accessed | tf_op | source)
XLA Modules:
  0.0 150.2 jit_solution(14126862159596036566)
XLA Ops:
  9.3 7.4 %multiply_reduce_fusion.3 = (f32[16,512]{1,0:T(8,128)S(1)}, f32[16,512]{1,0:T(8,128)S(1)}, f32[16,512]{1,0:T(8,128)S(1)}, f32[16,512]{1,0:T(8,128)S(1)}, f32[16,...) fusion(f32[127,16,512]{2,0,1:T(8,128)S(1)} %bitcast.900, ...), kind=kOutput, calls=%fused_computation.7 | convolution fusion | flops 826236928 | bytes 17661952 | tf_op jit(solution)/shard_map/dot_general | solution.py:123
  21.3 3.1 %collective-permute-start.2 = (f32[2,16,512]{2,1,0:T(8,128)S(1)}, f32[2,16,512]{2,1,0:T(8,128)S(1)}, u32[]{:S(2)}, u32[]{:S(2)}) collective-permute-start(f32[2,16,512]{2,1,0:T(8,128)S(1)} %pad_maximum_fusion.2), channel_id=1, source_target_pairs={{0,32},{16,48},{32,0},{48,16},{64,96},{80,112},{96,64},{112,80},{1... | collective-permute-start | bytes 196616 | tf_op jit(solution)/shard_map/ppermute | solution.py:64
  24.4 3.0 %collective-permute-done.2 = f32[2,16,512]{2,1,0:T(8,128)S(1)} collective-permute-done((f32[2,16,512]{2,1,0:T(8,128)S(1)}, f32[2,16,512]{2,1,0:T(8,128)S(1)}, u32[]{:S(2)}, u32[]{:S(2)}) %collective-permute-start.2) | collective-permute-done | bytes 65568 | tf_op jit(solution)/shard_map/ppermute | solution.py:64
  27.7 3.1 %collective-permute-start.3 = (f32[7,16,512]{2,1,0:T(8,128)S(1)}, f32[7,16,512]{2,1,0:T(8,128)S(1)}, u32[]{:S(2)}, u32[]{:S(2)}) collective-permute-start(f32[7,16,512]{2,1,0:T(8,128)S(1)} %constant_dynamic-update-slice_fusion.6), channel_id=1, source_target_pairs={{0,32},{16,48},{32,0},{48,16},{64,96},{80,112},{96,64},{112,80},{1... | collective-permute-start | bytes 688136 | tf_op jit(solution)/shard_map/ppermute | solution.py:62
  30.9 3.8 %collective-permute-start.4 = (f32[2,16,512]{2,1,0:T(8,128)S(1)}, f32[2,16,512]{2,1,0:T(8,128)S(1)}, u32[]{:S(2)}, u32[]{:S(2)}) collective-permute-start(f32[2,16,512]{2,1,0:T(8,128)S(1)} %pad_maximum_fusion.3), channel_id=1, source_target_pairs={{0,64},{16,80},{32,96},{48,112},{64,0},{80,16},{96,32},{112,48},{1... | collective-permute-start | bytes 196616 | tf_op jit(solution)/shard_map/ppermute | solution.py:64
  34.7 3.2 %collective-permute-done.4 = f32[2,16,512]{2,1,0:T(8,128)S(1)} collective-permute-done((f32[2,16,512]{2,1,0:T(8,128)S(1)}, f32[2,16,512]{2,1,0:T(8,128)S(1)}, u32[]{:S(2)}, u32[]{:S(2)}) %collective-permute-start.4) | collective-permute-done | bytes 65568 | tf_op jit(solution)/shard_map/ppermute | solution.py:64
  38.2 3.8 %collective-permute-start.5 = (f32[7,16,512]{2,1,0:T(8,128)S(1)}, f32[7,16,512]{2,1,0:T(8,128)S(1)}, u32[]{:S(2)}, u32[]{:S(2)}) collective-permute-start(f32[7,16,512]{2,1,0:T(8,128)S(1)} %constant_dynamic-update-slice_fusion.13), channel_id=1, source_target_pairs={{0,64},{16,80},{32,96},{48,112},{64,0},{80,16},{96,32},{112,48},{1... | collective-permute-start | bytes 688136 | tf_op jit(solution)/shard_map/ppermute | solution.py:62
  42.1 3.0 %collective-permute-start.6 = (f32[2,16,512]{2,1,0:T(8,128)S(1)}, f32[2,16,512]{2,1,0:T(8,128)S(1)}, u32[]{:S(2)}, u32[]{:S(2)}) collective-permute-start(f32[2,16,512]{2,1,0:T(8,128)S(1)} %pad_maximum_fusion.4), channel_id=1, source_target_pairs={{0,128},{16,144},{32,160},{48,176},{64,192},{80,208},{96,224},{112... | collective-permute-start | bytes 196616 | tf_op jit(solution)/shard_map/ppermute | solution.py:64
  45.1 7.7 %collective-permute-done.6 = f32[2,16,512]{2,1,0:T(8,128)S(1)} collective-permute-done((f32[2,16,512]{2,1,0:T(8,128)S(1)}, f32[2,16,512]{2,1,0:T(8,128)S(1)}, u32[]{:S(2)}, u32[]{:S(2)}) %collective-permute-start.6) | collective-permute-done | bytes 65568 | tf_op jit(solution)/shard_map/ppermute | solution.py:64
  54.3 3.0 %collective-permute-start.7 = (f32[7,16,512]{2,1,0:T(8,128)S(1)}, f32[7,16,512]{2,1,0:T(8,128)S(1)}, u32[]{:S(2)}, u32[]{:S(2)}) collective-permute-start(f32[7,16,512]{2,1,0:T(8,128)S(1)} %constant_dynamic-update-slice_fusion.20), channel_id=1, source_target_pairs={{0,128},{16,144},{32,160},{48,176},{64,192},{80,208},{96,224},{112... | collective-permute-start | bytes 688136 | tf_op jit(solution)/shard_map/ppermute | solution.py:62
  57.4 4.2 %collective-permute-start.8 = (f32[2,16,512]{2,1,0:T(8,128)S(1)}, f32[2,16,512]{2,1,0:T(8,128)S(1)}, u32[]{:S(2)}, u32[]{:S(2)}) collective-permute-start(f32[2,16,512]{2,1,0:T(8,128)S(1)} %pad_maximum_fusion.5), channel_id=1, source_target_pairs={{0,256},{16,272},{32,288},{48,304},{64,320},{80,336},{96,352},{112... | collective-permute-start | bytes 196616 | tf_op jit(solution)/shard_map/ppermute | solution.py:64
  61.7 2.8 %collective-permute-done.8 = f32[2,16,512]{2,1,0:T(8,128)S(1)} collective-permute-done((f32[2,16,512]{2,1,0:T(8,128)S(1)}, f32[2,16,512]{2,1,0:T(8,128)S(1)}, u32[]{:S(2)}, u32[]{:S(2)}) %collective-permute-start.8) | collective-permute-done | bytes 65568 | tf_op jit(solution)/shard_map/ppermute | solution.py:64
  64.5 4.8 %collective-permute-done.7 = f32[7,16,512]{2,1,0:T(8,128)S(1)} collective-permute-done((f32[7,16,512]{2,1,0:T(8,128)S(1)}, f32[7,16,512]{2,1,0:T(8,128)S(1)}, u32[]{:S(2)}, u32[]{:S(2)}) %collective-permute-start.7) | collective-permute-done | bytes 229408 | tf_op jit(solution)/shard_map/ppermute | solution.py:62
  69.5 4.3 %collective-permute-start.9 = (f32[7,16,512]{2,1,0:T(8,128)S(1)}, f32[7,16,512]{2,1,0:T(8,128)S(1)}, u32[]{:S(2)}, u32[]{:S(2)}) collective-permute-start(f32[7,16,512]{2,1,0:T(8,128)S(1)} %constant_dynamic-update-slice_fusion.27), channel_id=1, source_target_pairs={{0,256},{16,272},{32,288},{48,304},{64,320},{80,336},{96,352},{112... | collective-permute-start | bytes 688136 | tf_op jit(solution)/shard_map/ppermute | solution.py:62
  74.0 3.3 %collective-permute-start.10 = (f32[2,16,512]{2,1,0:T(8,128)S(1)}, f32[2,16,512]{2,1,0:T(8,128)S(1)}, u32[]{:S(2)}, u32[]{:S(2)}) collective-permute-start(f32[2,16,512]{2,1,0:T(8,128)S(1)} %pad_maximum_fusion), channel_id=1, source_target_pairs={{0,512},{16,528},{32,544},{48,560},{64,576},{80,592},{96,608},{112... | collective-permute-start | bytes 196616 | tf_op jit(solution)/shard_map/ppermute | solution.py:64
  77.3 6.8 %collective-permute-done.10 = f32[2,16,512]{2,1,0:T(8,128)S(1)} collective-permute-done((f32[2,16,512]{2,1,0:T(8,128)S(1)}, f32[2,16,512]{2,1,0:T(8,128)S(1)}, u32[]{:S(2)}, u32[]{:S(2)}) %collective-permute-start.10) | collective-permute-done | bytes 65568 | tf_op jit(solution)/shard_map/ppermute | solution.py:64
  86.0 5.0 %collective-permute-start.11 = (f32[7,16,512]{2,1,0:T(8,128)S(1)}, f32[7,16,512]{2,1,0:T(8,128)S(1)}, u32[]{:S(2)}, u32[]{:S(2)}) collective-permute-start(f32[7,16,512]{2,1,0:T(8,128)S(1)} %constant_dynamic-update-slice_fusion.34), channel_id=1, source_target_pairs={{0,512},{16,528},{32,544},{48,560},{64,576},{80,592},{96,608},{112... | collective-permute-start | bytes 688136 | tf_op jit(solution)/shard_map/ppermute | solution.py:62
  91.0 3.5 %multiply_reduce_fusion = f32[128,512]{1,0:T(8,128)S(1)} fusion(f32[128,16,512]{2,0,1:T(8,128)} %copy-done.1, f32[16,512]{1,0:T(8,128)S(1)} %get-tuple-element.57, f32[16,512]{1,0:T(8,128)S(1)} %get-tuple-element.98, f32[16,512]{1,0:T(8,128)S(1)} %get-tuple-element.99, f32[16,512]{1,0:T(8,128)S(1)} %get-tuple-element.100), kind=kLoop, calls=%fused_computation.4 | loop fusion | flops 6225920 | bytes 4587520 | tf_op jit(solution)/shard_map/reduce_sum | solution.py:138
  97.3 4.0 %collective-permute-done.11 = f32[7,16,512]{2,1,0:T(8,128)S(1)} collective-permute-done((f32[7,16,512]{2,1,0:T(8,128)S(1)}, f32[7,16,512]{2,1,0:T(8,128)S(1)}, u32[]{:S(2)}, u32[]{:S(2)}) %collective-permute-start.11) | collective-permute-done | bytes 229408 | tf_op jit(solution)/shard_map/ppermute | solution.py:62
  103.9 8.4 %collective-permute-start.12 = (f32[1]{0:T(128)}, f32[1]{0:T(128)}, u32[]{:S(2)}, u32[]{:S(2)}) collective-permute-start(f32[1]{0:T(128)} %bitcast.139), channel_id=1, source_target_pairs={{0,1},{1,0},{2,3},{3,2},{4,5},{5,4},{6,7},{7,6},{8,9},{9,8},{10,11... | collective-permute-start | bytes 20 | tf_op jit(solution)/shard_map/ppermute | solution.py:32
  113.3 9.1 %collective-permute-start.13 = (f32[1]{0:T(128)}, f32[1]{0:T(128)}, u32[]{:S(2)}, u32[]{:S(2)}) collective-permute-start(f32[1]{0:T(128)} %add.513), channel_id=1, source_target_pairs={{0,2},{1,3},{2,4},{3,5},{4,6},{5,7},{6,0},{7,1},{8,10},{9,11},{10,... | collective-permute-start | bytes 20 | tf_op jit(solution)/shard_map/ppermute | solution.py:32
  122.4 13.1 %collective-permute-start.14 = (f32[1]{0:T(128)}, f32[1]{0:T(128)}, u32[]{:S(2)}, u32[]{:S(2)}) collective-permute-start(f32[1]{0:T(128)} %add.513), channel_id=1, source_target_pairs={{0,4},{1,5},{2,6},{3,7},{4,0},{5,1},{6,2},{7,3},{8,12},{9,13},{10,... | collective-permute-start | bytes 20 | tf_op jit(solution)/shard_map/ppermute | solution.py:32
  135.5 3.2 %collective-permute-start.15 = (f32[1]{0:T(128)}, f32[1]{0:T(128)}, u32[]{:S(2)}, u32[]{:S(2)}) collective-permute-start(f32[1]{0:T(128)} %add.513), channel_id=1, source_target_pairs={{0,6},{1,7},{2,0},{3,1},{4,2},{5,3},{6,4},{7,5},{8,14},{9,15},{10,... | collective-permute-start | bytes 20 | tf_op jit(solution)/shard_map/ppermute | solution.py:32
  142.5 3.2 %collective-permute-start.16 = (f32[1]{0:T(128)}, f32[1]{0:T(128)}, u32[]{:S(2)}, u32[]{:S(2)}) collective-permute-start(f32[1]{0:T(128)} %add.516), channel_id=1, source_target_pairs={{0,8},{1,9},{2,10},{3,11},{4,12},{5,13},{6,14},{7,15},{8,0},{9,1},... | collective-permute-start | bytes 20 | tf_op jit(solution)/shard_map/ppermute | solution.py:32
  (113 shorter events, 27.2 us)
Async XLA Ops:
  7.0 9.8 %copy-start.1 = (f32[128,16,512]{2,0,1:T(8,128)}, f32[128,16,512]{2,0,1:T(8,128)S(1)}, u32[]{:S(2)}) copy-start(f32[128,16,512]{2,0,1:T(8,128)S(1)} %fusion.3) | copy-start | bytes 12582916
  16.8 4.4 %collective-permute-start.1 = (f32[2,16,512]{2,1,0:T(8,128)S(1)}, f32[2,16,512]{2,1,0:T(8,128)S(1)}, u32[]{:S(2)}, u32[]{:S(2)}) collective-permute-start(f32[2,16,512]{2,1,0:T(8,128)S(1)} %pad_maximum_fusion.1), channel_id=1, source_target_pairs={{0,16},{16,0},{32,48},{48,32},{64,80},{80,64},{96,112},{112,96},{1... | collective-permute-start | bytes 196616 | tf_op jit(solution)/shard_map/ppermute | solution.py:51
  18.8 8.7 %collective-permute-start = (f32[7,16,512]{2,1,0:T(8,128)S(1)}, f32[7,16,512]{2,1,0:T(8,128)S(1)}, u32[]{:S(2)}, u32[]{:S(2)}) collective-permute-start(f32[7,16,512]{2,1,0:T(8,128)S(1)} %constant_dynamic-update-slice_fusion), channel_id=1, source_target_pairs={{0,16},{16,0},{32,48},{48,32},{64,80},{80,64},{96,112},{112,96},{1... | collective-permute-start | bytes 688136 | tf_op jit(solution)/shard_map/ppermute | solution.py:62
  21.3 6.2 %collective-permute-start.2 = (f32[2,16,512]{2,1,0:T(8,128)S(1)}, f32[2,16,512]{2,1,0:T(8,128)S(1)}, u32[]{:S(2)}, u32[]{:S(2)}) collective-permute-start(f32[2,16,512]{2,1,0:T(8,128)S(1)} %pad_maximum_fusion.2), channel_id=1, source_target_pairs={{0,32},{16,48},{32,0},{48,16},{64,96},{80,112},{96,64},{112,80},{1... | collective-permute-start | bytes 196616 | tf_op jit(solution)/shard_map/ppermute | solution.py:64
  27.7 10.3 %collective-permute-start.3 = (f32[7,16,512]{2,1,0:T(8,128)S(1)}, f32[7,16,512]{2,1,0:T(8,128)S(1)}, u32[]{:S(2)}, u32[]{:S(2)}) collective-permute-start(f32[7,16,512]{2,1,0:T(8,128)S(1)} %constant_dynamic-update-slice_fusion.6), channel_id=1, source_target_pairs={{0,32},{16,48},{32,0},{48,16},{64,96},{80,112},{96,64},{112,80},{1... | collective-permute-start | bytes 688136 | tf_op jit(solution)/shard_map/ppermute | solution.py:62
  30.9 7.1 %collective-permute-start.4 = (f32[2,16,512]{2,1,0:T(8,128)S(1)}, f32[2,16,512]{2,1,0:T(8,128)S(1)}, u32[]{:S(2)}, u32[]{:S(2)}) collective-permute-start(f32[2,16,512]{2,1,0:T(8,128)S(1)} %pad_maximum_fusion.3), channel_id=1, source_target_pairs={{0,64},{16,80},{32,96},{48,112},{64,0},{80,16},{96,32},{112,48},{1... | collective-permute-start | bytes 196616 | tf_op jit(solution)/shard_map/ppermute | solution.py:64
  38.2 15.9 %collective-permute-start.5 = (f32[7,16,512]{2,1,0:T(8,128)S(1)}, f32[7,16,512]{2,1,0:T(8,128)S(1)}, u32[]{:S(2)}, u32[]{:S(2)}) collective-permute-start(f32[7,16,512]{2,1,0:T(8,128)S(1)} %constant_dynamic-update-slice_fusion.13), channel_id=1, source_target_pairs={{0,64},{16,80},{32,96},{48,112},{64,0},{80,16},{96,32},{112,48},{1... | collective-permute-start | bytes 688136 | tf_op jit(solution)/shard_map/ppermute | solution.py:62
  42.1 10.7 %collective-permute-start.6 = (f32[2,16,512]{2,1,0:T(8,128)S(1)}, f32[2,16,512]{2,1,0:T(8,128)S(1)}, u32[]{:S(2)}, u32[]{:S(2)}) collective-permute-start(f32[2,16,512]{2,1,0:T(8,128)S(1)} %pad_maximum_fusion.4), channel_id=1, source_target_pairs={{0,128},{16,144},{32,160},{48,176},{64,192},{80,208},{96,224},{112... | collective-permute-start | bytes 196616 | tf_op jit(solution)/shard_map/ppermute | solution.py:64
  54.3 15.0 %collective-permute-start.7 = (f32[7,16,512]{2,1,0:T(8,128)S(1)}, f32[7,16,512]{2,1,0:T(8,128)S(1)}, u32[]{:S(2)}, u32[]{:S(2)}) collective-permute-start(f32[7,16,512]{2,1,0:T(8,128)S(1)} %constant_dynamic-update-slice_fusion.20), channel_id=1, source_target_pairs={{0,128},{16,144},{32,160},{48,176},{64,192},{80,208},{96,224},{112... | collective-permute-start | bytes 688136 | tf_op jit(solution)/shard_map/ppermute | solution.py:62
  57.4 7.1 %collective-permute-start.8 = (f32[2,16,512]{2,1,0:T(8,128)S(1)}, f32[2,16,512]{2,1,0:T(8,128)S(1)}, u32[]{:S(2)}, u32[]{:S(2)}) collective-permute-start(f32[2,16,512]{2,1,0:T(8,128)S(1)} %pad_maximum_fusion.5), channel_id=1, source_target_pairs={{0,256},{16,272},{32,288},{48,304},{64,320},{80,336},{96,352},{112... | collective-permute-start | bytes 196616 | tf_op jit(solution)/shard_map/ppermute | solution.py:64
  69.5 25.0 %copy-start.3 = (bf16[128,512]{1,0:T(8,128)(2,1)S(1)}, bf16[128,512]{1,0:T(8,128)(2,1)}, u32[]{:S(2)}) copy-start(bf16[128,512]{1,0:T(8,128)(2,1)} %param.6) | copy-start | bytes 393220
  69.5 25.0 %copy-start.4 = (bf16[128,512]{1,0:T(8,128)(2,1)S(1)}, bf16[128,512]{1,0:T(8,128)(2,1)}, u32[]{:S(2)}) copy-start(bf16[128,512]{1,0:T(8,128)(2,1)} %param.9) | copy-start | bytes 393220
  69.5 16.2 %collective-permute-start.9 = (f32[7,16,512]{2,1,0:T(8,128)S(1)}, f32[7,16,512]{2,1,0:T(8,128)S(1)}, u32[]{:S(2)}, u32[]{:S(2)}) collective-permute-start(f32[7,16,512]{2,1,0:T(8,128)S(1)} %constant_dynamic-update-slice_fusion.27), channel_id=1, source_target_pairs={{0,256},{16,272},{32,288},{48,304},{64,320},{80,336},{96,352},{112... | collective-permute-start | bytes 688136 | tf_op jit(solution)/shard_map/ppermute | solution.py:62
  74.0 10.2 %collective-permute-start.10 = (f32[2,16,512]{2,1,0:T(8,128)S(1)}, f32[2,16,512]{2,1,0:T(8,128)S(1)}, u32[]{:S(2)}, u32[]{:S(2)}) collective-permute-start(f32[2,16,512]{2,1,0:T(8,128)S(1)} %pad_maximum_fusion), channel_id=1, source_target_pairs={{0,512},{16,528},{32,544},{48,560},{64,576},{80,592},{96,608},{112... | collective-permute-start | bytes 196616 | tf_op jit(solution)/shard_map/ppermute | solution.py:64
  77.3 18.0 %copy-start.2 = (f32[128,16,512]{2,0,1:T(8,128)S(1)}, f32[128,16,512]{2,0,1:T(8,128)}, u32[]{:S(2)}) copy-start(f32[128,16,512]{2,0,1:T(8,128)} %get-tuple-element.101) | copy-start | bytes 12582916
  86.0 15.3 %collective-permute-start.11 = (f32[7,16,512]{2,1,0:T(8,128)S(1)}, f32[7,16,512]{2,1,0:T(8,128)S(1)}, u32[]{:S(2)}, u32[]{:S(2)}) collective-permute-start(f32[7,16,512]{2,1,0:T(8,128)S(1)} %constant_dynamic-update-slice_fusion.34), channel_id=1, source_target_pairs={{0,512},{16,528},{32,544},{48,560},{64,576},{80,592},{96,608},{112... | collective-permute-start | bytes 688136 | tf_op jit(solution)/shard_map/ppermute | solution.py:62
  91.0 5.5 %copy-start.5 = (bf16[128,512]{1,0:T(8,128)(2,1)S(1)}, bf16[128,512]{1,0:T(8,128)(2,1)}, u32[]{:S(2)}) copy-start(bf16[128,512]{1,0:T(8,128)(2,1)} %param.8) | copy-start | bytes 393220
  91.0 5.5 %copy-start.6 = (bf16[128,512]{1,0:T(8,128)(2,1)S(1)}, bf16[128,512]{1,0:T(8,128)(2,1)}, u32[]{:S(2)}) copy-start(bf16[128,512]{1,0:T(8,128)(2,1)} %param.7) | copy-start | bytes 393220
  94.5 6.8 %copy-start.7 = (f32[16,512]{1,0:T(8,128)S(1)}, f32[16,512]{1,0:T(8,128)}, u32[]{:S(2)}) copy-start(f32[16,512]{1,0:T(8,128)} %param.10) | copy-start | bytes 98308
  103.9 8.7 %collective-permute-start.12 = (f32[1]{0:T(128)}, f32[1]{0:T(128)}, u32[]{:S(2)}, u32[]{:S(2)}) collective-permute-start(f32[1]{0:T(128)} %bitcast.139), channel_id=1, source_target_pairs={{0,1},{1,0},{2,3},{3,2},{4,5},{5,4},{6,7},{7,6},{8,9},{9,8},{10,11... | collective-permute-start | bytes 20 | tf_op jit(solution)/shard_map/ppermute | solution.py:32
  113.3 25.5 %collective-permute-start.13 = (f32[1]{0:T(128)}, f32[1]{0:T(128)}, u32[]{:S(2)}, u32[]{:S(2)}) collective-permute-start(f32[1]{0:T(128)} %add.513), channel_id=1, source_target_pairs={{0,2},{1,3},{2,4},{3,5},{4,6},{5,7},{6,0},{7,1},{8,10},{9,11},{10,... | collective-permute-start | bytes 20 | tf_op jit(solution)/shard_map/ppermute | solution.py:32
  122.4 16.3 %collective-permute-start.14 = (f32[1]{0:T(128)}, f32[1]{0:T(128)}, u32[]{:S(2)}, u32[]{:S(2)}) collective-permute-start(f32[1]{0:T(128)} %add.513), channel_id=1, source_target_pairs={{0,4},{1,5},{2,6},{3,7},{4,0},{5,1},{6,2},{7,3},{8,12},{9,13},{10,... | collective-permute-start | bytes 20 | tf_op jit(solution)/shard_map/ppermute | solution.py:32
  135.5 6.3 %collective-permute-start.15 = (f32[1]{0:T(128)}, f32[1]{0:T(128)}, u32[]{:S(2)}, u32[]{:S(2)}) collective-permute-start(f32[1]{0:T(128)} %add.513), channel_id=1, source_target_pairs={{0,6},{1,7},{2,0},{3,1},{4,2},{5,3},{6,4},{7,5},{8,14},{9,15},{10,... | collective-permute-start | bytes 20 | tf_op jit(solution)/shard_map/ppermute | solution.py:32
  142.5 5.5 %collective-permute-start.16 = (f32[1]{0:T(128)}, f32[1]{0:T(128)}, u32[]{:S(2)}, u32[]{:S(2)}) collective-permute-start(f32[1]{0:T(128)} %add.516), channel_id=1, source_target_pairs={{0,8},{1,9},{2,10},{3,11},{4,12},{5,13},{6,14},{7,15},{8,0},{9,1},... | collective-permute-start | bytes 20 | tf_op jit(solution)/shard_map/ppermute | solution.py:32
  (1 other events, 2.4 us)

commit v11 on v8

--- a/solution.py
+++ b/solution.py
@@ -59,13 +59,16 @@
         incoming = incoming + jnp.where(high, power(at) * f_l, 0.0)
         upper = upper + jnp.where(high, 0.0, power(size - 1 - at) * b_h)
         carry = jnp.stack([step * f_l + f_h, b_l + step * b_h])
-        partner = lax.ppermute(group, axis, pairs_of(size))
+        sent = jnp.concatenate([group[:3], group[5:]]) if k == 0 else group
+        partner = lax.ppermute(sent, axis, pairs_of(size))
         if k + 1 < len(sizes):
             carry_partner = lax.ppermute(carry, axis, pairs_of(sizes[k + 1]))
             partner, carry_partner = lax.optimization_barrier((partner, carry_partner))
         else:
             hidden = hide(incoming, upper)
             partner, hidden = lax.optimization_barrier((partner, hidden))
+        if k == 0:
+            partner = jnp.concatenate([partner[:3], group[3:5], partner[3:]])
         low_g = jnp.where(high, partner, group)
         high_g = jnp.where(high, group, partner)
         wa_l, wb_l, wc_l, u_l, v_l, zw_l, za_l = low_g

time: 145 us -> 146 us (level)
  no operation moved by 1% of the time
where the time goes in v11:
time: 146 us; the launch traced here: 145 us
  starting transfers between devices  74.9 us (51%)
  waiting for transfers between devices  38.6 us (26%)
  other arithmetic  14.3 us (10%)
  matrix products  9.49 us (6%)
  between operations  5.24 us (4%)
  local copies, waits for them, and re-layouts  2.48 us (2%)
    ppermute x4, starting transfers between devices, level_gather(): got.append(lax.ppermute(x, axis, perm))  33.9 us
    ppermute x5, waiting for transfers between devices, fused_scan(): carry_partner = lax.ppermute(carry, axis, pairs_of(sizes[k + 1]))  23.5 us
    ppermute x6, starting transfers between devices, fused_scan(): partner = lax.ppermute(sent, axis, pairs_of(size))  21.7 us
    ppermute x5, starting transfers between devices, fused_scan(): carry_partner = lax.ppermute(carry, axis, pairs_of(sizes[k + 1]))  17.4 us
    ppermute x6, waiting for transfers between devices, fused_scan(): partner = lax.ppermute(sent, axis, pairs_of(size))  11.7 us
    dot_general x1, matrix products, local(): jnp.dot(upper_tri, fallen, precision=PRECISION).reshape(rising.shape)  7.38 us
    reduce_sum x1, other arithmetic, finish(): mixed = jnp.sum(mixing[None] * states, axis=1)  3.47 us
    ppermute x4, waiting for transfers between devices, level_gather(): got.append(lax.ppermute(x, axis, perm))  3.34 us
  transfers between devices with their start and end apart: 16, of which 13 were waited for; matrix products, arithmetic and copies ran while one was open for 4% of the time, Pallas kernels for 0%

profile of v11, /device:TPU:126, one launch (start us, length us, event | category | flops | bytes accessed | tf_op | source)
XLA Modules:
  0.0 145.0 jit_solution(8864335201029995514)
XLA Ops:
  9.3 7.4 %multiply_reduce_fusion.3 = (f32[16,512]{1,0:T(8,128)S(1)}, f32[16,512]{1,0:T(8,128)S(1)}, f32[16,512]{1,0:T(8,128)S(1)}, f32[16,512]{1,0:T(8,128)S(1)}, f32[16,...) fusion(f32[127,16,512]{2,0,1:T(8,128)S(1)} %bitcast.905, ...), kind=kOutput, calls=%fused_computation.7 | convolution fusion | flops 826236928 | bytes 17661952 | tf_op jit(solution)/shard_map/dot_general | solution.py:126
  18.8 2.4 %collective-permute-start = (f32[5,16,512]{2,1,0:T(8,128)S(1)}, f32[5,16,512]{2,1,0:T(8,128)S(1)}, u32[]{:S(2)}, u32[]{:S(2)}) collective-permute-start(f32[5,16,512]{2,1,0:T(8,128)S(1)} %get-tuple-element.95), channel_id=1, source_target_pairs={{0,16},{16,0},{32,48},{48,32},{64,80},{80,64},{96,112},{112,96},{1... | collective-permute-start | bytes 491528 | tf_op jit(solution)/shard_map/ppermute | solution.py:63
  21.3 3.1 %collective-permute-start.2 = (f32[2,16,512]{2,1,0:T(8,128)S(1)}, f32[2,16,512]{2,1,0:T(8,128)S(1)}, u32[]{:S(2)}, u32[]{:S(2)}) collective-permute-start(f32[2,16,512]{2,1,0:T(8,128)S(1)} %pad_maximum_fusion.3), channel_id=1, source_target_pairs={{0,32},{16,48},{32,0},{48,16},{64,96},{80,112},{96,64},{112,80},{1... | collective-permute-start | bytes 196616 | tf_op jit(solution)/shard_map/ppermute | solution.py:65
  24.5 3.0 %collective-permute-done.2 = f32[2,16,512]{2,1,0:T(8,128)S(1)} collective-permute-done((f32[2,16,512]{2,1,0:T(8,128)S(1)}, f32[2,16,512]{2,1,0:T(8,128)S(1)}, u32[]{:S(2)}, u32[]{:S(2)}) %collective-permute-start.2) | collective-permute-done | bytes 65568 | tf_op jit(solution)/shard_map/ppermute | solution.py:65
  27.7 3.1 %collective-permute-start.3 = (f32[7,16,512]{2,1,0:T(8,128)S(1)}, f32[7,16,512]{2,1,0:T(8,128)S(1)}, u32[]{:S(2)}, u32[]{:S(2)}) collective-permute-start(f32[7,16,512]{2,1,0:T(8,128)S(1)} %constant_dynamic-update-slice_fusion.11), channel_id=1, source_target_pairs={{0,32},{16,48},{32,0},{48,16},{64,96},{80,112},{96,64},{112,80},{1... | collective-permute-start | bytes 688136 | tf_op jit(solution)/shard_map/ppermute | solution.py:63
  30.9 3.8 %collective-permute-start.4 = (f32[2,16,512]{2,1,0:T(8,128)S(1)}, f32[2,16,512]{2,1,0:T(8,128)S(1)}, u32[]{:S(2)}, u32[]{:S(2)}) collective-permute-start(f32[2,16,512]{2,1,0:T(8,128)S(1)} %pad_maximum_fusion.4), channel_id=1, source_target_pairs={{0,64},{16,80},{32,96},{48,112},{64,0},{80,16},{96,32},{112,48},{1... | collective-permute-start | bytes 196616 | tf_op jit(solution)/shard_map/ppermute | solution.py:65
  34.8 3.2 %collective-permute-done.4 = f32[2,16,512]{2,1,0:T(8,128)S(1)} collective-permute-done((f32[2,16,512]{2,1,0:T(8,128)S(1)}, f32[2,16,512]{2,1,0:T(8,128)S(1)}, u32[]{:S(2)}, u32[]{:S(2)}) %collective-permute-start.4) | collective-permute-done | bytes 65568 | tf_op jit(solution)/shard_map/ppermute | solution.py:65
  38.2 3.8 %collective-permute-start.5 = (f32[7,16,512]{2,1,0:T(8,128)S(1)}, f32[7,16,512]{2,1,0:T(8,128)S(1)}, u32[]{:S(2)}, u32[]{:S(2)}) collective-permute-start(f32[7,16,512]{2,1,0:T(8,128)S(1)} %constant_dynamic-update-slice_fusion.18), channel_id=1, source_target_pairs={{0,64},{16,80},{32,96},{48,112},{64,0},{80,16},{96,32},{112,48},{1... | collective-permute-start | bytes 688136 | tf_op jit(solution)/shard_map/ppermute | solution.py:63
  42.1 3.0 %collective-permute-start.6 = (f32[2,16,512]{2,1,0:T(8,128)S(1)}, f32[2,16,512]{2,1,0:T(8,128)S(1)}, u32[]{:S(2)}, u32[]{:S(2)}) collective-permute-start(f32[2,16,512]{2,1,0:T(8,128)S(1)} %pad_maximum_fusion.5), channel_id=1, source_target_pairs={{0,128},{16,144},{32,160},{48,176},{64,192},{80,208},{96,224},{112... | collective-permute-start | bytes 196616 | tf_op jit(solution)/shard_map/ppermute | solution.py:65
  45.1 7.7 %collective-permute-done.6 = f32[2,16,512]{2,1,0:T(8,128)S(1)} collective-permute-done((f32[2,16,512]{2,1,0:T(8,128)S(1)}, f32[2,16,512]{2,1,0:T(8,128)S(1)}, u32[]{:S(2)}, u32[]{:S(2)}) %collective-permute-start.6) | collective-permute-done | bytes 65568 | tf_op jit(solution)/shard_map/ppermute | solution.py:65
  54.3 3.0 %collective-permute-start.7 = (f32[7,16,512]{2,1,0:T(8,128)S(1)}, f32[7,16,512]{2,1,0:T(8,128)S(1)}, u32[]{:S(2)}, u32[]{:S(2)}) collective-permute-start(f32[7,16,512]{2,1,0:T(8,128)S(1)} %constant_dynamic-update-slice_fusion.25), channel_id=1, source_target_pairs={{0,128},{16,144},{32,160},{48,176},{64,192},{80,208},{96,224},{112... | collective-permute-start | bytes 688136 | tf_op jit(solution)/shard_map/ppermute | solution.py:63
  57.5 4.2 %collective-permute-start.8 = (f32[2,16,512]{2,1,0:T(8,128)S(1)}, f32[2,16,512]{2,1,0:T(8,128)S(1)}, u32[]{:S(2)}, u32[]{:S(2)}) collective-permute-start(f32[2,16,512]{2,1,0:T(8,128)S(1)} %pad_maximum_fusion.6), channel_id=1, source_target_pairs={{0,256},{16,272},{32,288},{48,304},{64,320},{80,336},{96,352},{112... | collective-permute-start | bytes 196616 | tf_op jit(solution)/shard_map/ppermute | solution.py:65
  61.7 2.8 %collective-permute-done.8 = f32[2,16,512]{2,1,0:T(8,128)S(1)} collective-permute-done((f32[2,16,512]{2,1,0:T(8,128)S(1)}, f32[2,16,512]{2,1,0:T(8,128)S(1)}, u32[]{:S(2)}, u32[]{:S(2)}) %collective-permute-start.8) | collective-permute-done | bytes 65568 | tf_op jit(solution)/shard_map/ppermute | solution.py:65
  64.5 4.8 %collective-permute-done.7 = f32[7,16,512]{2,1,0:T(8,128)S(1)} collective-permute-done((f32[7,16,512]{2,1,0:T(8,128)S(1)}, f32[7,16,512]{2,1,0:T(8,128)S(1)}, u32[]{:S(2)}, u32[]{:S(2)}) %collective-permute-start.7) | collective-permute-done | bytes 229408 | tf_op jit(solution)/shard_map/ppermute | solution.py:63
  69.6 4.3 %collective-permute-start.9 = (f32[7,16,512]{2,1,0:T(8,128)S(1)}, f32[7,16,512]{2,1,0:T(8,128)S(1)}, u32[]{:S(2)}, u32[]{:S(2)}) collective-permute-start(f32[7,16,512]{2,1,0:T(8,128)S(1)} %constant_dynamic-update-slice_fusion.32), channel_id=1, source_target_pairs={{0,256},{16,272},{32,288},{48,304},{64,320},{80,336},{96,352},{112... | collective-permute-start | bytes 688136 | tf_op jit(solution)/shard_map/ppermute | solution.py:63
  74.0 3.3 %collective-permute-start.10 = (f32[2,16,512]{2,1,0:T(8,128)S(1)}, f32[2,16,512]{2,1,0:T(8,128)S(1)}, u32[]{:S(2)}, u32[]{:S(2)}) collective-permute-start(f32[2,16,512]{2,1,0:T(8,128)S(1)} %pad_maximum_fusion.1), channel_id=1, source_target_pairs={{0,512},{16,528},{32,544},{48,560},{64,576},{80,592},{96,608},{112... | collective-permute-start | bytes 196616 | tf_op jit(solution)/shard_map/ppermute | solution.py:65
  77.4 6.8 %collective-permute-done.10 = f32[2,16,512]{2,1,0:T(8,128)S(1)} collective-permute-done((f32[2,16,512]{2,1,0:T(8,128)S(1)}, f32[2,16,512]{2,1,0:T(8,128)S(1)}, u32[]{:S(2)}, u32[]{:S(2)}) %collective-permute-start.10) | collective-permute-done | bytes 65568 | tf_op jit(solution)/shard_map/ppermute | solution.py:65
  86.0 5.0 %collective-permute-start.11 = (f32[7,16,512]{2,1,0:T(8,128)S(1)}, f32[7,16,512]{2,1,0:T(8,128)S(1)}, u32[]{:S(2)}, u32[]{:S(2)}) collective-permute-start(f32[7,16,512]{2,1,0:T(8,128)S(1)} %constant_dynamic-update-slice_fusion.39), channel_id=1, source_target_pairs={{0,512},{16,528},{32,544},{48,560},{64,576},{80,592},{96,608},{112... | collective-permute-start | bytes 688136 | tf_op jit(solution)/shard_map/ppermute | solution.py:63
  91.1 3.5 %multiply_reduce_fusion = f32[128,512]{1,0:T(8,128)S(1)} fusion(f32[128,16,512]{2,0,1:T(8,128)} %copy-done.1, f32[16,512]{1,0:T(8,128)S(1)} %get-tuple-element.57, f32[16,512]{1,0:T(8,128)S(1)} %get-tuple-element.108, f32[16,512]{1,0:T(8,128)S(1)} %get-tuple-element.109, f32[16,512]{1,0:T(8,128)S(1)} %get-tuple-element.110), kind=kLoop, calls=%fused_computation.4 | loop fusion | flops 6225920 | bytes 4587520 | tf_op jit(solution)/shard_map/reduce_sum | solution.py:141
  97.3 4.0 %collective-permute-done.11 = f32[7,16,512]{2,1,0:T(8,128)S(1)} collective-permute-done((f32[7,16,512]{2,1,0:T(8,128)S(1)}, f32[7,16,512]{2,1,0:T(8,128)S(1)}, u32[]{:S(2)}, u32[]{:S(2)}) %collective-permute-start.11) | collective-permute-done | bytes 229408 | tf_op jit(solution)/shard_map/ppermute | solution.py:63
  104.0 8.4 %collective-permute-start.12 = (f32[1]{0:T(128)}, f32[1]{0:T(128)}, u32[]{:S(2)}, u32[]{:S(2)}) collective-permute-start(f32[1]{0:T(128)} %bitcast.139), channel_id=1, source_target_pairs={{0,1},{1,0},{2,3},{3,2},{4,5},{5,4},{6,7},{7,6},{8,9},{9,8},{10,11... | collective-permute-start | bytes 20 | tf_op jit(solution)/shard_map/ppermute | solution.py:32
  113.3 9.1 %collective-permute-start.13 = (f32[1]{0:T(128)}, f32[1]{0:T(128)}, u32[]{:S(2)}, u32[]{:S(2)}) collective-permute-start(f32[1]{0:T(128)} %add.510), channel_id=1, source_target_pairs={{0,2},{1,3},{2,0},{3,1},{4,6},{5,7},{6,4},{7,5},{8,10},{9,11},{10,... | collective-permute-start | bytes 20 | tf_op jit(solution)/shard_map/ppermute | solution.py:32
  123.3 13.1 %collective-permute-start.14 = (f32[1]{0:T(128)}, f32[1]{0:T(128)}, u32[]{:S(2)}, u32[]{:S(2)}) collective-permute-start(f32[1]{0:T(128)} %add.511), channel_id=1, source_target_pairs={{0,4},{1,5},{2,6},{3,7},{4,0},{5,1},{6,2},{7,3},{8,12},{9,13},{10,... | collective-permute-start | bytes 20 | tf_op jit(solution)/shard_map/ppermute | solution.py:32
  137.3 3.2 %collective-permute-start.15 = (f32[1]{0:T(128)}, f32[1]{0:T(128)}, u32[]{:S(2)}, u32[]{:S(2)}) collective-permute-start(f32[1]{0:T(128)} %add.512), channel_id=1, source_target_pairs={{0,8},{1,9},{2,10},{3,11},{4,12},{5,13},{6,14},{7,15},{8,0},{9,1},... | collective-permute-start | bytes 20 | tf_op jit(solution)/shard_map/ppermute | solution.py:32
  (114 shorter events, 23.6 us)
Async XLA Ops:
  7.0 9.8 %copy-start.1 = (f32[128,16,512]{2,0,1:T(8,128)}, f32[128,16,512]{2,0,1:T(8,128)S(1)}, u32[]{:S(2)}) copy-start(f32[128,16,512]{2,0,1:T(8,128)S(1)} %fusion.3) | copy-start | bytes 12582916
  7.0 2.4 %copy-start = (f32[16,512]{1,0:T(8,128)S(1)}, f32[16,512]{1,0:T(8,128)}, u32[]{:S(2)}) copy-start(f32[16,512]{1,0:T(8,128)} %param.11) | copy-start | bytes 98308
  16.8 4.5 %collective-permute-start.1 = (f32[2,16,512]{2,1,0:T(8,128)S(1)}, f32[2,16,512]{2,1,0:T(8,128)S(1)}, u32[]{:S(2)}, u32[]{:S(2)}) collective-permute-start(f32[2,16,512]{2,1,0:T(8,128)S(1)} %pad_maximum_fusion.2), channel_id=1, source_target_pairs={{0,16},{16,0},{32,48},{48,32},{64,80},{80,64},{96,112},{112,96},{1... | collective-permute-start | bytes 196616 | tf_op jit(solution)/shard_map/ppermute | solution.py:51
  18.8 8.7 %collective-permute-start = (f32[5,16,512]{2,1,0:T(8,128)S(1)}, f32[5,16,512]{2,1,0:T(8,128)S(1)}, u32[]{:S(2)}, u32[]{:S(2)}) collective-permute-start(f32[5,16,512]{2,1,0:T(8,128)S(1)} %get-tuple-element.95), channel_id=1, source_target_pairs={{0,16},{16,0},{32,48},{48,32},{64,80},{80,64},{96,112},{112,96},{1... | collective-permute-start | bytes 491528 | tf_op jit(solution)/shard_map/ppermute | solution.py:63
  21.3 6.2 %collective-permute-start.2 = (f32[2,16,512]{2,1,0:T(8,128)S(1)}, f32[2,16,512]{2,1,0:T(8,128)S(1)}, u32[]{:S(2)}, u32[]{:S(2)}) collective-permute-start(f32[2,16,512]{2,1,0:T(8,128)S(1)} %pad_maximum_fusion.3), channel_id=1, source_target_pairs={{0,32},{16,48},{32,0},{48,16},{64,96},{80,112},{96,64},{112,80},{1... | collective-permute-start | bytes 196616 | tf_op jit(solution)/shard_map/ppermute | solution.py:65
  27.7 10.3 %collective-permute-start.3 = (f32[7,16,512]{2,1,0:T(8,128)S(1)}, f32[7,16,512]{2,1,0:T(8,128)S(1)}, u32[]{:S(2)}, u32[]{:S(2)}) collective-permute-start(f32[7,16,512]{2,1,0:T(8,128)S(1)} %constant_dynamic-update-slice_fusion.11), channel_id=1, source_target_pairs={{0,32},{16,48},{32,0},{48,16},{64,96},{80,112},{96,64},{112,80},{1... | collective-permute-start | bytes 688136 | tf_op jit(solution)/shard_map/ppermute | solution.py:63
  30.9 7.1 %collective-permute-start.4 = (f32[2,16,512]{2,1,0:T(8,128)S(1)}, f32[2,16,512]{2,1,0:T(8,128)S(1)}, u32[]{:S(2)}, u32[]{:S(2)}) collective-permute-start(f32[2,16,512]{2,1,0:T(8,128)S(1)} %pad_maximum_fusion.4), channel_id=1, source_target_pairs={{0,64},{16,80},{32,96},{48,112},{64,0},{80,16},{96,32},{112,48},{1... | collective-permute-start | bytes 196616 | tf_op jit(solution)/shard_map/ppermute | solution.py:65
  38.2 15.9 %collective-permute-start.5 = (f32[7,16,512]{2,1,0:T(8,128)S(1)}, f32[7,16,512]{2,1,0:T(8,128)S(1)}, u32[]{:S(2)}, u32[]{:S(2)}) collective-permute-start(f32[7,16,512]{2,1,0:T(8,128)S(1)} %constant_dynamic-update-slice_fusion.18), channel_id=1, source_target_pairs={{0,64},{16,80},{32,96},{48,112},{64,0},{80,16},{96,32},{112,48},{1... | collective-permute-start | bytes 688136 | tf_op jit(solution)/shard_map/ppermute | solution.py:63
  42.1 10.7 %collective-permute-start.6 = (f32[2,16,512]{2,1,0:T(8,128)S(1)}, f32[2,16,512]{2,1,0:T(8,128)S(1)}, u32[]{:S(2)}, u32[]{:S(2)}) collective-permute-start(f32[2,16,512]{2,1,0:T(8,128)S(1)} %pad_maximum_fusion.5), channel_id=1, source_target_pairs={{0,128},{16,144},{32,160},{48,176},{64,192},{80,208},{96,224},{112... | collective-permute-start | bytes 196616 | tf_op jit(solution)/shard_map/ppermute | solution.py:65
  54.3 15.0 %collective-permute-start.7 = (f32[7,16,512]{2,1,0:T(8,128)S(1)}, f32[7,16,512]{2,1,0:T(8,128)S(1)}, u32[]{:S(2)}, u32[]{:S(2)}) collective-permute-start(f32[7,16,512]{2,1,0:T(8,128)S(1)} %constant_dynamic-update-slice_fusion.25), channel_id=1, source_target_pairs={{0,128},{16,144},{32,160},{48,176},{64,192},{80,208},{96,224},{112... | collective-permute-start | bytes 688136 | tf_op jit(solution)/shard_map/ppermute | solution.py:63
  57.5 7.1 %collective-permute-start.8 = (f32[2,16,512]{2,1,0:T(8,128)S(1)}, f32[2,16,512]{2,1,0:T(8,128)S(1)}, u32[]{:S(2)}, u32[]{:S(2)}) collective-permute-start(f32[2,16,512]{2,1,0:T(8,128)S(1)} %pad_maximum_fusion.6), channel_id=1, source_target_pairs={{0,256},{16,272},{32,288},{48,304},{64,320},{80,336},{96,352},{112... | collective-permute-start | bytes 196616 | tf_op jit(solution)/shard_map/ppermute | solution.py:65
  69.5 25.0 %copy-start.3 = (bf16[128,512]{1,0:T(8,128)(2,1)S(1)}, bf16[128,512]{1,0:T(8,128)(2,1)}, u32[]{:S(2)}) copy-start(bf16[128,512]{1,0:T(8,128)(2,1)} %param.6) | copy-start | bytes 393220
  69.5 25.0 %copy-start.4 = (bf16[128,512]{1,0:T(8,128)(2,1)S(1)}, bf16[128,512]{1,0:T(8,128)(2,1)}, u32[]{:S(2)}) copy-start(bf16[128,512]{1,0:T(8,128)(2,1)} %param.9) | copy-start | bytes 393220
  69.6 16.2 %collective-permute-start.9 = (f32[7,16,512]{2,1,0:T(8,128)S(1)}, f32[7,16,512]{2,1,0:T(8,128)S(1)}, u32[]{:S(2)}, u32[]{:S(2)}) collective-permute-start(f32[7,16,512]{2,1,0:T(8,128)S(1)} %constant_dynamic-update-slice_fusion.32), channel_id=1, source_target_pairs={{0,256},{16,272},{32,288},{48,304},{64,320},{80,336},{96,352},{112... | collective-permute-start | bytes 688136 | tf_op jit(solution)/shard_map/ppermute | solution.py:63
  74.0 10.2 %collective-permute-start.10 = (f32[2,16,512]{2,1,0:T(8,128)S(1)}, f32[2,16,512]{2,1,0:T(8,128)S(1)}, u32[]{:S(2)}, u32[]{:S(2)}) collective-permute-start(f32[2,16,512]{2,1,0:T(8,128)S(1)} %pad_maximum_fusion.1), channel_id=1, source_target_pairs={{0,512},{16,528},{32,544},{48,560},{64,576},{80,592},{96,608},{112... | collective-permute-start | bytes 196616 | tf_op jit(solution)/shard_map/ppermute | solution.py:65
  77.4 18.0 %copy-start.2 = (f32[128,16,512]{2,0,1:T(8,128)S(1)}, f32[128,16,512]{2,0,1:T(8,128)}, u32[]{:S(2)}) copy-start(f32[128,16,512]{2,0,1:T(8,128)} %get-tuple-element.111) | copy-start | bytes 12582916
  86.0 15.3 %collective-permute-start.11 = (f32[7,16,512]{2,1,0:T(8,128)S(1)}, f32[7,16,512]{2,1,0:T(8,128)S(1)}, u32[]{:S(2)}, u32[]{:S(2)}) collective-permute-start(f32[7,16,512]{2,1,0:T(8,128)S(1)} %constant_dynamic-update-slice_fusion.39), channel_id=1, source_target_pairs={{0,512},{16,528},{32,544},{48,560},{64,576},{80,592},{96,608},{112... | collective-permute-start | bytes 688136 | tf_op jit(solution)/shard_map/ppermute | solution.py:63
  91.0 5.5 %copy-start.5 = (bf16[128,512]{1,0:T(8,128)(2,1)S(1)}, bf16[128,512]{1,0:T(8,128)(2,1)}, u32[]{:S(2)}) copy-start(bf16[128,512]{1,0:T(8,128)(2,1)} %param.8) | copy-start | bytes 393220
  91.1 5.5 %copy-start.6 = (bf16[128,512]{1,0:T(8,128)(2,1)S(1)}, bf16[128,512]{1,0:T(8,128)(2,1)}, u32[]{:S(2)}) copy-start(bf16[128,512]{1,0:T(8,128)(2,1)} %param.7) | copy-start | bytes 393220
  94.6 6.8 %copy-start.7 = (f32[16,512]{1,0:T(8,128)S(1)}, f32[16,512]{1,0:T(8,128)}, u32[]{:S(2)}) copy-start(f32[16,512]{1,0:T(8,128)} %param.10) | copy-start | bytes 98308
  104.0 8.7 %collective-permute-start.12 = (f32[1]{0:T(128)}, f32[1]{0:T(128)}, u32[]{:S(2)}, u32[]{:S(2)}) collective-permute-start(f32[1]{0:T(128)} %bitcast.139), channel_id=1, source_target_pairs={{0,1},{1,0},{2,3},{3,2},{4,5},{5,4},{6,7},{7,6},{8,9},{9,8},{10,11... | collective-permute-start | bytes 20 | tf_op jit(solution)/shard_map/ppermute | solution.py:32
  113.3 9.5 %collective-permute-start.13 = (f32[1]{0:T(128)}, f32[1]{0:T(128)}, u32[]{:S(2)}, u32[]{:S(2)}) collective-permute-start(f32[1]{0:T(128)} %add.510), channel_id=1, source_target_pairs={{0,2},{1,3},{2,0},{3,1},{4,6},{5,7},{6,4},{7,5},{8,10},{9,11},{10,... | collective-permute-start | bytes 20 | tf_op jit(solution)/shard_map/ppermute | solution.py:32
  123.3 13.5 %collective-permute-start.14 = (f32[1]{0:T(128)}, f32[1]{0:T(128)}, u32[]{:S(2)}, u32[]{:S(2)}) collective-permute-start(f32[1]{0:T(128)} %add.511), channel_id=1, source_target_pairs={{0,4},{1,5},{2,6},{3,7},{4,0},{5,1},{6,2},{7,3},{8,12},{9,13},{10,... | collective-permute-start | bytes 20 | tf_op jit(solution)/shard_map/ppermute | solution.py:32
  137.3 5.5 %collective-permute-start.15 = (f32[1]{0:T(128)}, f32[1]{0:T(128)}, u32[]{:S(2)}, u32[]{:S(2)}) collective-permute-start(f32[1]{0:T(128)} %add.512), channel_id=1, source_target_pairs={{0,8},{1,9},{2,10},{3,11},{4,12},{5,13},{6,14},{7,15},{8,0},{9,1},... | collective-permute-start | bytes 20 | tf_op jit(solution)/shard_map/ppermute | solution.py:32

commit v12 on v8

--- a/solution.py
+++ b/solution.py
@@ -83,7 +83,7 @@
 
 
 def group_sum(x, axis, n, groups):
-    for stride, size in levels_of(n, groups):
+    for stride, size in levels_of(n, groups)[::-1]:
         x = x + sum(level_gather(x, axis, n, stride, size))
     return x
 

time: 145 us -> 145 us (level)
  starting transfers between devices: 74.9 us -> 76.4 us
  waiting for transfers between devices: 37.9 us -> 36.4 us
    ppermute x4, waiting for transfers between devices: 2.73 us -> 1.21 us  [level_gather(): got.append(lax.ppermute(x, axis, perm))]
    ppermute x4, starting transfers between devices: 33.9 us -> 35.4 us  [level_gather(): got.append(lax.ppermute(x, axis, perm))]
where the time goes in v12:
time: 145 us
  starting transfers between devices  76.4 us (53%)
  waiting for transfers between devices  36.4 us (25%)
  other arithmetic  14.3 us (10%)
  matrix products  9.47 us (7%)
  between operations  5.46 us (4%)
  local copies, waits for them, and re-layouts  2.45 us (2%)
    ppermute x4, starting transfers between devices, level_gather(): got.append(lax.ppermute(x, axis, perm))  35.4 us
    ppermute x5, waiting for transfers between devices, fused_scan(): carry_partner = lax.ppermute(carry, axis, pairs_of(sizes[k + 1]))  23.5 us
    ppermute x6, starting transfers between devices, fused_scan(): partner = lax.ppermute(group, axis, pairs_of(size))  21.7 us
    ppermute x5, starting transfers between devices, fused_scan(): carry_partner = lax.ppermute(carry, axis, pairs_of(sizes[k + 1]))  17.4 us
    ppermute x6, waiting for transfers between devices, fused_scan(): partner = lax.ppermute(group, axis, pairs_of(size))  11.7 us
    dot_general x1, matrix products, local(): jnp.dot(upper_tri, fallen, precision=PRECISION).reshape(rising.shape)  7.36 us
    reduce_sum x1, other arithmetic, finish(): mixed = jnp.sum(mixing[None] * states, axis=1)  3.47 us
  transfers between devices with their start and end apart: 16, of which 13 were waited for; matrix products, arithmetic and copies ran while one was open for 4% of the time, Pallas kernels for 0%

profile of v12, /device:TPU:126, one launch (start us, length us, event | category | flops | bytes accessed | tf_op | source)
XLA Modules:
  0.0 144.5 jit_solution(7417274312109406797)
XLA Ops:
  9.3 7.4 %multiply_reduce_fusion.3 = (f32[16,512]{1,0:T(8,128)S(1)}, f32[16,512]{1,0:T(8,128)S(1)}, f32[16,512]{1,0:T(8,128)S(1)}, f32[16,512]{1,0:T(8,128)S(1)}, f32[16,...) fusion(f32[127,16,512]{2,0,1:T(8,128)S(1)} %bitcast.900, ...), kind=kOutput, calls=%fused_computation.7 | convolution fusion | flops 826236928 | bytes 17661952 | tf_op jit(solution)/shard_map/dot_general | solution.py:123
  18.7 2.4 %collective-permute-start = (f32[7,16,512]{2,1,0:T(8,128)S(1)}, f32[7,16,512]{2,1,0:T(8,128)S(1)}, u32[]{:S(2)}, u32[]{:S(2)}) collective-permute-start(f32[7,16,512]{2,1,0:T(8,128)S(1)} %constant_dynamic-update-slice_fusion), channel_id=1, source_target_pairs={{0,16},{16,0},{32,48},{48,32},{64,80},{80,64},{96,112},{112,96},{1... | collective-permute-start | bytes 688136 | tf_op jit(solution)/shard_map/ppermute | solution.py:62
  21.3 3.1 %collective-permute-start.2 = (f32[2,16,512]{2,1,0:T(8,128)S(1)}, f32[2,16,512]{2,1,0:T(8,128)S(1)}, u32[]{:S(2)}, u32[]{:S(2)}) collective-permute-start(f32[2,16,512]{2,1,0:T(8,128)S(1)} %pad_maximum_fusion.2), channel_id=1, source_target_pairs={{0,32},{16,48},{32,0},{48,16},{64,96},{80,112},{96,64},{112,80},{1... | collective-permute-start | bytes 196616 | tf_op jit(solution)/shard_map/ppermute | solution.py:64
  24.4 3.0 %collective-permute-done.2 = f32[2,16,512]{2,1,0:T(8,128)S(1)} collective-permute-done((f32[2,16,512]{2,1,0:T(8,128)S(1)}, f32[2,16,512]{2,1,0:T(8,128)S(1)}, u32[]{:S(2)}, u32[]{:S(2)}) %collective-permute-start.2) | collective-permute-done | bytes 65568 | tf_op jit(solution)/shard_map/ppermute | solution.py:64
  27.6 3.1 %collective-permute-start.3 = (f32[7,16,512]{2,1,0:T(8,128)S(1)}, f32[7,16,512]{2,1,0:T(8,128)S(1)}, u32[]{:S(2)}, u32[]{:S(2)}) collective-permute-start(f32[7,16,512]{2,1,0:T(8,128)S(1)} %constant_dynamic-update-slice_fusion.6), channel_id=1, source_target_pairs={{0,32},{16,48},{32,0},{48,16},{64,96},{80,112},{96,64},{112,80},{1... | collective-permute-start | bytes 688136 | tf_op jit(solution)/shard_map/ppermute | solution.py:62
  30.9 3.8 %collective-permute-start.4 = (f32[2,16,512]{2,1,0:T(8,128)S(1)}, f32[2,16,512]{2,1,0:T(8,128)S(1)}, u32[]{:S(2)}, u32[]{:S(2)}) collective-permute-start(f32[2,16,512]{2,1,0:T(8,128)S(1)} %pad_maximum_fusion.3), channel_id=1, source_target_pairs={{0,64},{16,80},{32,96},{48,112},{64,0},{80,16},{96,32},{112,48},{1... | collective-permute-start | bytes 196616 | tf_op jit(solution)/shard_map/ppermute | solution.py:64
  34.7 3.2 %collective-permute-done.4 = f32[2,16,512]{2,1,0:T(8,128)S(1)} collective-permute-done((f32[2,16,512]{2,1,0:T(8,128)S(1)}, f32[2,16,512]{2,1,0:T(8,128)S(1)}, u32[]{:S(2)}, u32[]{:S(2)}) %collective-permute-start.4) | collective-permute-done | bytes 65568 | tf_op jit(solution)/shard_map/ppermute | solution.py:64
  38.1 3.8 %collective-permute-start.5 = (f32[7,16,512]{2,1,0:T(8,128)S(1)}, f32[7,16,512]{2,1,0:T(8,128)S(1)}, u32[]{:S(2)}, u32[]{:S(2)}) collective-permute-start(f32[7,16,512]{2,1,0:T(8,128)S(1)} %constant_dynamic-update-slice_fusion.13), channel_id=1, source_target_pairs={{0,64},{16,80},{32,96},{48,112},{64,0},{80,16},{96,32},{112,48},{1... | collective-permute-start | bytes 688136 | tf_op jit(solution)/shard_map/ppermute | solution.py:62
  42.1 3.0 %collective-permute-start.6 = (f32[2,16,512]{2,1,0:T(8,128)S(1)}, f32[2,16,512]{2,1,0:T(8,128)S(1)}, u32[]{:S(2)}, u32[]{:S(2)}) collective-permute-start(f32[2,16,512]{2,1,0:T(8,128)S(1)} %pad_maximum_fusion.4), channel_id=1, source_target_pairs={{0,128},{16,144},{32,160},{48,176},{64,192},{80,208},{96,224},{112... | collective-permute-start | bytes 196616 | tf_op jit(solution)/shard_map/ppermute | solution.py:64
  45.1 7.7 %collective-permute-done.6 = f32[2,16,512]{2,1,0:T(8,128)S(1)} collective-permute-done((f32[2,16,512]{2,1,0:T(8,128)S(1)}, f32[2,16,512]{2,1,0:T(8,128)S(1)}, u32[]{:S(2)}, u32[]{:S(2)}) %collective-permute-start.6) | collective-permute-done | bytes 65568 | tf_op jit(solution)/shard_map/ppermute | solution.py:64
  54.3 3.0 %collective-permute-start.7 = (f32[7,16,512]{2,1,0:T(8,128)S(1)}, f32[7,16,512]{2,1,0:T(8,128)S(1)}, u32[]{:S(2)}, u32[]{:S(2)}) collective-permute-start(f32[7,16,512]{2,1,0:T(8,128)S(1)} %constant_dynamic-update-slice_fusion.20), channel_id=1, source_target_pairs={{0,128},{16,144},{32,160},{48,176},{64,192},{80,208},{96,224},{112... | collective-permute-start | bytes 688136 | tf_op jit(solution)/shard_map/ppermute | solution.py:62
  57.4 4.2 %collective-permute-start.8 = (f32[2,16,512]{2,1,0:T(8,128)S(1)}, f32[2,16,512]{2,1,0:T(8,128)S(1)}, u32[]{:S(2)}, u32[]{:S(2)}) collective-permute-start(f32[2,16,512]{2,1,0:T(8,128)S(1)} %pad_maximum_fusion.5), channel_id=1, source_target_pairs={{0,256},{16,272},{32,288},{48,304},{64,320},{80,336},{96,352},{112... | collective-permute-start | bytes 196616 | tf_op jit(solution)/shard_map/ppermute | solution.py:64
  61.6 2.8 %collective-permute-done.8 = f32[2,16,512]{2,1,0:T(8,128)S(1)} collective-permute-done((f32[2,16,512]{2,1,0:T(8,128)S(1)}, f32[2,16,512]{2,1,0:T(8,128)S(1)}, u32[]{:S(2)}, u32[]{:S(2)}) %collective-permute-start.8) | collective-permute-done | bytes 65568 | tf_op jit(solution)/shard_map/ppermute | solution.py:64
  64.4 4.8 %collective-permute-done.7 = f32[7,16,512]{2,1,0:T(8,128)S(1)} collective-permute-done((f32[7,16,512]{2,1,0:T(8,128)S(1)}, f32[7,16,512]{2,1,0:T(8,128)S(1)}, u32[]{:S(2)}, u32[]{:S(2)}) %collective-permute-start.7) | collective-permute-done | bytes 229408 | tf_op jit(solution)/shard_map/ppermute | solution.py:62
  69.5 4.3 %collective-permute-start.9 = (f32[7,16,512]{2,1,0:T(8,128)S(1)}, f32[7,16,512]{2,1,0:T(8,128)S(1)}, u32[]{:S(2)}, u32[]{:S(2)}) collective-permute-start(f32[7,16,512]{2,1,0:T(8,128)S(1)} %constant_dynamic-update-slice_fusion.27), channel_id=1, source_target_pairs={{0,256},{16,272},{32,288},{48,304},{64,320},{80,336},{96,352},{112... | collective-permute-start | bytes 688136 | tf_op jit(solution)/shard_map/ppermute | solution.py:62
  73.9 3.3 %collective-permute-start.10 = (f32[2,16,512]{2,1,0:T(8,128)S(1)}, f32[2,16,512]{2,1,0:T(8,128)S(1)}, u32[]{:S(2)}, u32[]{:S(2)}) collective-permute-start(f32[2,16,512]{2,1,0:T(8,128)S(1)} %pad_maximum_fusion), channel_id=1, source_target_pairs={{0,512},{16,528},{32,544},{48,560},{64,576},{80,592},{96,608},{112... | collective-permute-start | bytes 196616 | tf_op jit(solution)/shard_map/ppermute | solution.py:64
  77.3 6.8 %collective-permute-done.10 = f32[2,16,512]{2,1,0:T(8,128)S(1)} collective-permute-done((f32[2,16,512]{2,1,0:T(8,128)S(1)}, f32[2,16,512]{2,1,0:T(8,128)S(1)}, u32[]{:S(2)}, u32[]{:S(2)}) %collective-permute-start.10) | collective-permute-done | bytes 65568 | tf_op jit(solution)/shard_map/ppermute | solution.py:64
  85.9 5.0 %collective-permute-start.11 = (f32[7,16,512]{2,1,0:T(8,128)S(1)}, f32[7,16,512]{2,1,0:T(8,128)S(1)}, u32[]{:S(2)}, u32[]{:S(2)}) collective-permute-start(f32[7,16,512]{2,1,0:T(8,128)S(1)} %constant_dynamic-update-slice_fusion.34), channel_id=1, source_target_pairs={{0,512},{16,528},{32,544},{48,560},{64,576},{80,592},{96,608},{112... | collective-permute-start | bytes 688136 | tf_op jit(solution)/shard_map/ppermute | solution.py:62
  91.0 3.5 %multiply_reduce_fusion = f32[128,512]{1,0:T(8,128)S(1)} fusion(f32[128,16,512]{2,0,1:T(8,128)} %copy-done.1, f32[16,512]{1,0:T(8,128)S(1)} %get-tuple-element.57, f32[16,512]{1,0:T(8,128)S(1)} %get-tuple-element.98, f32[16,512]{1,0:T(8,128)S(1)} %get-tuple-element.99, f32[16,512]{1,0:T(8,128)S(1)} %get-tuple-element.100), kind=kLoop, calls=%fused_computation.4 | loop fusion | flops 6225920 | bytes 4587520 | tf_op jit(solution)/shard_map/reduce_sum | solution.py:138
  97.2 4.0 %collective-permute-done.11 = f32[7,16,512]{2,1,0:T(8,128)S(1)} collective-permute-done((f32[7,16,512]{2,1,0:T(8,128)S(1)}, f32[7,16,512]{2,1,0:T(8,128)S(1)}, u32[]{:S(2)}, u32[]{:S(2)}) %collective-permute-start.11) | collective-permute-done | bytes 229408 | tf_op jit(solution)/shard_map/ppermute | solution.py:62
  103.9 4.7 %collective-permute-start.12 = (f32[1]{0:T(128)}, f32[1]{0:T(128)}, u32[]{:S(2)}, u32[]{:S(2)}) collective-permute-start(f32[1]{0:T(128)} %bitcast.139), channel_id=1, source_target_pairs={{0,8},{1,9},{2,10},{3,11},{4,12},{5,13},{6,14},{7,15},{8,0},{9,1},... | collective-permute-start | bytes 20 | tf_op jit(solution)/shard_map/ppermute | solution.py:32
  109.9 17.8 %collective-permute-start.13 = (f32[1]{0:T(128)}, f32[1]{0:T(128)}, u32[]{:S(2)}, u32[]{:S(2)}) collective-permute-start(f32[1]{0:T(128)} %add.510), channel_id=1, source_target_pairs={{0,4},{1,5},{2,6},{3,7},{4,0},{5,1},{6,2},{7,3},{8,12},{9,13},{10,... | collective-permute-start | bytes 20 | tf_op jit(solution)/shard_map/ppermute | solution.py:32
  128.5 7.4 %collective-permute-start.14 = (f32[1]{0:T(128)}, f32[1]{0:T(128)}, u32[]{:S(2)}, u32[]{:S(2)}) collective-permute-start(f32[1]{0:T(128)} %add.511), channel_id=1, source_target_pairs={{0,2},{1,3},{2,0},{3,1},{4,6},{5,7},{6,4},{7,5},{8,10},{9,11},{10,... | collective-permute-start | bytes 20 | tf_op jit(solution)/shard_map/ppermute | solution.py:32
  136.7 5.5 %collective-permute-start.15 = (f32[1]{0:T(128)}, f32[1]{0:T(128)}, u32[]{:S(2)}, u32[]{:S(2)}) collective-permute-start(f32[1]{0:T(128)} %add.512), channel_id=1, source_target_pairs={{0,1},{1,0},{2,3},{3,2},{4,5},{5,4},{6,7},{7,6},{8,9},{9,8},{10,11... | collective-permute-start | bytes 20 | tf_op jit(solution)/shard_map/ppermute | solution.py:32
  (111 shorter events, 21.4 us)
Async XLA Ops:
  7.0 9.7 %copy-start.1 = (f32[128,16,512]{2,0,1:T(8,128)}, f32[128,16,512]{2,0,1:T(8,128)S(1)}, u32[]{:S(2)}) copy-start(f32[128,16,512]{2,0,1:T(8,128)S(1)} %fusion.3) | copy-start | bytes 12582916
  7.0 2.4 %copy-start = (f32[16,512]{1,0:T(8,128)S(1)}, f32[16,512]{1,0:T(8,128)}, u32[]{:S(2)}) copy-start(f32[16,512]{1,0:T(8,128)} %param.11) | copy-start | bytes 98308
  16.7 4.4 %collective-permute-start.1 = (f32[2,16,512]{2,1,0:T(8,128)S(1)}, f32[2,16,512]{2,1,0:T(8,128)S(1)}, u32[]{:S(2)}, u32[]{:S(2)}) collective-permute-start(f32[2,16,512]{2,1,0:T(8,128)S(1)} %pad_maximum_fusion.1), channel_id=1, source_target_pairs={{0,16},{16,0},{32,48},{48,32},{64,80},{80,64},{96,112},{112,96},{1... | collective-permute-start | bytes 196616 | tf_op jit(solution)/shard_map/ppermute | solution.py:51
  18.7 8.7 %collective-permute-start = (f32[7,16,512]{2,1,0:T(8,128)S(1)}, f32[7,16,512]{2,1,0:T(8,128)S(1)}, u32[]{:S(2)}, u32[]{:S(2)}) collective-permute-start(f32[7,16,512]{2,1,0:T(8,128)S(1)} %constant_dynamic-update-slice_fusion), channel_id=1, source_target_pairs={{0,16},{16,0},{32,48},{48,32},{64,80},{80,64},{96,112},{112,96},{1... | collective-permute-start | bytes 688136 | tf_op jit(solution)/shard_map/ppermute | solution.py:62
  21.3 6.2 %collective-permute-start.2 = (f32[2,16,512]{2,1,0:T(8,128)S(1)}, f32[2,16,512]{2,1,0:T(8,128)S(1)}, u32[]{:S(2)}, u32[]{:S(2)}) collective-permute-start(f32[2,16,512]{2,1,0:T(8,128)S(1)} %pad_maximum_fusion.2), channel_id=1, source_target_pairs={{0,32},{16,48},{32,0},{48,16},{64,96},{80,112},{96,64},{112,80},{1... | collective-permute-start | bytes 196616 | tf_op jit(solution)/shard_map/ppermute | solution.py:64
  27.6 10.3 %collective-permute-start.3 = (f32[7,16,512]{2,1,0:T(8,128)S(1)}, f32[7,16,512]{2,1,0:T(8,128)S(1)}, u32[]{:S(2)}, u32[]{:S(2)}) collective-permute-start(f32[7,16,512]{2,1,0:T(8,128)S(1)} %constant_dynamic-update-slice_fusion.6), channel_id=1, source_target_pairs={{0,32},{16,48},{32,0},{48,16},{64,96},{80,112},{96,64},{112,80},{1... | collective-permute-start | bytes 688136 | tf_op jit(solution)/shard_map/ppermute | solution.py:62
  30.9 7.1 %collective-permute-start.4 = (f32[2,16,512]{2,1,0:T(8,128)S(1)}, f32[2,16,512]{2,1,0:T(8,128)S(1)}, u32[]{:S(2)}, u32[]{:S(2)}) collective-permute-start(f32[2,16,512]{2,1,0:T(8,128)S(1)} %pad_maximum_fusion.3), channel_id=1, source_target_pairs={{0,64},{16,80},{32,96},{48,112},{64,0},{80,16},{96,32},{112,48},{1... | collective-permute-start | bytes 196616 | tf_op jit(solution)/shard_map/ppermute | solution.py:64
  38.1 15.9 %collective-permute-start.5 = (f32[7,16,512]{2,1,0:T(8,128)S(1)}, f32[7,16,512]{2,1,0:T(8,128)S(1)}, u32[]{:S(2)}, u32[]{:S(2)}) collective-permute-start(f32[7,16,512]{2,1,0:T(8,128)S(1)} %constant_dynamic-update-slice_fusion.13), channel_id=1, source_target_pairs={{0,64},{16,80},{32,96},{48,112},{64,0},{80,16},{96,32},{112,48},{1... | collective-permute-start | bytes 688136 | tf_op jit(solution)/shard_map/ppermute | solution.py:62
  42.1 10.7 %collective-permute-start.6 = (f32[2,16,512]{2,1,0:T(8,128)S(1)}, f32[2,16,512]{2,1,0:T(8,128)S(1)}, u32[]{:S(2)}, u32[]{:S(2)}) collective-permute-start(f32[2,16,512]{2,1,0:T(8,128)S(1)} %pad_maximum_fusion.4), channel_id=1, source_target_pairs={{0,128},{16,144},{32,160},{48,176},{64,192},{80,208},{96,224},{112... | collective-permute-start | bytes 196616 | tf_op jit(solution)/shard_map/ppermute | solution.py:64
  54.3 15.0 %collective-permute-start.7 = (f32[7,16,512]{2,1,0:T(8,128)S(1)}, f32[7,16,512]{2,1,0:T(8,128)S(1)}, u32[]{:S(2)}, u32[]{:S(2)}) collective-permute-start(f32[7,16,512]{2,1,0:T(8,128)S(1)} %constant_dynamic-update-slice_fusion.20), channel_id=1, source_target_pairs={{0,128},{16,144},{32,160},{48,176},{64,192},{80,208},{96,224},{112... | collective-permute-start | bytes 688136 | tf_op jit(solution)/shard_map/ppermute | solution.py:62
  57.4 7.1 %collective-permute-start.8 = (f32[2,16,512]{2,1,0:T(8,128)S(1)}, f32[2,16,512]{2,1,0:T(8,128)S(1)}, u32[]{:S(2)}, u32[]{:S(2)}) collective-permute-start(f32[2,16,512]{2,1,0:T(8,128)S(1)} %pad_maximum_fusion.5), channel_id=1, source_target_pairs={{0,256},{16,272},{32,288},{48,304},{64,320},{80,336},{96,352},{112... | collective-permute-start | bytes 196616 | tf_op jit(solution)/shard_map/ppermute | solution.py:64
  69.5 25.0 %copy-start.3 = (bf16[128,512]{1,0:T(8,128)(2,1)S(1)}, bf16[128,512]{1,0:T(8,128)(2,1)}, u32[]{:S(2)}) copy-start(bf16[128,512]{1,0:T(8,128)(2,1)} %param.6) | copy-start | bytes 393220
  69.5 25.0 %copy-start.4 = (bf16[128,512]{1,0:T(8,128)(2,1)S(1)}, bf16[128,512]{1,0:T(8,128)(2,1)}, u32[]{:S(2)}) copy-start(bf16[128,512]{1,0:T(8,128)(2,1)} %param.9) | copy-start | bytes 393220
  69.5 16.2 %collective-permute-start.9 = (f32[7,16,512]{2,1,0:T(8,128)S(1)}, f32[7,16,512]{2,1,0:T(8,128)S(1)}, u32[]{:S(2)}, u32[]{:S(2)}) collective-permute-start(f32[7,16,512]{2,1,0:T(8,128)S(1)} %constant_dynamic-update-slice_fusion.27), channel_id=1, source_target_pairs={{0,256},{16,272},{32,288},{48,304},{64,320},{80,336},{96,352},{112... | collective-permute-start | bytes 688136 | tf_op jit(solution)/shard_map/ppermute | solution.py:62
  73.9 10.2 %collective-permute-start.10 = (f32[2,16,512]{2,1,0:T(8,128)S(1)}, f32[2,16,512]{2,1,0:T(8,128)S(1)}, u32[]{:S(2)}, u32[]{:S(2)}) collective-permute-start(f32[2,16,512]{2,1,0:T(8,128)S(1)} %pad_maximum_fusion), channel_id=1, source_target_pairs={{0,512},{16,528},{32,544},{48,560},{64,576},{80,592},{96,608},{112... | collective-permute-start | bytes 196616 | tf_op jit(solution)/shard_map/ppermute | solution.py:64
  77.3 18.0 %copy-start.2 = (f32[128,16,512]{2,0,1:T(8,128)S(1)}, f32[128,16,512]{2,0,1:T(8,128)}, u32[]{:S(2)}) copy-start(f32[128,16,512]{2,0,1:T(8,128)} %get-tuple-element.101) | copy-start | bytes 12582916
  85.9 15.3 %collective-permute-start.11 = (f32[7,16,512]{2,1,0:T(8,128)S(1)}, f32[7,16,512]{2,1,0:T(8,128)S(1)}, u32[]{:S(2)}, u32[]{:S(2)}) collective-permute-start(f32[7,16,512]{2,1,0:T(8,128)S(1)} %constant_dynamic-update-slice_fusion.34), channel_id=1, source_target_pairs={{0,512},{16,528},{32,544},{48,560},{64,576},{80,592},{96,608},{112... | collective-permute-start | bytes 688136 | tf_op jit(solution)/shard_map/ppermute | solution.py:62
  91.0 5.5 %copy-start.5 = (bf16[128,512]{1,0:T(8,128)(2,1)S(1)}, bf16[128,512]{1,0:T(8,128)(2,1)}, u32[]{:S(2)}) copy-start(bf16[128,512]{1,0:T(8,128)(2,1)} %param.8) | copy-start | bytes 393220
  91.0 5.5 %copy-start.6 = (bf16[128,512]{1,0:T(8,128)(2,1)S(1)}, bf16[128,512]{1,0:T(8,128)(2,1)}, u32[]{:S(2)}) copy-start(bf16[128,512]{1,0:T(8,128)(2,1)} %param.7) | copy-start | bytes 393220
  94.5 6.8 %copy-start.7 = (f32[16,512]{1,0:T(8,128)S(1)}, f32[16,512]{1,0:T(8,128)}, u32[]{:S(2)}) copy-start(f32[16,512]{1,0:T(8,128)} %param.10) | copy-start | bytes 98308
  103.9 5.4 %collective-permute-start.12 = (f32[1]{0:T(128)}, f32[1]{0:T(128)}, u32[]{:S(2)}, u32[]{:S(2)}) collective-permute-start(f32[1]{0:T(128)} %bitcast.139), channel_id=1, source_target_pairs={{0,8},{1,9},{2,10},{3,11},{4,12},{5,13},{6,14},{7,15},{8,0},{9,1},... | collective-permute-start | bytes 20 | tf_op jit(solution)/shard_map/ppermute | solution.py:32
  109.9 17.9 %collective-permute-start.13 = (f32[1]{0:T(128)}, f32[1]{0:T(128)}, u32[]{:S(2)}, u32[]{:S(2)}) collective-permute-start(f32[1]{0:T(128)} %add.510), channel_id=1, source_target_pairs={{0,4},{1,5},{2,6},{3,7},{4,0},{5,1},{6,2},{7,3},{8,12},{9,13},{10,... | collective-permute-start | bytes 20 | tf_op jit(solution)/shard_map/ppermute | solution.py:32
  128.5 7.6 %collective-permute-start.14 = (f32[1]{0:T(128)}, f32[1]{0:T(128)}, u32[]{:S(2)}, u32[]{:S(2)}) collective-permute-start(f32[1]{0:T(128)} %add.511), channel_id=1, source_target_pairs={{0,2},{1,3},{2,0},{3,1},{4,6},{5,7},{6,4},{7,5},{8,10},{9,11},{10,... | collective-permute-start | bytes 20 | tf_op jit(solution)/shard_map/ppermute | solution.py:32
  136.7 5.7 %collective-permute-start.15 = (f32[1]{0:T(128)}, f32[1]{0:T(128)}, u32[]{:S(2)}, u32[]{:S(2)}) collective-permute-start(f32[1]{0:T(128)} %add.512), channel_id=1, source_target_pairs={{0,1},{1,0},{2,3},{3,2},{4,5},{5,4},{6,7},{7,6},{8,9},{9,8},{10,11... | collective-permute-start | bytes 20 | tf_op jit(solution)/shard_map/ppermute | solution.py:32
